TPU v7x, 32 devices: a whole 2x2x4 slice. The times are simulated.
32 devices in a mesh: groups: 2 (over x), seq: 16 (over z, y, core).
Axes of the slice: x: 2, y: 2, z: 4, core: 2. Of those that a mesh axis runs over, the one named last changes fastest.
Arguments:
- se_streams: bfloat16 [8192, 12288], P(('groups', 'seq')), parts along dimension 0, may hold values from -6 to 6
- mr_gates: bfloat16 [8192, 8192], P(('groups', 'seq')), parts along dimension 0, may hold values from -6 to 6
- se_feat: bfloat16 [7, 12288], replicated, may hold values from -2 to 2
- se_filter: bfloat16 [7, 256], replicated, may hold values from -2 to 2
- mr_feat: bfloat16 [7, 12288], replicated, may hold values from -2 to 2
- mr_filter: bfloat16 [128, 256], replicated, may hold values from -0.5 to 0.5
- mr_skip: bfloat16 [4096], replicated, may hold values from -1 to 1
- req_ends: int32 [32], P('groups'), parts along dimension 0, may hold values from 0 to 4095, as said below
- decode_row: int32 [32], P('groups'), parts along dimension 0, may hold values from 0 to 15, each once
Outputs:
- hyena_out: bfloat16 [8192, 4096], P(('groups', 'seq')), parts along dimension 0
- tail_cache: bfloat16 [32, 127, 4096], P('groups', None, 'seq'), parts along dimension 0
There are 2 independent parts, one for each index of `groups`. A program takes and returns all parts, laid end to end along the dimension named above; an argument that names none is the same for every part. Nothing has to cross between parts.
Inputs may be any that keep to these rules, and one draw needn't show every extreme that they name: `req_ends`: the rows of one device hold at most 4 entries, and some device holds exactly 4.
All inputs are finite; a program needn't handle non-finite values.
Results may differ from a plain program's by a relative error of at most 0.0085.
Values may be sent and summed in bfloat16 or wider, within the bound.
No kernel may reach another device: no remote copies, remote signals or barrier semaphores. Data moves between devices by JAX's collectives and lax.ppermute only.
A program may use at most 192 MiB of HBM per device.

v0:
```python
import jax
import jax.numpy as jnp
from jax import lax
from jax.sharding import PartitionSpec as P

ENDS_MAX = 4


def passed_along(x, axis, by):
    length = lax.axis_size(axis)
    pairs = [(i, i + by) for i in range(length) if 0 <= i + by < length]
    return lax.ppermute(x, axis, pairs)


def request_of(positions, req_ends):
    return jnp.sum((req_ends[None, :] < positions[:, None]).astype(jnp.int32), axis=1)


def short_conv(values, weights, segment):
    length = weights.shape[0]
    out_count = values.shape[0] - length + 1
    latest = length - 1
    current = segment[latest:]
    summed = values[latest:].astype(jnp.float32) * weights[0].astype(jnp.float32)
    for lag_step in range(1, length):
        earlier = values[latest - lag_step : latest - lag_step + out_count].astype(jnp.float32)
        same_req = segment[latest - lag_step : latest - lag_step + out_count] == current
        summed = summed + jnp.where(
            same_req[:, None], earlier * weights[lag_step].astype(jnp.float32), 0.0
        )
    return summed


def toeplitz(taps_table):
    tap_count = taps_table.shape[0]
    zero_rows = jnp.zeros_like(taps_table)
    row_vector = jnp.concatenate([zero_rows, taps_table[::-1], zero_rows], axis=0)
    tiled = jnp.tile(row_vector, (tap_count, 1))[: tap_count * (3 * tap_count - 1)]
    skewed = tiled.reshape(tap_count, 3 * tap_count - 1, taps_table.shape[1])
    return skewed[:, tap_count - 1 : 3 * tap_count - 1]


def long_conv(z_ext, segment, taps_table, slot_count):
    tap_count = taps_table.shape[0]
    blocks = z_ext.shape[0] // tap_count - 1
    channels = z_ext.shape[1]
    filters = taps_table.shape[1]
    shaped = z_ext.reshape(blocks + 1, tap_count, channels)
    window = jnp.concatenate([shaped[:-1], shaped[1:]], axis=1)
    seg_shaped = segment.reshape(blocks + 1, tap_count)
    seg_window = jnp.concatenate([seg_shaped[:-1], seg_shaped[1:]], axis=1)
    base_seg = seg_shaped[1:, :1]
    rel_source = seg_window - base_seg
    rel_target = seg_shaped[1:] - base_seg
    slot_ids = jnp.arange(slot_count, dtype=jnp.int32)
    source_hit = rel_source[:, :, None] == slot_ids[None, None, :]
    grouped = window.reshape(blocks, 2 * tap_count, filters, channels // filters)
    stacked = jnp.where(
        source_hit[:, :, None, :, None], grouped[:, :, :, None, :], jnp.zeros((), grouped.dtype)
    )
    matrix = toeplitz(taps_table)
    result = jnp.einsum("tsf,bsfjg->btfjg", matrix, stacked, preferred_element_type=jnp.float32)
    target_hit = (rel_target[:, :, None] == slot_ids[None, None, :]).astype(jnp.float32)
    picked = jnp.sum(result * target_hit[:, :, None, :, None], axis=3)
    return picked.reshape(blocks * tap_count, channels)


def pick_entries(lookup_table, indices):
    hits = indices[:, None] == jnp.arange(lookup_table.shape[0], dtype=jnp.int32)[None, :]
    return jnp.sum(jnp.where(hits, lookup_table[None, :], 0), axis=1)


def cut_tails(z_ext, req_ends, ext_start, requests, is_valid, tail_len):
    last_pos = pick_entries(req_ends, requests)
    first_pos = jnp.where(requests > 0, pick_entries(req_ends, jnp.maximum(requests - 1, 0)) + 1, 0)
    offsets = jnp.arange(tail_len, dtype=jnp.int32)[None, :]
    positions = last_pos[:, None] - tail_len + 1 + offsets
    inside = (positions >= first_pos[:, None]) & is_valid[:, None]
    rows_wanted = positions - ext_start
    row_ids = jnp.arange(z_ext.shape[0], dtype=jnp.int32)
    select = ((rows_wanted[:, :, None] == row_ids[None, None, :]) & inside[:, :, None]).astype(
        jnp.bfloat16
    )
    picked = jnp.einsum("ris,sc->ric", select, z_ext, preferred_element_type=jnp.float32)
    return picked.astype(jnp.bfloat16)


def place_rows(states, target, row_count):
    placing = (jnp.arange(row_count, dtype=jnp.int32)[:, None] == target[None, :]).astype(
        jnp.bfloat16
    )
    placed = jnp.einsum("ts,sic->tic", placing, states, preferred_element_type=jnp.float32)
    return placed.astype(jnp.bfloat16)


def local(
    se_streams, mr_gates, se_feat, se_filter, mr_feat, mr_filter, mr_skip, req_ends, decode_row
):
    tok_rows = se_streams.shape[0]
    channels = mr_gates.shape[1] // 2
    shards = lax.axis_size("seq")
    device = lax.axis_index("seq")
    offset = device * tok_rows
    reach_rows = se_feat.shape[0] - 1
    tap_count = mr_filter.shape[0]
    tail_len = tap_count - 1
    group_ch = channels // se_filter.shape[1]
    total_req = req_ends.shape[0]
    slot_total = ENDS_MAX + 1
    rim_depth = 2 * reach_rows
    prev_se, prev_mr = passed_along(
        (se_streams[tok_rows - rim_depth :], mr_gates[tok_rows - reach_rows :]), "seq", 1
    )
    se_ext = jnp.concatenate([prev_se, se_streams], axis=0)
    seg_ext = request_of(
        offset - rim_depth + jnp.arange(tok_rows + rim_depth, dtype=jnp.int32), req_ends
    )
    featured = short_conv(se_ext, se_feat, seg_ext)
    z_one = (featured[:, channels : 2 * channels] * featured[:, 2 * channels :]).astype(
        jnp.bfloat16
    )
    conv_one = short_conv(z_one, jnp.repeat(se_filter, group_ch, axis=1), seg_ext[reach_rows:])
    y_se = (featured[reach_rows:, :channels] * conv_one).astype(jnp.bfloat16)
    prev_y = passed_along(y_se[tok_rows - reach_rows :], "seq", 1)
    y_ext = jnp.concatenate([prev_y, y_se], axis=0)
    seg_mr = seg_ext[rim_depth - reach_rows :]
    gates_ext = jnp.concatenate([prev_mr, mr_gates], axis=0)
    gate_feat = short_conv(gates_ext, mr_feat[:, : 2 * channels], seg_mr)
    value_feat = short_conv(y_ext, mr_feat[:, 2 * channels :], seg_mr)
    q_two = gate_feat[:, :channels]
    z_two = (gate_feat[:, channels:] * value_feat).astype(jnp.bfloat16)
    prev_z = passed_along(z_two[tok_rows - tail_len :], "seq", 1)
    z_ext = jnp.concatenate([jnp.zeros((1, channels), jnp.bfloat16), prev_z, z_two], axis=0)
    seg_long = request_of(
        offset - tap_count + jnp.arange(tok_rows + tap_count, dtype=jnp.int32), req_ends
    )
    first_req = request_of(jnp.reshape(offset, (1,)), req_ends)[0]
    past_req = request_of(jnp.reshape(offset + tok_rows, (1,)), req_ends)[0]
    slot_local = jnp.arange(ENDS_MAX, dtype=jnp.int32)
    local_req = jnp.minimum(first_req + slot_local, total_req - 1)
    states = cut_tails(
        z_ext, req_ends, offset - tap_count, local_req, first_req + slot_local < past_req, tail_len
    )
    received = lax.all_to_all(states, "seq", split_axis=2, concat_axis=0, tiled=True)
    conv_two = long_conv(z_ext, seg_long, mr_filter, slot_total)
    mixed = (conv_two + mr_skip.astype(jnp.float32) * z_two.astype(jnp.float32)).astype(
        jnp.bfloat16
    )
    slot_index = jnp.arange(shards * ENDS_MAX, dtype=jnp.int32)
    source = slot_index // ENDS_MAX
    within = slot_index % ENDS_MAX
    source_first = request_of(source * tok_rows, req_ends)
    source_past = request_of((source + 1) * tok_rows, req_ends)
    requests = source_first + within
    is_valid = requests < source_past
    target = jnp.where(
        is_valid, pick_entries(decode_row, jnp.minimum(requests, total_req - 1)), total_req
    )
    tail_cache = place_rows(received, target, total_req)
    hyena_out = (q_two * mixed.astype(jnp.float32)).astype(jnp.bfloat16)
    return (hyena_out, tail_cache)


def solution(mesh):
    placed = (
        P(("groups", "seq"), None),
        P(("groups", "seq"), None),
        P(),
        P(),
        P(),
        P(),
        P(),
        P("groups"),
        P("groups"),
    )
    return jax.shard_map(
        local,
        mesh=mesh,
        in_specs=placed,
        out_specs=(P(("groups", "seq"), None), P("groups", None, "seq")),
        check_vma=False,
    )
```

profile of v0, /device:TPU:18, one launch (start us, length us, event | category | flops | bytes accessed | tf_op | source)
XLA Modules:
  0.0 292.7 jit_solution(8408316643419227497)
XLA Ops:
  0.6 0.9 slice.335
  1.6 1.9 collective-permute-start
  3.5 1.1 slice.361
  4.6 3.5 %collective-permute-start.1 = (bf16[12,12288]{1,0:T(8,128)(2,1)S(1)}, bf16[12,12288]{1,0:T(8,128)(2,1)S(1)}, u32[]{:S(2)}, u32[]{:S(2)}) collective-permute-start(bf16[12,12288]{1,0:T(8,128)(2,1)S(1)} %slice.361), channel_id=1, source_target_pairs={{0,1},{1,2},{2,3},{3,4},{4,5},{5,6},{6,7},{7,8},{8,9},{9,10},{10,1... | collective-permute-start | bytes 884744 | tf_op jit(solution)/shard_map/ppermute | solution.py:12
  8.2 1.8 slice_convert_fusion.13
  10.0 1.2 slice_convert_fusion.20
  11.3 0.7 convert_reduce_fusion.1
  12.1 1.9 slice_convert_fusion.6
  14.0 1.0 slice_convert_fusion.27
  16.4 0.6 fusion.45
  17.1 0.7 add_maximum_fusion
  17.8 30.0 %select_add_fusion = f32[262,12288]{1,0:T(8,128)S(1)} fusion(bf16[12,12288]{1,0:T(8,128)(2,1)S(1)} %collective-permute-done.1, bf16[256,12288]{1,0:T(8,128)(2,1)} %param.9, f32[12288]{0:T(1024)S(1)} %bitcast.82, f32[12288]{0:T(1024)S(1)} %bitcast.83, f32[12288]{0:T(1024)S(1)} %bitcast.78, f32[12288]{0:T(1024)S(1)} %bitcast.79, f32[12288]{0:T(1024)S(1)} %bitcast.80, ...), kind=kLoop, calls=%fused_computation.12 | loop fusion | flops 151314432 | bytes 19809828 | tf_op jit(solution)/shard_map/add | solution.py:28
  47.8 0.5 fusion.13
  48.4 5.9 %fusion.19 = bf16[256,4096]{1,0:T(8,128)(2,1)S(1)} fusion(f32[262,12288]{1,0:T(8,128)S(1)} %select_add_fusion, bf16[262,4096]{1,0:T(8,128)(2,1)S(1)} %fusion.13, f32[4096]{0:T(1024)S(1)} %convert_element_type.327, f32[4096]{0:T(1024)S(1)} %convert_element_type.323, f32[4096]{0:T(1024)S(1)} %convert_element_type.319, f32[4096]{0:T(1024)S(1)} %convert_element_type.315, ...), kind=kLoop, calls=%fused_computation.47 | loop fusion | flops 29360128 | bytes 21087744 | tf_op jit(solution)/shard_map/convert_element_type | solution.py:123
  54.3 2.1 collective-permute-start.2
  56.4 11.7 %select_add_fusion.1 = f32[256,8192]{1,0:T(8,128)S(1)} fusion(bf16[256,8192]{1,0:T(8,128)(2,1)S(1)} %copy-done.2, bf16[6,8192]{1,0:T(8,128)(2,1)S(1)} %collective-permute-done, f32[8192]{0:T(1024)S(1)} %bitcast.85, f32[8192]{0:T(1024)S(1)} %bitcast.86, f32[8192]{0:T(1024)S(1)} %bitcast.87, f32[8192]{0:T(1024)S(1)} %bitcast.88, f32[8192]{0:T(1024)S(1)} %bitcast.89, ...), kind=kLoop, calls=%fused_computation.20 | loop fusion | flops 92274688 | bytes 12912128 | tf_op jit(solution)/shard_map/add | solution.py:28
  68.1 6.4 %fusion.20 = bf16[256,4096]{1,0:T(8,128)(2,1)S(1)} fusion(f32[256,8192]{1,0:T(8,128)S(1)} %select_add_fusion.1, bf16[256,4096]{1,0:T(8,128)(2,1)S(1)} %fusion.19, bf16[6,4096]{1,0:T(8,128)(2,1)S(1)} %collective-permute-done.2, f32[4096]{0:T(1024)S(1)} %bitcast.96, f32[4096]{0:T(1024)S(1)} %bitcast.97, f32[4096]{0:T(1024)S(1)} %bitcast.92, ...), kind=kLoop, calls=%fused_computation.49 | loop fusion | flops 48234496 | bytes 8553984 | tf_op jit(solution)/shard_map/convert_element_type | solution.py:131
  74.5 0.3 slice.463
  74.8 3.5 %collective-permute-start.3 = (bf16[127,4096]{1,0:T(8,128)(2,1)S(1)}, bf16[127,4096]{1,0:T(8,128)(2,1)}, u32[]{:S(2)}, u32[]{:S(2)}) collective-permute-start(bf16[127,4096]{1,0:T(8,128)(2,1)S(1)} %slice.463), channel_id=1, source_target_pairs={{0,1},{1,2},{2,3},{3,4},{4,5},{5,6},{6,7},{7,8},{8,9},{9,10},{10,1... | collective-permute-start | bytes 3121160 | tf_op jit(solution)/shard_map/ppermute | solution.py:12
  78.3 1.3 fusion.46
  79.9 0.7 compare_select_fusion
  80.7 11.2 %collective-permute-done.3 = bf16[127,4096]{1,0:T(8,128)(2,1)} collective-permute-done((bf16[127,4096]{1,0:T(8,128)(2,1)S(1)}, bf16[127,4096]{1,0:T(8,128)(2,1)}, u32[]{:S(2)}, u32[]{:S(2)}) %collective-permute-start.3) | collective-permute-done | bytes 1040416 | tf_op jit(solution)/shard_map/ppermute | solution.py:12
  91.9 2.1 pad_maximum_fusion.2
  94.1 1.7 copy-done.1
  95.7 4.3 %convolution_convert_fusion = bf16[4,127,4096]{2,1,0:T(8,128)(2,1)} fusion(bf16[384,4096]{1,0:T(8,128)(2,1)S(1)} %pad_maximum_fusion.2, s32[4,127]{1,0:T(4,128)S(1)} %fusion.41, pred[4,127]{1,0:T(4,128)(4,1)S(1)} %fusion.42), kind=kOutput, calls=%fused_computation.32 | convolution fusion | flops 1600500736 | bytes 7309804 | tf_op jit(solution)/shard_map/ris,sc->ric/dot_general | solution.py:84
  100.1 7.5 %copy.43 = bf16[4,127,4096]{1,0,2:T(4,128)(2,1)} copy(bf16[4,127,4096]{2,1,0:T(8,128)(2,1)} %convolution_convert_fusion) | data formatting | bytes 8323072 | tf_op jit(solution)/shard_map/convert_element_type | solution.py:85
  107.6 5.4 %all-to-all-start = ((bf16[4,127,4096]{1,0,2:T(4,128)(2,1)}), bf16[4,127,4096]{1,0,2:T(4,128)(2,1)}, u32[]{:S(2)}, u32[]{:S(2)}) async-start(bf16[4,127,4096]{1,0,2:T(4,128)(2,1)} %copy.43), calls=%async_computation | async-start | bytes 8388608 | tf_op jit(solution)/shard_map/all_to_all | solution.py:144
  113.1 10.5 %tile.4 = bf16[128,384,256]{2,1,0:T(8,128)(2,1)} broadcast(bf16[384,256]{1,0:T(8,128)(2,1)S(1)} %pad_maximum_fusion.4), dimensions={1,2} | broadcast | bytes 25362432 | tf_op jit(solution)/shard_map/tile | solution.py:38
  123.5 20.4 %slice.465 = bf16[49024,256]{1,0:T(8,128)(2,1)} slice(bf16[49152,256]{1,0:T(8,128)(2,1)} %bitcast.73), slice={[0:49024], [0:256]} | slice | bytes 50200576 | tf_op jit(solution)/shard_map/slice | solution.py:38
  143.9 24.6 %reshape.350 = bf16[128,383,256]{2,1,0:T(8,128)(2,1)} reshape(bf16[49024,256]{1,0:T(8,128)(2,1)} %slice.465) | data formatting | bytes 50200576 | tf_op jit(solution)/shard_map/reshape | solution.py:39
  168.6 16.3 %slice.466 = bf16[128,256,256]{2,1,0:T(8,128)(2,1)} slice(bf16[128,383,256]{2,1,0:T(8,128)(2,1)} %reshape.350), slice={[0:128], [127:383], [0:256]} | slice | bytes 33554432 | tf_op jit(solution)/shard_map/slice | solution.py:40
  184.9 23.0 %copy.47 = bf16[128,256,256]{1,0,2:T(8,128)(2,1)} copy(bf16[128,256,256]{2,1,0:T(8,128)(2,1)} %slice.466) | data formatting | bytes 33554432
  208.4 2.5 copy.38
  210.9 4.0 %concatenate.36 = bf16[2,128,256,1,16]{1,0,4,2,3:T(2,128)(2,1)} reshape(bf16[256,4096]{0,1:T(8,128)(2,1)} %copy.38) | data formatting | bytes 4194304 | tf_op jit(solution)/shard_map/concatenate | solution.py:49
  214.9 3.1 %slice.464 = bf16[256,4096]{1,0:T(8,128)(2,1)} slice(bf16[384,4096]{1,0:T(8,128)(2,1)} %copy-done.1), slice={[0:256], [0:4096]} | slice | bytes 4194304 | tf_op jit(solution)/shard_map/slice | solution.py:49
  218.0 4.1 %copy.37 = bf16[256,4096]{0,1:T(8,128)(2,1)} copy(bf16[256,4096]{1,0:T(8,128)(2,1)} %slice.464) | data formatting | bytes 4194304 | tf_op jit(solution)/shard_map/slice | solution.py:49
  222.1 4.0 %concatenate.35 = bf16[2,128,256,1,16]{1,0,4,2,3:T(2,128)(2,1)} reshape(bf16[256,4096]{0,1:T(8,128)(2,1)} %copy.37) | data formatting | bytes 4194304 | tf_op jit(solution)/shard_map/concatenate | solution.py:49
  226.1 9.8 %maximum_bitcast_fusion = bf16[2,256,256,16]{1,0,3,2:T(2,128)(2,1)} fusion(bf16[2,128,256,1,16]{1,0,4,2,3:T(2,128)(2,1)} %concatenate.36, bf16[2,128,256,1,16]{1,0,4,2,3:T(2,128)(2,1)} %concatenate.35), kind=kLoop, calls=%fused_computation.56 | loop fusion | flops 8388608 | bytes 8388608 | tf_op jit(solution)/shard_map/jit(_where)/broadcast_in_dim | solution.py:58
  235.9 3.1 %copy.39 = bf16[2,256,256,16]{1,3,0,2:T(8,128)(2,1)S(1)} copy(bf16[2,256,256,16]{1,0,3,2:T(2,128)(2,1)} %maximum_bitcast_fusion) | data formatting | bytes 8388608 | tf_op jit(solution)/shard_map/jit(_where)/broadcast_in_dim | solution.py:58
  239.0 11.7 %fusion = f32[2,128,256,16]{1,3,0,2:T(8,128)} fusion(f32[2,128,5]{1,2,0:T(8,128)S(1)} %fusion.36, bf16[128,256,256]{1,0,2:T(8,128)(2,1)} %copy.47, pred[2,256,5]{1,2,0:T(8,128)(4,1)S(1)} %iota_compare_fusion.1, bf16[2,256,256,16]{1,3,0,2:T(8,128)(2,1)S(1)} %copy.39), kind=kOutput, calls=%fused_computation.1 | convolution fusion | flops 2704277504 | bytes 25173504 | tf_op jit(solution)/shard_map/tsf,bsfjg->btfjg/dot_general | solution.py:62
  250.7 4.3 %copy.41 = f32[2,128,256,16]{1,0,3,2:T(2,128)S(1)} copy(f32[2,128,256,16]{1,3,0,2:T(8,128)} %fusion) | data formatting | bytes 8388608 | tf_op jit(solution)/shard_map/reduce_sum | solution.py:64
  255.0 2.2 copy.50
  257.3 5.6 %copy.42 = f32[256,4096]{1,0:T(8,128)} copy(f32[256,4096]{0,1:T(8,128)} %bitcast.75) | data formatting | bytes 8388608 | tf_op jit(solution)/shard_map/reshape | solution.py:65
  262.9 5.8 %fusion.21 = bf16[256,4096]{1,0:T(8,128)(2,1)} fusion(f32[256,8192]{1,0:T(8,128)} %copy-done, f32[256,4096]{1,0:T(8,128)} %copy.42, bf16[256,4096]{1,0:T(8,128)(2,1)S(1)} %fusion.20, f32[4096]{0:T(1024)S(1)} %convert_element_type.338), kind=kLoop, calls=%fused_computation.51 | loop fusion | flops 7340032 | bytes 12599296 | tf_op jit(solution)/shard_map/convert_element_type | solution.py:160
  268.7 4.7 %copy.44 = bf16[4,127,4096]{1,2,0:T(8,128)(2,1)} copy(bf16[4,127,4096]{1,0,2:T(4,128)(2,1)} %all-to-all-done) | data formatting | bytes 8323072 | tf_op jit(solution)/shard_map/all_to_all | solution.py:144
  273.3 8.1 %copy.45 = bf16[16,4,127,256]{3,1,0,2:T(4,128)(2,1)} copy(bf16[16,4,127,256]{2,3,0,1:T(8,128)(2,1)} %bitcast.76) | data formatting | bytes 8323072 | tf_op jit(solution)/shard_map/all_to_all | solution.py:144
  281.4 7.5 %all_to_all.16 = bf16[64,127,256]{2,0,1:T(8,128)(2,1)} reshape(bf16[16,4,127,256]{3,1,0,2:T(4,128)(2,1)} %copy.45) | data formatting | bytes 8323072 | tf_op jit(solution)/shard_map/all_to_all | solution.py:144
  288.9 3.8 %convolution_convert_fusion.1 = bf16[16,127,256]{2,0,1:T(8,128)(2,1)} fusion(bf16[64,127,256]{2,0,1:T(8,128)(2,1)} %all_to_all.16, s32[64]{0:T(128)S(1)} %compare_select_fusion.1), kind=kOutput, calls=%fused_computation.69 | convolution fusion | flops 67105792 | bytes 5202176 | tf_op jit(solution)/shard_map/ts,sic->tic/dot_general | solution.py:92
  (57 shorter events, 2.6 us)
Async XLA Ops:
  0.6 15.8 %copy-start.4 = (s32[16]{0:T(128)S(1)}, s32[16]{0:T(128)}, u32[]{:S(2)}) copy-start(s32[16]{0:T(128)} %param.16) | copy-start | bytes 196
  1.6 54.8 %collective-permute-start = (bf16[6,8192]{1,0:T(8,128)(2,1)S(1)}, bf16[6,8192]{1,0:T(8,128)(2,1)S(1)}, u32[]{:S(2)}, u32[]{:S(2)}) collective-permute-start(bf16[6,8192]{1,0:T(8,128)(2,1)S(1)} %slice.335), channel_id=1, source_target_pairs={{0,1},{1,2},{2,3},{3,4},{4,5},{5,6},{6,7},{7,8},{8,9},{9,10},{10,1... | collective-permute-start | bytes 294920 | tf_op jit(solution)/shard_map/ppermute | solution.py:12
  4.6 13.2 %collective-permute-start.1 = (bf16[12,12288]{1,0:T(8,128)(2,1)S(1)}, bf16[12,12288]{1,0:T(8,128)(2,1)S(1)}, u32[]{:S(2)}, u32[]{:S(2)}) collective-permute-start(bf16[12,12288]{1,0:T(8,128)(2,1)S(1)} %slice.361), channel_id=1, source_target_pairs={{0,1},{1,2},{2,3},{3,4},{4,5},{5,6},{6,7},{7,8},{8,9},{9,10},{10,1... | collective-permute-start | bytes 884744 | tf_op jit(solution)/shard_map/ppermute | solution.py:12
  48.3 8.1 %copy-start.2 = (bf16[256,8192]{1,0:T(8,128)(2,1)S(1)}, bf16[256,8192]{1,0:T(8,128)(2,1)}, u32[]{:S(2)}) copy-start(bf16[256,8192]{1,0:T(8,128)(2,1)} %param.10) | copy-start | bytes 12582916
  54.3 13.8 %collective-permute-start.2 = (bf16[6,4096]{1,0:T(8,128)(2,1)S(1)}, bf16[6,4096]{1,0:T(8,128)(2,1)S(1)}, u32[]{:S(2)}, u32[]{:S(2)}) collective-permute-start(bf16[6,4096]{1,0:T(8,128)(2,1)S(1)} %slice.452), channel_id=1, source_target_pairs={{0,1},{1,2},{2,3},{3,4},{4,5},{5,6},{6,7},{7,8},{8,9},{9,10},{10,1... | collective-permute-start | bytes 147464 | tf_op jit(solution)/shard_map/ppermute | solution.py:12
  68.1 6.4 %copy-start = (f32[256,8192]{1,0:T(8,128)}, f32[256,8192]{1,0:T(8,128)S(1)}, u32[]{:S(2)}) copy-start(f32[256,8192]{1,0:T(8,128)S(1)} %select_add_fusion.1) | copy-start | bytes 25165828
  74.8 17.1 %collective-permute-start.3 = (bf16[127,4096]{1,0:T(8,128)(2,1)S(1)}, bf16[127,4096]{1,0:T(8,128)(2,1)}, u32[]{:S(2)}, u32[]{:S(2)}) collective-permute-start(bf16[127,4096]{1,0:T(8,128)(2,1)S(1)} %slice.463), channel_id=1, source_target_pairs={{0,1},{1,2},{2,3},{3,4},{4,5},{5,6},{6,7},{7,8},{8,9},{9,10},{10,1... | collective-permute-start | bytes 3121160 | tf_op jit(solution)/shard_map/ppermute | solution.py:12
  94.1 1.7 copy-start.1
  107.6 5.4 %copy-start.3 = (bf16[128,256]{1,0:T(8,128)(2,1)S(1)}, bf16[128,256]{1,0:T(8,128)(2,1)}, u32[]{:S(2)}) copy-start(bf16[128,256]{1,0:T(8,128)(2,1)} %param.14) | copy-start | bytes 196612
  107.6 161.1 %all-to-all-start = ((bf16[4,127,4096]{1,0,2:T(4,128)(2,1)}), bf16[4,127,4096]{1,0,2:T(4,128)(2,1)}, u32[]{:S(2)}, u32[]{:S(2)}) async-start(bf16[4,127,4096]{1,0,2:T(4,128)(2,1)} %copy.43), calls=%async_computation | async-start | bytes 8388608 | tf_op jit(solution)/shard_map/all_to_all | solution.py:144
  184.9 23.0 %copy-start.5 = (bf16[4096]{0:T(1024)(128)(2,1)S(1)}, bf16[4096]{0:T(1024)(128)(2,1)}, u32[]{:S(2)}) copy-start(bf16[4096]{0:T(1024)(128)(2,1)} %param.15) | copy-start | bytes 24580
  184.9 23.3 %copy-start.6 = (s32[16]{0:T(128)S(1)}, s32[16]{0:T(128)}, u32[]{:S(2)}) copy-start(s32[16]{0:T(128)} %param.17) | copy-start | bytes 196
where the time goes:
time: 297 us; the launch traced here: 293 us
  local copies, waits for them, and re-layouts  161 us (54%)
  other arithmetic  83.2 us (28%)
  matrix products  19.8 us (7%)
  starting transfers between devices  16.4 us (6%)
  waiting for transfers between devices  11.2 us (4%)
    add x2, other arithmetic, short_conv(): summed + jnp.where(same_req[:, None], earlier * weights[lag_step].astype(...  41.7 us
    unnamed x16, local copies, waits for them, and re-layouts  26.9 us
    reshape x1, local copies, waits for them, and re-layouts, toeplitz(): skewed = tiled.reshape(tap_count, 3 * tap_count - 1, taps_table.shape[1])  24.6 us
    slice x1, local copies, waits for them, and re-layouts, toeplitz(): jnp.tile(row_vector, (tap_count, 1))[:tap_count * (3 * tap_count - 1)]  20.4 us
    all_to_all x3, local copies, waits for them, and re-layouts, local(): lax.all_to_all(states, 'seq', split_axis=2, concat_axis=0, tiled=True)  20.2 us
    slice x1, local copies, waits for them, and re-layouts, toeplitz(): return skewed[:, tap_count - 1:3 * tap_count - 1]  16.3 us
    dot_general x1, matrix products, long_conv(): jnp.einsum('tsf,bsfjg->btfjg', matrix, stacked, preferred_element_type=jn...  11.7 us
    ppermute x4, waiting for transfers between devices, passed_along(): return lax.ppermute(x, axis, pairs)  11.2 us
  transfers between devices with their start and end apart: 5, of which 1 were waited for; matrix products, arithmetic and copies ran while one was open for 74% of the time, Pallas kernels for 0%

commit v1 on v0

--- a/solution.py
+++ b/solution.py
@@ -2,6 +2,8 @@
 import jax.numpy as jnp
 from jax import lax
 from jax.sharding import PartitionSpec as P
+from jax.experimental import pallas as pl
+from jax.experimental.pallas import tpu as pltpu
 
 ENDS_MAX = 4
 
@@ -31,13 +33,78 @@
     return summed
 
 
+HALO = 32
+TILE = 512
+
+
+def chain_kernel(dist_ref, sq, sk, sv, hq, hk, hv, mq, mk, gq_h, gk_h, fq, fk, fv, filt, wq, wk, wv,
+                 z2_ref, q2_ref, xq, xk, xv, xa, xb, zs, ys):
+    rows = xq.shape[0]
+    for main, halo, x in ((sq, hq, xq), (sk, hk, xk), (sv, hv, xv), (mq, gq_h, xa), (mk, gk_h, xb)):
+        x[0:HALO, :] = halo[...].astype(jnp.float32)
+        x[HALO:rows, :] = main[...].astype(jnp.float32)
+
+    def sconv(x, w, first):
+        dist = dist_ref[first:rows, :]
+        acc = x[first:rows, :] * w[0:1, :]
+        for lag in range(1, w.shape[0]):
+            term = x[first - lag : rows - lag, :] * w[lag : lag + 1, :]
+            acc = acc + jnp.where(dist >= lag, term, 0.0)
+        return acc
+
+    k1 = sconv(xk, fk, 16)
+    v1 = sconv(xv, fv, 16)
+    zs[16:rows, :] = (k1 * v1).astype(jnp.bfloat16).astype(jnp.float32)
+    q1 = sconv(xq, fq, 24)
+    c1 = sconv(zs, filt, 24)
+    ys[24:rows, :] = (q1 * c1).astype(jnp.bfloat16).astype(jnp.float32)
+    v2 = sconv(ys, wv, HALO)
+    k2 = sconv(xb, wk, HALO)
+    z2_ref[...] = (k2 * v2).astype(jnp.bfloat16)
+    q2_ref[...] = sconv(xa, wq, HALO)
+
+
+def short_chain(dist, se_streams, se_halo, mr_gates, mr_halo, se_feat, se_filt, mr_feat):
+    tok_rows = se_streams.shape[0]
+    channels = mr_gates.shape[1] // 2
+    steps = channels // TILE
+    rows = tok_rows + HALO
+    taps = se_feat.shape[0]
+
+    def col(part):
+        return lambda j: (0, j + part * steps)
+
+    main = [pl.BlockSpec((tok_rows, TILE), col(p)) for p in range(3)]
+    halo = [pl.BlockSpec((HALO, TILE), col(p)) for p in range(3)]
+    wts = [pl.BlockSpec((taps, TILE), col(p)) for p in range(3)]
+    return pl.pallas_call(
+        chain_kernel,
+        grid=(steps,),
+        in_specs=[pl.BlockSpec((rows, 1), lambda j: (0, 0))] + main + halo + main[:2] + halo[:2] + wts
+        + [wts[0]] + wts,
+        out_specs=[pl.BlockSpec((tok_rows, TILE), col(0)), pl.BlockSpec((tok_rows, TILE), col(0))],
+        out_shape=[jax.ShapeDtypeStruct((tok_rows, channels), jnp.bfloat16),
+                   jax.ShapeDtypeStruct((tok_rows, channels), jnp.float32)],
+        scratch_shapes=[pltpu.VMEM((rows, TILE), jnp.float32) for _ in range(7)],
+    )(dist, se_streams, se_streams, se_streams, se_halo, se_halo, se_halo, mr_gates, mr_gates,
+      mr_halo, mr_halo, se_feat, se_feat, se_feat, se_filt, mr_feat, mr_feat, mr_feat)
+
+
+def seg_start(positions, req_ends):
+    seg = request_of(positions, req_ends)
+    prev_end = jnp.where(seg > 0, pick_entries(req_ends, jnp.maximum(seg - 1, 0)), -1)
+    return prev_end + 1
+
+
 def toeplitz(taps_table):
     tap_count = taps_table.shape[0]
-    zero_rows = jnp.zeros_like(taps_table)
-    row_vector = jnp.concatenate([zero_rows, taps_table[::-1], zero_rows], axis=0)
-    tiled = jnp.tile(row_vector, (tap_count, 1))[: tap_count * (3 * tap_count - 1)]
-    skewed = tiled.reshape(tap_count, 3 * tap_count - 1, taps_table.shape[1])
-    return skewed[:, tap_count - 1 : 3 * tap_count - 1]
+    t_ids = jnp.arange(tap_count, dtype=jnp.int32)[:, None, None]
+    s_ids = jnp.arange(2 * tap_count, dtype=jnp.int32)[None, :, None]
+    j_ids = jnp.arange(tap_count, dtype=jnp.int32)[None, None, :]
+    onehot = (tap_count + t_ids - s_ids == j_ids).astype(taps_table.dtype)
+    return jnp.einsum("tsj,jf->tsf", onehot, taps_table, preferred_element_type=jnp.float32).astype(
+        taps_table.dtype
+    )
 
 
 def long_conv(z_ext, segment, taps_table, slot_count):
@@ -109,26 +176,22 @@
     slot_total = ENDS_MAX + 1
     rim_depth = 2 * reach_rows
     prev_se, prev_mr = passed_along(
-        (se_streams[tok_rows - rim_depth :], mr_gates[tok_rows - reach_rows :]), "seq", 1
-    )
-    se_ext = jnp.concatenate([prev_se, se_streams], axis=0)
-    seg_ext = request_of(
-        offset - rim_depth + jnp.arange(tok_rows + rim_depth, dtype=jnp.int32), req_ends
-    )
-    featured = short_conv(se_ext, se_feat, seg_ext)
-    z_one = (featured[:, channels : 2 * channels] * featured[:, 2 * channels :]).astype(
-        jnp.bfloat16
-    )
-    conv_one = short_conv(z_one, jnp.repeat(se_filter, group_ch, axis=1), seg_ext[reach_rows:])
-    y_se = (featured[reach_rows:, :channels] * conv_one).astype(jnp.bfloat16)
-    prev_y = passed_along(y_se[tok_rows - reach_rows :], "seq", 1)
-    y_ext = jnp.concatenate([prev_y, y_se], axis=0)
-    seg_mr = seg_ext[rim_depth - reach_rows :]
-    gates_ext = jnp.concatenate([prev_mr, mr_gates], axis=0)
-    gate_feat = short_conv(gates_ext, mr_feat[:, : 2 * channels], seg_mr)
-    value_feat = short_conv(y_ext, mr_feat[:, 2 * channels :], seg_mr)
-    q_two = gate_feat[:, :channels]
-    z_two = (gate_feat[:, channels:] * value_feat).astype(jnp.bfloat16)
+        (se_streams[tok_rows - 3 * reach_rows :], mr_gates[tok_rows - reach_rows :]), "seq", 1
+    )
+    se_halo = jnp.pad(prev_se, ((HALO - 3 * reach_rows, 0), (0, 0)))
+    mr_halo = jnp.pad(prev_mr, ((HALO - reach_rows, 0), (0, 0)))
+    ext_pos = offset - HALO + jnp.arange(tok_rows + HALO, dtype=jnp.int32)
+    dist = (ext_pos - seg_start(ext_pos, req_ends))[:, None]
+    z_two, q_two = short_chain(
+        dist,
+        se_streams,
+        se_halo,
+        mr_gates,
+        mr_halo,
+        se_feat.astype(jnp.float32),
+        jnp.repeat(se_filter, group_ch, axis=1).astype(jnp.float32),
+        mr_feat.astype(jnp.float32),
+    )
     prev_z = passed_along(z_two[tok_rows - tail_len :], "seq", 1)
     z_ext = jnp.concatenate([jnp.zeros((1, channels), jnp.bfloat16), prev_z, z_two], axis=0)
     seg_long = request_of(

time: 297 us -> 221 us (0.74)
  local copies, waits for them, and re-layouts: 161 us -> 93.2 us
  other arithmetic: 83.2 us -> 28 us
  Pallas kernels: 0 us -> 41.7 us
  matrix products: 19.8 us -> 28.9 us
  starting transfers between devices: 16.4 us -> 12.6 us
    pallas_call x0 -> x1, Pallas kernels: none -> 41.7 us  [short_chain(): pl.pallas_call(chain_kernel, grid=(steps,), in_specs=[pl.BlockSpec((rows,...]
    add x3, other arithmetic: 41.7 us -> 0.01 us  [the longest x1 0.01 us: seg_start(): return prev_end + 1]
    slice x4 -> x1, local copies, waits for them, and re-layouts: 37.8 us -> 1.24 us  [local(): se_streams[tok_rows - 3 * reach_rows:]]
    reshape x1 -> x0, local copies, waits for them, and re-layouts: 24.6 us -> none  [toeplitz(): skewed = tiled.reshape(tap_count, 3 * tap_count - 1, taps_table.shape[1])]
    unnamed x16 -> x15, local copies, waits for them, and re-layouts: 26.9 us -> 3.91 us
    convert_element_type x8 -> x2, local copies, waits for them, and re-layouts: 3.17 us -> 24.3 us  [the longest x1 23.1 us: toeplitz(): jnp.einsum('tsj,jf->tsf', onehot, taps_table, preferred_element_type=jnp....]
    another operation x1 -> x0, local copies, waits for them, and re-layouts: 10.5 us -> none  [toeplitz(): jnp.tile(row_vector, (tap_count, 1))[:tap_count * (3 * tap_count - 1)]]
    convert_element_type x4 -> x2, other arithmetic: 13.8 us -> 3.42 us  [the longest x1 1.71 us: local(): mr_feat.astype(jnp.float32)]
  transfers between devices with their start and end apart: 5 -> 4, of which waited for: 1 -> 1; matrix products, arithmetic and copies ran while one was open for 74% -> 49% of each run, Pallas kernels for 0% -> 0%
where the time goes in v1:
time: 221 us; the launch traced here: 218 us
  local copies, waits for them, and re-layouts  93.2 us (42%)
  Pallas kernels  41.7 us (19%)
  matrix products  28.9 us (13%)
  other arithmetic  28 us (13%)
  waiting for transfers between devices  12.8 us (6%)
  starting transfers between devices  12.6 us (6%)
    pallas_call x1, Pallas kernels, short_chain(): pl.pallas_call(chain_kernel, grid=(steps,), in_specs=[pl.BlockSpec((rows,...  41.7 us
    convert_element_type x1, local copies, waits for them, and re-layouts, toeplitz(): jnp.einsum('tsj,jf->tsf', onehot, taps_table, preferred_element_type=jnp....  23.1 us
    all_to_all x3, local copies, waits for them, and re-layouts, local(): lax.all_to_all(states, 'seq', split_axis=2, concat_axis=0, tiled=True)  20.2 us
    ppermute x3, waiting for transfers between devices, passed_along(): return lax.ppermute(x, axis, pairs)  12.8 us
    dot_general x1, matrix products, long_conv(): jnp.einsum('tsf,bsfjg->btfjg', matrix, stacked, preferred_element_type=jn...  11.6 us
    broadcast_in_dim x1, other arithmetic, long_conv(): jnp.where(source_hit[:, :, None, :, None], grouped[:, :, :, None, :], jnp...  9.8 us
    dot_general x1, matrix products, toeplitz(): jnp.einsum('tsj,jf->tsf', onehot, taps_table, preferred_element_type=jnp....  9.12 us
    concatenate x2, local copies, waits for them, and re-layouts, long_conv(): window = jnp.concatenate([shaped[:-1], shaped[1:]], axis=1)  7.94 us
  transfers between devices with their start and end apart: 4, of which 1 were waited for; matrix products, arithmetic and copies ran while one was open for 49% of the time, Pallas kernels for 0%

profile of v1, /device:TPU:18, one launch (start us, length us, event | category | flops | bytes accessed | tf_op | source)
XLA Modules:
  0.0 218.0 jit_solution(6467280142766848520)
XLA Ops:
  0.7 1.2 slice.51
  1.9 1.9 collective-permute-start
  3.8 0.9 slice.52
  4.8 3.5 %collective-permute-start.1 = (bf16[6,8192]{1,0:T(8,128)(2,1)S(1)}, bf16[6,8192]{1,0:T(8,128)(2,1)S(1)}, u32[]{:S(2)}, u32[]{:S(2)}) collective-permute-start(bf16[6,8192]{1,0:T(8,128)(2,1)S(1)} %slice.52), channel_id=1, source_target_pairs={{0,1},{1,2},{2,3},{3,4},{4,5},{5,6},{6,7},{7,8},{8,9},{9,10},{10,1... | collective-permute-start | bytes 294920 | tf_op jit(solution)/shard_map/ppermute | solution.py:14
  8.3 0.7 convert_reduce_fusion.1
  9.1 0.7 select_reduce_fusion
  9.8 1.7 convert_element_type.70.fq.fk.fv
  11.5 1.0 broadcast_in_dim.68
  12.5 1.2 convert_element_type.72.filt
  13.7 1.7 convert_element_type.73.wq.wk.wv
  15.4 0.7 fusion.25
  16.1 0.8 reshape_subtract_fusion.dist_ref
  16.9 0.6 add_maximum_fusion.1
  17.5 0.8 pad.9.gq_h.gk_h
  18.4 1.0 pad.8.hq.hk.hv
  19.4 41.7 %shard_map.104 = (bf16[256,4096]{1,0:T(8,128)(2,1)}, f32[256,4096]{1,0:T(8,128)}) custom-call(s32[288,1]{1,0:T(8,128)} %reshape_subtract_fusion.dist_ref, bf16[256,12288]{1,0:T(8,128)(2,1)} %sv.1, bf16[256,12288]{1,0:T(8,128)(2,1)} %sv.1, bf16[256,12288]{1,0:T(8,128)(2,1)} %sv.1, bf16[32,12288]{1,0:T(8,128)(2,1)} %pad.8.hq.hk.hv, ...), custom_call_target="tpu_custom_call" | custom-call | tf_op jit(solution)/shard_map/pallas_call | solution.py:80
  61.1 1.5 slice.59
  62.6 1.9 collective-permute-start.2
  64.5 1.3 fusion.26
  65.8 0.2 select_reduce_fusion.2
  66.1 0.6 compare_select_fusion
  66.9 12.8 %collective-permute-done.2 = bf16[127,4096]{1,0:T(8,128)(2,1)S(1)} collective-permute-done((bf16[127,4096]{1,0:T(8,128)(2,1)S(1)}, bf16[127,4096]{1,0:T(8,128)(2,1)S(1)}, u32[]{:S(2)}, u32[]{:S(2)}) %collective-permute-start.2) | collective-permute-done | bytes 1040416 | tf_op jit(solution)/shard_map/ppermute | solution.py:14
  79.6 2.5 %pad_maximum_fusion = bf16[384,4096]{1,0:T(8,128)(2,1)S(1)} fusion(bf16[256,4096]{1,0:T(8,128)(2,1)} %get-tuple-element.5, bf16[127,4096]{1,0:T(8,128)(2,1)S(1)} %collective-permute-done.2, bf16[384]{0:T(512)(128)(2,1)S(1)} %pad.12.clone), kind=kLoop, calls=%fused_computation.16 | loop fusion | flops 9437184 | bytes 6284032 | tf_op jit(solution)/shard_map/concatenate | solution.py:196
  82.2 1.6 copy-done.3
  83.8 4.3 %convolution_convert_fusion = bf16[4,127,4096]{2,1,0:T(8,128)(2,1)} fusion(bf16[384,4096]{1,0:T(8,128)(2,1)S(1)} %pad_maximum_fusion, s32[4,127]{1,0:T(4,128)S(1)} %fusion.21, pred[4,127]{1,0:T(4,128)(4,1)S(1)} %fusion.22), kind=kOutput, calls=%fused_computation.11 | convolution fusion | flops 1600500736 | bytes 7309804 | tf_op jit(solution)/shard_map/ris,sc->ric/dot_general | solution.py:151
  88.2 7.4 %copy.56 = bf16[4,127,4096]{1,0,2:T(4,128)(2,1)} copy(bf16[4,127,4096]{2,1,0:T(8,128)(2,1)} %convolution_convert_fusion) | data formatting | bytes 8323072 | tf_op jit(solution)/shard_map/convert_element_type | solution.py:152
  95.6 5.2 %all-to-all-start = ((bf16[4,127,4096]{1,0,2:T(4,128)(2,1)}), bf16[4,127,4096]{1,0,2:T(4,128)(2,1)}, u32[]{:S(2)}, u32[]{:S(2)}) async-start(bf16[4,127,4096]{1,0,2:T(4,128)(2,1)} %copy.56), calls=%async_computation | async-start | bytes 8388608 | tf_op jit(solution)/shard_map/all_to_all | solution.py:207
  100.9 9.1 %convert_bitcast_fusion = bf16[128,256,256,1,1]{2,1,0,4,3:T(8,128)(2,1)} fusion(s32[128,256]{1,0:T(8,128)S(1)} %iota_subtract_fusion, bf16[128,256]{1,0:T(8,128)(2,1)S(1)} %copy-done), kind=kOutput, calls=%fused_computation.5 | convolution fusion | flops 2160066560 | bytes 16973824 | tf_op jit(solution)/shard_map/tsj,jf->tsf/dot_general | solution.py:105
  110.1 23.1 %copy.59 = bf16[128,256,256,1,1]{1,0,4,3,2:T(8,128)(2,1)} copy(bf16[128,256,256,1,1]{2,1,0,4,3:T(8,128)(2,1)} %convert_bitcast_fusion) | data formatting | bytes 33554432 | tf_op jit(solution)/shard_map/convert_element_type | solution.py:105
  133.2 0.1 convert_reduce_fusion
  133.3 0.1 slice_reduce_fusion
  133.5 0.1 select_reduce_fusion.1
  133.8 2.5 %copy.51 = bf16[256,4096]{0,1:T(8,128)(2,1)} copy(bf16[256,4096]{1,0:T(8,128)(2,1)S(1)} %copy-done.2) | data formatting | bytes 4194304 | tf_op jit(solution)/shard_map/pallas_call | solution.py:80
  136.2 4.0 %concatenate.21 = bf16[2,128,256,1,16]{1,0,4,2,3:T(2,128)(2,1)} reshape(bf16[256,4096]{0,1:T(8,128)(2,1)} %copy.51) | data formatting | bytes 4194304 | tf_op jit(solution)/shard_map/concatenate | solution.py:116
  140.2 3.1 %slice.61 = bf16[256,4096]{1,0:T(8,128)(2,1)} slice(bf16[384,4096]{1,0:T(8,128)(2,1)} %copy-done.3), slice={[0:256], [0:4096]} | slice | bytes 4194304 | tf_op jit(solution)/shard_map/slice | solution.py:116
  143.3 4.1 %copy.50 = bf16[256,4096]{0,1:T(8,128)(2,1)} copy(bf16[256,4096]{1,0:T(8,128)(2,1)} %slice.61) | data formatting | bytes 4194304 | tf_op jit(solution)/shard_map/slice | solution.py:116
  147.4 4.0 %concatenate.20 = bf16[2,128,256,1,16]{1,0,4,2,3:T(2,128)(2,1)} reshape(bf16[256,4096]{0,1:T(8,128)(2,1)} %copy.50) | data formatting | bytes 4194304 | tf_op jit(solution)/shard_map/concatenate | solution.py:116
  151.4 9.8 %maximum_bitcast_fusion = bf16[2,256,256,16]{1,0,3,2:T(2,128)(2,1)} fusion(bf16[2,128,256,1,16]{1,0,4,2,3:T(2,128)(2,1)} %concatenate.21, bf16[2,128,256,1,16]{1,0,4,2,3:T(2,128)(2,1)} %concatenate.20), kind=kLoop, calls=%fused_computation.13 | loop fusion | flops 8388608 | bytes 8388608 | tf_op jit(solution)/shard_map/jit(_where)/broadcast_in_dim | solution.py:125
  161.2 3.1 %copy.52 = bf16[2,256,256,16]{1,3,0,2:T(8,128)(2,1)S(1)} copy(bf16[2,256,256,16]{1,0,3,2:T(2,128)(2,1)} %maximum_bitcast_fusion) | data formatting | bytes 8388608 | tf_op jit(solution)/shard_map/jit(_where)/broadcast_in_dim | solution.py:125
  164.3 11.6 %fusion = f32[2,128,256,16]{1,3,0,2:T(8,128)} fusion(f32[2,128,5]{1,2,0:T(8,128)S(1)} %fusion.16, bf16[128,256,256,1,1]{1,0,4,3,2:T(8,128)(2,1)} %copy.59, pred[2,256,5]{1,2,0:T(8,128)(4,1)S(1)} %iota_compare_fusion.6, bf16[2,256,256,16]{1,3,0,2:T(8,128)(2,1)S(1)} %copy.52), kind=kOutput, calls=%fused_computation.1 | convolution fusion | flops 2704277504 | bytes 25173504 | tf_op jit(solution)/shard_map/tsf,bsfjg->btfjg/dot_general | solution.py:129
  176.0 4.3 %copy.54 = f32[2,128,256,16]{1,0,3,2:T(2,128)S(1)} copy(f32[2,128,256,16]{1,3,0,2:T(8,128)} %fusion) | data formatting | bytes 8388608 | tf_op jit(solution)/shard_map/reduce_sum | solution.py:131
  180.3 2.2 %copy.64 = f32[512,8,2,128]{3,1,2,0:T(8,128)} copy(f32[512,8,2,128]{3,2,1,0:T(2,128)S(1)} %bitcast.43) | data formatting | bytes 8388608
  182.6 5.6 %copy.55 = f32[256,4096]{1,0:T(8,128)} copy(f32[256,4096]{0,1:T(8,128)} %bitcast.44) | data formatting | bytes 8388608 | tf_op jit(solution)/shard_map/reshape | solution.py:132
  188.2 5.8 %multiply_convert_fusion = bf16[256,4096]{1,0:T(8,128)(2,1)} fusion(f32[256,4096]{1,0:T(8,128)} %get-tuple-element.4, f32[256,4096]{1,0:T(8,128)} %copy.55, bf16[256,4096]{1,0:T(8,128)(2,1)S(1)} %copy-done.2, f32[4096]{0:T(1024)S(1)} %convert_element_type.77), kind=kLoop, calls=%fused_computation.14 | loop fusion | flops 7340032 | bytes 12599296 | tf_op jit(solution)/shard_map/convert_element_type | solution.py:223
  194.0 4.7 %copy.57 = bf16[4,127,4096]{1,2,0:T(8,128)(2,1)} copy(bf16[4,127,4096]{1,0,2:T(4,128)(2,1)} %all-to-all-done) | data formatting | bytes 8323072 | tf_op jit(solution)/shard_map/all_to_all | solution.py:207
  198.6 8.1 %copy.58 = bf16[16,4,127,256]{3,1,0,2:T(4,128)(2,1)} copy(bf16[16,4,127,256]{2,3,0,1:T(8,128)(2,1)} %bitcast.45) | data formatting | bytes 8323072 | tf_op jit(solution)/shard_map/all_to_all | solution.py:207
  206.7 7.5 %all_to_all.16 = bf16[64,127,256]{2,0,1:T(8,128)(2,1)} reshape(bf16[16,4,127,256]{3,1,0,2:T(4,128)(2,1)} %copy.58) | data formatting | bytes 8323072 | tf_op jit(solution)/shard_map/all_to_all | solution.py:207
  214.2 3.8 %convolution_convert_fusion.1 = bf16[16,127,256]{2,0,1:T(8,128)(2,1)} fusion(bf16[64,127,256]{2,0,1:T(8,128)(2,1)} %all_to_all.16, s32[64]{0:T(128)S(1)} %compare_select_fusion.1), kind=kOutput, calls=%fused_computation.18 | convolution fusion | flops 67105792 | bytes 5202176 | tf_op jit(solution)/shard_map/ts,sic->tic/dot_general | solution.py:159
  (36 shorter events, 0.6 us)
Async XLA Ops:
  0.6 100.3 %copy-start = (bf16[128,256]{1,0:T(8,128)(2,1)S(1)}, bf16[128,256]{1,0:T(8,128)(2,1)}, u32[]{:S(2)}) copy-start(bf16[128,256]{1,0:T(8,128)(2,1)} %param.14) | copy-start | bytes 196612
  0.6 14.7 %copy-start.4 = (s32[16]{0:T(128)S(1)}, s32[16]{0:T(128)}, u32[]{:S(2)}) copy-start(s32[16]{0:T(128)} %param.16) | copy-start | bytes 196
  1.9 16.5 %collective-permute-start = (bf16[18,12288]{1,0:T(8,128)(2,1)S(1)}, bf16[18,12288]{1,0:T(8,128)(2,1)S(1)}, u32[]{:S(2)}, u32[]{:S(2)}) collective-permute-start(bf16[18,12288]{1,0:T(8,128)(2,1)S(1)} %slice.51), channel_id=1, source_target_pairs={{0,1},{1,2},{2,3},{3,4},{4,5},{5,6},{6,7},{7,8},{8,9},{9,10},{10,1... | collective-permute-start | bytes 1327112 | tf_op jit(solution)/shard_map/ppermute | solution.py:14
  4.8 12.7 %collective-permute-start.1 = (bf16[6,8192]{1,0:T(8,128)(2,1)S(1)}, bf16[6,8192]{1,0:T(8,128)(2,1)S(1)}, u32[]{:S(2)}, u32[]{:S(2)}) collective-permute-start(bf16[6,8192]{1,0:T(8,128)(2,1)S(1)} %slice.52), channel_id=1, source_target_pairs={{0,1},{1,2},{2,3},{3,4},{4,5},{5,6},{6,7},{7,8},{8,9},{9,10},{10,1... | collective-permute-start | bytes 294920 | tf_op jit(solution)/shard_map/ppermute | solution.py:14
  62.6 17.0 %collective-permute-start.2 = (bf16[127,4096]{1,0:T(8,128)(2,1)S(1)}, bf16[127,4096]{1,0:T(8,128)(2,1)S(1)}, u32[]{:S(2)}, u32[]{:S(2)}) collective-permute-start(bf16[127,4096]{1,0:T(8,128)(2,1)S(1)} %slice.59), channel_id=1, source_target_pairs={{0,1},{1,2},{2,3},{3,4},{4,5},{5,6},{6,7},{7,8},{8,9},{9,10},{10,1... | collective-permute-start | bytes 3121160 | tf_op jit(solution)/shard_map/ppermute | solution.py:14
  82.2 1.6 copy-start.3
  95.6 98.4 %all-to-all-start = ((bf16[4,127,4096]{1,0,2:T(4,128)(2,1)}), bf16[4,127,4096]{1,0,2:T(4,128)(2,1)}, u32[]{:S(2)}, u32[]{:S(2)}) async-start(bf16[4,127,4096]{1,0,2:T(4,128)(2,1)} %copy.56), calls=%async_computation | async-start | bytes 8388608 | tf_op jit(solution)/shard_map/all_to_all | solution.py:207
  110.0 23.1 %copy-start.5 = (bf16[4096]{0:T(1024)(128)(2,1)S(1)}, bf16[4096]{0:T(1024)(128)(2,1)}, u32[]{:S(2)}) copy-start(bf16[4096]{0:T(1024)(128)(2,1)} %param.15) | copy-start | bytes 24580
  110.0 23.4 %copy-start.6 = (s32[16]{0:T(128)S(1)}, s32[16]{0:T(128)}, u32[]{:S(2)}) copy-start(s32[16]{0:T(128)} %param.17) | copy-start | bytes 196
  110.0 23.7 %copy-start.2 = (bf16[256,4096]{1,0:T(8,128)(2,1)S(1)}, bf16[256,4096]{1,0:T(8,128)(2,1)}, u32[]{:S(2)}) copy-start(bf16[256,4096]{1,0:T(8,128)(2,1)} %get-tuple-element.5) | copy-start | bytes 6291460
  206.7 11.3 %copy-start.1 = (bf16[128,256]{1,0:T(8,128)(2,1)S(1)}, bf16[128,256]{1,0:T(8,128)(2,1)}, u32[]{:S(2)}) copy-start(bf16[128,256]{1,0:T(8,128)(2,1)} %param.14) | copy-start | bytes 196612

commit v2 on v1

--- a/solution.py
+++ b/solution.py
@@ -88,6 +88,60 @@
         scratch_shapes=[pltpu.VMEM((rows, TILE), jnp.float32) for _ in range(7)],
     )(dist, se_streams, se_streams, se_streams, se_halo, se_halo, se_halo, mr_gates, mr_gates,
       mr_halo, mr_halo, se_feat, se_feat, se_feat, se_filt, mr_feat, mr_feat, mr_feat)
+
+
+LANES = 256
+GROUP_LANES = 128
+
+
+def long_kernel(tss_ref, spos_ref, prev_ref, z_ref, q2_ref, skip_ref, u_ref, out_ref):
+    blk = prev_ref.shape[0]
+    tile = z_ref.shape[1]
+    width = u_ref.shape[1]
+    per_group = tile // u_ref.shape[0]
+    z = z_ref[...]
+    windows = (jnp.concatenate([prev_ref[...], z[:blk]], axis=0), z)
+    masks = [
+        spos_ref[:, b * blk : b * blk + width] >= tss_ref[b * blk : (b + 1) * blk, :] for b in range(2)
+    ]
+    lane_grp = lax.broadcasted_iota(jnp.int32, (1, GROUP_LANES), 1) // per_group
+    halves = tile // GROUP_LANES
+    groups_half = GROUP_LANES // per_group
+    acc = [[jnp.zeros((blk, GROUP_LANES), jnp.float32) for _ in range(halves)] for _ in range(2)]
+    for g in range(u_ref.shape[0]):
+        half = g // groups_half
+        row = jnp.broadcast_to(u_ref[g : g + 1, :], (blk, width))
+        taps = pltpu.roll(row, 0, 1, stride=1, stride_axis=0)
+        for b in range(2):
+            mat = jnp.where(masks[b], taps, 0.0).astype(jnp.bfloat16)
+            part = windows[b][:, half * GROUP_LANES : (half + 1) * GROUP_LANES]
+            res = jnp.dot(mat, part, preferred_element_type=jnp.float32)
+            acc[b][half] = jnp.where(lane_grp == g % groups_half, res, acc[b][half])
+    conv = jnp.concatenate([jnp.concatenate(acc[b], axis=1) for b in range(2)], axis=0)
+    mixed = (conv + skip_ref[...] * z.astype(jnp.float32)).astype(jnp.bfloat16)
+    out_ref[...] = (q2_ref[...] * mixed.astype(jnp.float32)).astype(jnp.bfloat16)
+
+
+def long_conv_out(tss, spos, prev_z, z_two, q_two, skip, taps_rows):
+    tok_rows, channels = z_two.shape
+    blk = prev_z.shape[0]
+    steps = channels // LANES
+    per_group = channels // taps_rows.shape[0]
+    return pl.pallas_call(
+        long_kernel,
+        grid=(steps,),
+        in_specs=[
+            pl.BlockSpec(tss.shape, lambda j: (0, 0)),
+            pl.BlockSpec(spos.shape, lambda j: (0, 0)),
+            pl.BlockSpec((blk, LANES), lambda j: (0, j)),
+            pl.BlockSpec((tok_rows, LANES), lambda j: (0, j)),
+            pl.BlockSpec((tok_rows, LANES), lambda j: (0, j)),
+            pl.BlockSpec((1, LANES), lambda j: (0, j)),
+            pl.BlockSpec((LANES // per_group, taps_rows.shape[1]), lambda j: (j, 0)),
+        ],
+        out_specs=pl.BlockSpec((tok_rows, LANES), lambda j: (0, j)),
+        out_shape=jax.ShapeDtypeStruct((tok_rows, channels), jnp.bfloat16),
+    )(tss, spos, prev_z, z_two, q_two, skip, taps_rows)
 
 
 def seg_start(positions, req_ends):
@@ -192,11 +246,8 @@
         jnp.repeat(se_filter, group_ch, axis=1).astype(jnp.float32),
         mr_feat.astype(jnp.float32),
     )
-    prev_z = passed_along(z_two[tok_rows - tail_len :], "seq", 1)
-    z_ext = jnp.concatenate([jnp.zeros((1, channels), jnp.bfloat16), prev_z, z_two], axis=0)
-    seg_long = request_of(
-        offset - tap_count + jnp.arange(tok_rows + tap_count, dtype=jnp.int32), req_ends
-    )
+    prev_z = passed_along(z_two[tok_rows - tap_count :], "seq", 1)
+    z_ext = jnp.concatenate([prev_z, z_two], axis=0)
     first_req = request_of(jnp.reshape(offset, (1,)), req_ends)[0]
     past_req = request_of(jnp.reshape(offset + tok_rows, (1,)), req_ends)[0]
     slot_local = jnp.arange(ENDS_MAX, dtype=jnp.int32)
@@ -205,9 +256,17 @@
         z_ext, req_ends, offset - tap_count, local_req, first_req + slot_local < past_req, tail_len
     )
     received = lax.all_to_all(states, "seq", split_axis=2, concat_axis=0, tiled=True)
-    conv_two = long_conv(z_ext, seg_long, mr_filter, slot_total)
-    mixed = (conv_two + mr_skip.astype(jnp.float32) * z_two.astype(jnp.float32)).astype(
-        jnp.bfloat16
+    tgt_pos = offset + jnp.arange(tok_rows, dtype=jnp.int32)
+    tss = seg_start(tgt_pos, req_ends)[:, None]
+    spos = (offset - tap_count + jnp.arange(tok_rows + tap_count, dtype=jnp.int32))[None, :]
+    filt_t = mr_filter[::-1].T.astype(jnp.float32)
+    filters = filt_t.shape[0]
+    taps_rows = jnp.concatenate(
+        [jnp.zeros((filters, 1), jnp.float32), filt_t, jnp.zeros((filters, tap_count - 1), jnp.float32)],
+        axis=1,
+    )
+    hyena_out = long_conv_out(
+        tss, spos, prev_z, z_two, q_two, mr_skip.astype(jnp.float32)[None, :], taps_rows
     )
     slot_index = jnp.arange(shards * ENDS_MAX, dtype=jnp.int32)
     source = slot_index // ENDS_MAX
@@ -220,7 +279,6 @@
         is_valid, pick_entries(decode_row, jnp.minimum(requests, total_req - 1)), total_req
     )
     tail_cache = place_rows(received, target, total_req)
-    hyena_out = (q_two * mixed.astype(jnp.float32)).astype(jnp.bfloat16)
     return (hyena_out, tail_cache)
 
 

time: 221 us -> 216 us (0.977)
  waiting for transfers between devices: 12.8 us -> 84.8 us
  local copies, waits for them, and re-layouts: 93.2 us -> 36.4 us
  matrix products: 28.9 us -> 10.1 us
  other arithmetic: 28 us -> 10.9 us
  Pallas kernels: 41.7 us -> 58.7 us
    all_to_all x1, waiting for transfers between devices: 0.01 us -> 72.1 us  [local(): lax.all_to_all(states, 'seq', split_axis=2, concat_axis=0, tiled=True)]
    convert_element_type x1 -> x0, local copies, waits for them, and re-layouts: 23.1 us -> none  [toeplitz(): jnp.einsum('tsj,jf->tsf', onehot, taps_table, preferred_element_type=jnp....]
    dot_general x2 -> x0, matrix products: 20.8 us -> none  [the longest x1 11.6 us: long_conv(): jnp.einsum('tsf,bsfjg->btfjg', matrix, stacked, preferred_element_type=jn...]
    pallas_call x0 -> x1, Pallas kernels: none -> 17 us  [long_conv_out(): pl.pallas_call(long_kernel, grid=(steps,), in_specs=[pl.BlockSpec(tss.sha...]
    broadcast_in_dim x1, other arithmetic: 9.8 us -> 0.6 us  [local(): mr_skip.astype(jnp.float32)[None, :]]
    concatenate x3 -> x2, local copies, waits for them, and re-layouts: 7.94 us -> 0.08 us  [local(): jnp.concatenate([jnp.zeros((filters, 1), jnp.float32), filt_t, jnp.zeros(...]
    slice x5 -> x1, local copies, waits for them, and re-layouts: 8.83 us -> 1.29 us  [local(): prev_z = passed_along(z_two[tok_rows - tap_count:], 'seq', 1)]
    convert_element_type x3 -> x1, other arithmetic: 5.82 us -> 0.01 us  [local(): filt_t = mr_filter[::-1].T.astype(jnp.float32)]
  transfers between devices with their start and end apart: 4 -> 4, of which waited for: 1 -> 2; matrix products, arithmetic and copies ran while one was open for 49% -> 7% of each run, Pallas kernels for 0% -> 8%
where the time goes in v2:
time: 216 us; the launch traced here: 214 us
  waiting for transfers between devices  84.8 us (39%)
  Pallas kernels  58.7 us (27%)
  local copies, waits for them, and re-layouts  36.4 us (17%)
  starting transfers between devices  12.7 us (6%)
  other arithmetic  10.9 us (5%)
  matrix products  10.1 us (5%)
    all_to_all x1, waiting for transfers between devices, local(): lax.all_to_all(states, 'seq', split_axis=2, concat_axis=0, tiled=True)  72.1 us
    pallas_call x1, Pallas kernels, short_chain(): pl.pallas_call(chain_kernel, grid=(steps,), in_specs=[pl.BlockSpec((rows,...  41.7 us
    all_to_all x3, local copies, waits for them, and re-layouts, local(): lax.all_to_all(states, 'seq', split_axis=2, concat_axis=0, tiled=True)  20.2 us
    pallas_call x1, Pallas kernels, long_conv_out(): pl.pallas_call(long_kernel, grid=(steps,), in_specs=[pl.BlockSpec(tss.sha...  17 us
    ppermute x3, waiting for transfers between devices, passed_along(): return lax.ppermute(x, axis, pairs)  12.7 us
    convert_element_type x1, local copies, waits for them, and re-layouts, cut_tails(): return picked.astype(jnp.bfloat16)  7.49 us
    ppermute x3, starting transfers between devices, passed_along(): return lax.ppermute(x, axis, pairs)  7.37 us
    dot_general x1, matrix products, cut_tails(): jnp.einsum('ris,sc->ric', select, z_ext, preferred_element_type=jnp.float32)  6.32 us
  transfers between devices with their start and end apart: 4, of which 2 were waited for; matrix products, arithmetic and copies ran while one was open for 7% of the time, Pallas kernels for 8%

profile of v2, /device:TPU:18, one launch (start us, length us, event | category | flops | bytes accessed | tf_op | source)
XLA Modules:
  0.0 214.4 jit_solution(287617974627722404)
XLA Ops:
  0.6 0.0 copy-start.3
  0.6 0.0 copy-start.1
  0.7 1.2 slice.9
  1.9 1.9 collective-permute-start
  3.8 0.9 slice.10
  4.8 3.5 %collective-permute-start.1 = (bf16[6,8192]{1,0:T(8,128)(2,1)S(1)}, bf16[6,8192]{1,0:T(8,128)(2,1)S(1)}, u32[]{:S(2)}, u32[]{:S(2)}) collective-permute-start(bf16[6,8192]{1,0:T(8,128)(2,1)S(1)} %slice.10), channel_id=1, source_target_pairs={{0,1},{1,2},{2,3},{3,4},{4,5},{5,6},{6,7},{7,8},{8,9},{9,10},{10,1... | collective-permute-start | bytes 294920 | tf_op jit(solution)/shard_map/ppermute | solution.py:14
  8.3 0.7 convert_reduce_fusion
  9.1 0.7 select_reduce_fusion
  9.8 1.7 convert_element_type.52.fq.fk.fv
  11.5 1.0 broadcast_in_dim.65
  12.5 1.1 convert_element_type.54.filt
  13.7 0.8 convert_element_type.55.wq.wk.wv
  14.4 0.7 fusion.15
  15.2 0.8 reshape_subtract_fusion.dist_ref
  15.9 0.7 add_maximum_fusion.2
  16.6 0.0 collective-permute-done.1
  16.6 0.8 pad.9.gq_h.gk_h
  17.5 0.0 collective-permute-done
  17.5 1.0 pad.8.hq.hk.hv
  18.5 41.7 %shard_map.104 = (bf16[256,4096]{1,0:T(8,128)(2,1)}, f32[256,4096]{1,0:T(8,128)}) custom-call(s32[288,1]{1,0:T(8,128)} %reshape_subtract_fusion.dist_ref, bf16[256,12288]{1,0:T(8,128)(2,1)} %sv.1, bf16[256,12288]{1,0:T(8,128)(2,1)} %sv.1, bf16[256,12288]{1,0:T(8,128)(2,1)} %sv.1, bf16[32,12288]{1,0:T(8,128)(2,1)} %pad.8.hq.hk.hv, ...), custom_call_target="tpu_custom_call" | custom-call | tf_op jit(solution)/shard_map/pallas_call | solution.py:80
  60.2 1.3 slice.11
  61.5 1.9 collective-permute-start.2
  63.4 1.3 fusion.16
  64.8 0.2 select_reduce_fusion.3
  65.0 0.7 compare_select_fusion
  65.7 0.1 fusion.11
  65.8 0.1 fusion.10
  65.9 12.7 %collective-permute-done.2.prev_ref = bf16[128,4096]{1,0:T(8,128)(2,1)S(1)} collective-permute-done((bf16[128,4096]{1,0:T(8,128)(2,1)S(1)}, bf16[128,4096]{1,0:T(8,128)(2,1)S(1)}, u32[]{:S(2)}, u32[]{:S(2)}) %collective-permute-start.2) | collective-permute-done | bytes 1048608 | tf_op jit(solution)/shard_map/ppermute | solution.py:14
  78.5 6.3 %convolution_convert_fusion = bf16[4,127,4096]{2,1,0:T(8,128)(2,1)} fusion(bf16[256,4096]{1,0:T(8,128)(2,1)} %get-tuple-element.4.z_ref, bf16[128,4096]{1,0:T(8,128)(2,1)S(1)} %collective-permute-done.2.prev_ref, s32[4,127]{1,0:T(4,128)S(1)} %fusion.10, pred[4,127]{1,0:T(4,128)(4,1)S(1)} %fusion.11), kind=kOutput, calls=%fused_computation | convolution fusion | flops 1606792192 | bytes 7309804 | tf_op jit(solution)/shard_map/ris,sc->ric/dot_general | solution.py:205
  84.9 7.5 %copy.34 = bf16[4,127,4096]{1,0,2:T(4,128)(2,1)} copy(bf16[4,127,4096]{2,1,0:T(8,128)(2,1)} %convolution_convert_fusion) | data formatting | bytes 8323072 | tf_op jit(solution)/shard_map/convert_element_type | solution.py:206
  92.3 5.4 %all-to-all-start = ((bf16[4,127,4096]{1,0,2:T(4,128)(2,1)}), bf16[4,127,4096]{1,0,2:T(4,128)(2,1)}, u32[]{:S(2)}, u32[]{:S(2)}) async-start(bf16[4,127,4096]{1,0,2:T(4,128)(2,1)} %copy.34), calls=%async_computation | async-start | bytes 8388608 | tf_op jit(solution)/shard_map/all_to_all | solution.py:258
  97.7 0.1 convert_reduce_fusion.1
  97.8 0.1 select_reduce_fusion.1
  97.9 0.8 copy.33.tss_ref
  98.7 0.6 broadcast_in_dim.80
  99.3 0.1 copy.32
  99.4 0.2 rev.3
  99.7 0.1 pad.14.clone
  99.8 0.5 iota_add_fusion.2.spos_ref
  100.3 0.1 convert_reduce_fusion.2
  100.4 0.1 select_reduce_fusion.2
  100.5 0.8 maximum_maximum_fusion.u_ref
  101.4 17.0 %shard_map.105 = bf16[256,4096]{1,0:T(8,128)(2,1)} custom-call(s32[256,1]{1,0:T(8,128)} %copy.33.tss_ref, s32[1,384]{1,0:T(1,128)} %iota_add_fusion.2.spos_ref, bf16[128,4096]{1,0:T(8,128)(2,1)} %copy-done, bf16[256,4096]{1,0:T(8,128)(2,1)} %get-tuple-element.4.z_ref, f32[256,4096]{1,0:T(8,128)} %get-tuple-element.5.q2_ref, f32[1,4096]{1,0:T(1,128)} %bitcast.18, ...), custom_call_target="tpu_custom_call" | custom-call | tf_op jit(solution)/shard_map/pallas_call | solution.py:130
  118.3 72.1 %all-to-all-done = bf16[4,127,4096]{1,0,2:T(4,128)(2,1)} async-done(((bf16[4,127,4096]{1,0,2:T(4,128)(2,1)}), bf16[4,127,4096]{1,0,2:T(4,128)(2,1)}, u32[]{:S(2)}, u32[]{:S(2)}) %all-to-all-start) | async-done | bytes 4161568 | tf_op jit(solution)/shard_map/all_to_all | solution.py:258
  190.4 4.7 %copy.35 = bf16[4,127,4096]{1,2,0:T(8,128)(2,1)} copy(bf16[4,127,4096]{1,0,2:T(4,128)(2,1)} %all-to-all-done) | data formatting | bytes 8323072 | tf_op jit(solution)/shard_map/all_to_all | solution.py:258
  195.1 8.1 %copy.36 = bf16[16,4,127,256]{3,1,0,2:T(4,128)(2,1)} copy(bf16[16,4,127,256]{2,3,0,1:T(8,128)(2,1)} %bitcast.17) | data formatting | bytes 8323072 | tf_op jit(solution)/shard_map/all_to_all | solution.py:258
  203.1 7.5 %all_to_all.16 = bf16[64,127,256]{2,0,1:T(8,128)(2,1)} reshape(bf16[16,4,127,256]{3,1,0,2:T(4,128)(2,1)} %copy.36) | data formatting | bytes 8323072 | tf_op jit(solution)/shard_map/all_to_all | solution.py:258
  210.6 3.8 %convolution_convert_fusion.1 = bf16[16,127,256]{2,0,1:T(8,128)(2,1)} fusion(bf16[64,127,256]{2,0,1:T(8,128)(2,1)} %all_to_all.16, s32[64]{0:T(128)S(1)} %compare_select_fusion.1), kind=kOutput, calls=%fused_computation.4 | convolution fusion | flops 67105792 | bytes 5202176 | tf_op jit(solution)/shard_map/ts,sic->tic/dot_general | solution.py:213
  (23 shorter events, 0.1 us)
Async XLA Ops:
  0.6 13.8 %copy-start.3 = (s32[16]{0:T(128)S(1)}, s32[16]{0:T(128)}, u32[]{:S(2)}) copy-start(s32[16]{0:T(128)} %param.16) | copy-start | bytes 196
  0.6 13.0 %copy-start.1 = (bf16[7,12288]{1,0:T(8,128)(2,1)S(1)}, bf16[7,12288]{1,0:T(8,128)(2,1)}, u32[]{:S(2)}) copy-start(bf16[7,12288]{1,0:T(8,128)(2,1)} %param.13) | copy-start | bytes 516100
  1.9 15.6 %collective-permute-start = (bf16[18,12288]{1,0:T(8,128)(2,1)S(1)}, bf16[18,12288]{1,0:T(8,128)(2,1)S(1)}, u32[]{:S(2)}, u32[]{:S(2)}) collective-permute-start(bf16[18,12288]{1,0:T(8,128)(2,1)S(1)} %slice.9), channel_id=1, source_target_pairs={{0,1},{1,2},{2,3},{3,4},{4,5},{5,6},{6,7},{7,8},{8,9},{9,10},{10,1... | collective-permute-start | bytes 1327112 | tf_op jit(solution)/shard_map/ppermute | solution.py:14
  4.8 11.9 %collective-permute-start.1 = (bf16[6,8192]{1,0:T(8,128)(2,1)S(1)}, bf16[6,8192]{1,0:T(8,128)(2,1)S(1)}, u32[]{:S(2)}, u32[]{:S(2)}) collective-permute-start(bf16[6,8192]{1,0:T(8,128)(2,1)S(1)} %slice.10), channel_id=1, source_target_pairs={{0,1},{1,2},{2,3},{3,4},{4,5},{5,6},{6,7},{7,8},{8,9},{9,10},{10,1... | collective-permute-start | bytes 294920 | tf_op jit(solution)/shard_map/ppermute | solution.py:14
  61.5 17.0 %collective-permute-start.2 = (bf16[128,4096]{1,0:T(8,128)(2,1)S(1)}, bf16[128,4096]{1,0:T(8,128)(2,1)S(1)}, u32[]{:S(2)}, u32[]{:S(2)}) collective-permute-start(bf16[128,4096]{1,0:T(8,128)(2,1)S(1)} %slice.11), channel_id=1, source_target_pairs={{0,1},{1,2},{2,3},{3,4},{4,5},{5,6},{6,7},{7,8},{8,9},{9,10},{10,1... | collective-permute-start | bytes 3145736 | tf_op jit(solution)/shard_map/ppermute | solution.py:14
  78.5 6.3 %copy-start = (bf16[128,4096]{1,0:T(8,128)(2,1)}, bf16[128,4096]{1,0:T(8,128)(2,1)S(1)}, u32[]{:S(2)}) copy-start(bf16[128,4096]{1,0:T(8,128)(2,1)S(1)} %collective-permute-done.2.prev_ref) | copy-start | bytes 3145732
  92.3 6.4 %copy-start.4 = (bf16[4096]{0:T(1024)(128)(2,1)S(1)}, bf16[4096]{0:T(1024)(128)(2,1)}, u32[]{:S(2)}) copy-start(bf16[4096]{0:T(1024)(128)(2,1)} %param.15) | copy-start | bytes 24580
  92.3 7.0 %copy-start.2 = (bf16[128,256]{1,0:T(8,128)(2,1)S(1)}, bf16[128,256]{1,0:T(8,128)(2,1)}, u32[]{:S(2)}) copy-start(bf16[128,256]{1,0:T(8,128)(2,1)} %param.14) | copy-start | bytes 196612
  92.3 8.0 %copy-start.5 = (s32[16]{0:T(128)S(1)}, s32[16]{0:T(128)}, u32[]{:S(2)}) copy-start(s32[16]{0:T(128)} %param.17) | copy-start | bytes 196
  92.3 98.1 %all-to-all-start = ((bf16[4,127,4096]{1,0,2:T(4,128)(2,1)}), bf16[4,127,4096]{1,0,2:T(4,128)(2,1)}, u32[]{:S(2)}, u32[]{:S(2)}) async-start(bf16[4,127,4096]{1,0,2:T(4,128)(2,1)} %copy.34), calls=%async_computation | async-start | bytes 8388608 | tf_op jit(solution)/shard_map/all_to_all | solution.py:258

commit v3 on v2

--- a/solution.py
+++ b/solution.py
@@ -60,16 +60,20 @@
     ys[24:rows, :] = (q1 * c1).astype(jnp.bfloat16).astype(jnp.float32)
     v2 = sconv(ys, wv, HALO)
     k2 = sconv(xb, wk, HALO)
-    z2_ref[...] = (k2 * v2).astype(jnp.bfloat16)
+    z2 = (k2 * v2).astype(jnp.bfloat16)
+    chunk = z2_ref.shape[2]
+    for i in range(z2_ref.shape[0]):
+        z2_ref[i] = z2[:, i * chunk : (i + 1) * chunk]
     q2_ref[...] = sconv(xa, wq, HALO)
 
 
-def short_chain(dist, se_streams, se_halo, mr_gates, mr_halo, se_feat, se_filt, mr_feat):
+def short_chain(dist, se_streams, se_halo, mr_gates, mr_halo, se_feat, se_filt, mr_feat, shards):
     tok_rows = se_streams.shape[0]
     channels = mr_gates.shape[1] // 2
     steps = channels // TILE
     rows = tok_rows + HALO
     taps = se_feat.shape[0]
+    chunk = channels // shards
 
     def col(part):
         return lambda j: (0, j + part * steps)
@@ -82,25 +86,27 @@
         grid=(steps,),
         in_specs=[pl.BlockSpec((rows, 1), lambda j: (0, 0))] + main + halo + main[:2] + halo[:2] + wts
         + [wts[0]] + wts,
-        out_specs=[pl.BlockSpec((tok_rows, TILE), col(0)), pl.BlockSpec((tok_rows, TILE), col(0))],
-        out_shape=[jax.ShapeDtypeStruct((tok_rows, channels), jnp.bfloat16),
+        out_specs=[
+            pl.BlockSpec((TILE // chunk, tok_rows, chunk), lambda j: (j, 0, 0)),
+            pl.BlockSpec((tok_rows, TILE), col(0)),
+        ],
+        out_shape=[jax.ShapeDtypeStruct((shards, tok_rows, chunk), jnp.bfloat16),
                    jax.ShapeDtypeStruct((tok_rows, channels), jnp.float32)],
         scratch_shapes=[pltpu.VMEM((rows, TILE), jnp.float32) for _ in range(7)],
     )(dist, se_streams, se_streams, se_streams, se_halo, se_halo, se_halo, mr_gates, mr_gates,
       mr_halo, mr_halo, se_feat, se_feat, se_feat, se_filt, mr_feat, mr_feat, mr_feat)
 
 
-LANES = 256
 GROUP_LANES = 128
 
 
 def long_kernel(tss_ref, spos_ref, prev_ref, z_ref, q2_ref, skip_ref, u_ref, out_ref):
-    blk = prev_ref.shape[0]
-    tile = z_ref.shape[1]
+    blk = prev_ref.shape[1]
+    tile = z_ref.shape[2]
     width = u_ref.shape[1]
     per_group = tile // u_ref.shape[0]
-    z = z_ref[...]
-    windows = (jnp.concatenate([prev_ref[...], z[:blk]], axis=0), z)
+    z = z_ref[0]
+    windows = (jnp.concatenate([prev_ref[0], z[:blk]], axis=0), z)
     masks = [
         spos_ref[:, b * blk : b * blk + width] >= tss_ref[b * blk : (b + 1) * blk, :] for b in range(2)
     ]
@@ -123,9 +129,9 @@
 
 
 def long_conv_out(tss, spos, prev_z, z_two, q_two, skip, taps_rows):
-    tok_rows, channels = z_two.shape
-    blk = prev_z.shape[0]
-    steps = channels // LANES
+    steps, tok_rows, lanes = z_two.shape
+    channels = steps * lanes
+    blk = prev_z.shape[1]
     per_group = channels // taps_rows.shape[0]
     return pl.pallas_call(
         long_kernel,
@@ -133,13 +139,13 @@
         in_specs=[
             pl.BlockSpec(tss.shape, lambda j: (0, 0)),
             pl.BlockSpec(spos.shape, lambda j: (0, 0)),
-            pl.BlockSpec((blk, LANES), lambda j: (0, j)),
-            pl.BlockSpec((tok_rows, LANES), lambda j: (0, j)),
-            pl.BlockSpec((tok_rows, LANES), lambda j: (0, j)),
-            pl.BlockSpec((1, LANES), lambda j: (0, j)),
-            pl.BlockSpec((LANES // per_group, taps_rows.shape[1]), lambda j: (j, 0)),
+            pl.BlockSpec((1, blk, lanes), lambda j: (j, 0, 0)),
+            pl.BlockSpec((1, tok_rows, lanes), lambda j: (j, 0, 0)),
+            pl.BlockSpec((tok_rows, lanes), lambda j: (0, j)),
+            pl.BlockSpec((1, lanes), lambda j: (0, j)),
+            pl.BlockSpec((lanes // per_group, taps_rows.shape[1]), lambda j: (j, 0)),
         ],
-        out_specs=pl.BlockSpec((tok_rows, LANES), lambda j: (0, j)),
+        out_specs=pl.BlockSpec((tok_rows, lanes), lambda j: (0, j)),
         out_shape=jax.ShapeDtypeStruct((tok_rows, channels), jnp.bfloat16),
     )(tss, spos, prev_z, z_two, q_two, skip, taps_rows)
 
@@ -245,17 +251,10 @@
         se_feat.astype(jnp.float32),
         jnp.repeat(se_filter, group_ch, axis=1).astype(jnp.float32),
         mr_feat.astype(jnp.float32),
-    )
-    prev_z = passed_along(z_two[tok_rows - tap_count :], "seq", 1)
-    z_ext = jnp.concatenate([prev_z, z_two], axis=0)
-    first_req = request_of(jnp.reshape(offset, (1,)), req_ends)[0]
-    past_req = request_of(jnp.reshape(offset + tok_rows, (1,)), req_ends)[0]
-    slot_local = jnp.arange(ENDS_MAX, dtype=jnp.int32)
-    local_req = jnp.minimum(first_req + slot_local, total_req - 1)
-    states = cut_tails(
-        z_ext, req_ends, offset - tap_count, local_req, first_req + slot_local < past_req, tail_len
-    )
-    received = lax.all_to_all(states, "seq", split_axis=2, concat_axis=0, tiled=True)
+        shards,
+    )
+    prev_z = passed_along(z_two[:, tok_rows - tap_count :], "seq", 1)
+    received = lax.all_to_all(z_two, "seq", split_axis=0, concat_axis=0, tiled=True)
     tgt_pos = offset + jnp.arange(tok_rows, dtype=jnp.int32)
     tss = seg_start(tgt_pos, req_ends)[:, None]
     spos = (offset - tap_count + jnp.arange(tok_rows + tap_count, dtype=jnp.int32))[None, :]
@@ -268,17 +267,20 @@
     hyena_out = long_conv_out(
         tss, spos, prev_z, z_two, q_two, mr_skip.astype(jnp.float32)[None, :], taps_rows
     )
-    slot_index = jnp.arange(shards * ENDS_MAX, dtype=jnp.int32)
-    source = slot_index // ENDS_MAX
-    within = slot_index % ENDS_MAX
-    source_first = request_of(source * tok_rows, req_ends)
-    source_past = request_of((source + 1) * tok_rows, req_ends)
-    requests = source_first + within
-    is_valid = requests < source_past
-    target = jnp.where(
-        is_valid, pick_entries(decode_row, jnp.minimum(requests, total_req - 1)), total_req
-    )
-    tail_cache = place_rows(received, target, total_req)
+    z_all = received.reshape(shards * tok_rows, received.shape[2])
+    z_all = jnp.concatenate([jnp.zeros((tap_count, z_all.shape[1]), z_all.dtype), z_all], axis=0)
+    rows_ids = jnp.arange(total_req, dtype=jnp.int32)
+    owner = jnp.sum(
+        jnp.where(decode_row[None, :] == rows_ids[:, None], rows_ids[None, :], 0), axis=1
+    )
+    last_pos = pick_entries(req_ends, owner)
+    first_pos = jnp.where(owner > 0, pick_entries(req_ends, jnp.maximum(owner - 1, 0)) + 1, 0)
+    pieces = jax.vmap(
+        lambda begin: lax.dynamic_slice_in_dim(z_all, begin, tail_len, 0)
+    )(last_pos - tail_len + 1 + tap_count)
+    positions = last_pos[:, None] - tail_len + 1 + jnp.arange(tail_len, dtype=jnp.int32)[None, :]
+    inside = positions >= first_pos[:, None]
+    tail_cache = jnp.where(inside[:, :, None], pieces, jnp.zeros((), pieces.dtype))
     return (hyena_out, tail_cache)
 
 

time: 216 us -> 166 us (0.77)
  waiting for transfers between devices: 84.8 us -> 52.7 us
  matrix products: 10.1 us -> 0 us
  local copies, waits for them, and re-layouts: 36.4 us -> 31.4 us
  other arithmetic: 10.9 us -> 8.2 us
    all_to_all x1, waiting for transfers between devices: 72.1 us -> 0.01 us  [local(): lax.all_to_all(z_two, 'seq', split_axis=0, concat_axis=0, tiled=True)]
    ppermute x3, waiting for transfers between devices: 12.7 us -> 52.7 us  [passed_along(): return lax.ppermute(x, axis, pairs)]
    all_to_all x3 -> x0, local copies, waits for them, and re-layouts: 20.2 us -> none  [local(): lax.all_to_all(states, 'seq', split_axis=2, concat_axis=0, tiled=True)]
    gather x0 -> x48, local copies, waits for them, and re-layouts: none -> 20.1 us
    dot_general x2 -> x0, matrix products: 10.1 us -> none  [the longest x1 6.32 us: cut_tails(): jnp.einsum('ris,sc->ric', select, z_ext, preferred_element_type=jnp.float32)]
    convert_element_type x1 -> x0, local copies, waits for them, and re-layouts: 7.49 us -> none  [cut_tails(): return picked.astype(jnp.bfloat16)]
  transfers between devices with their start and end apart: 4 -> 4, of which waited for: 2 -> 2; matrix products, arithmetic and copies ran while one was open for 7% -> 8% of each run, Pallas kernels for 8% -> 10%
where the time goes in v3:
time: 166 us; the launch traced here: 165 us
  Pallas kernels  58.6 us (35%)
  waiting for transfers between devices  52.7 us (32%)
  local copies, waits for them, and re-layouts  31.4 us (19%)
  starting transfers between devices  12.9 us (8%)
  other arithmetic  8.2 us (5%)
    ppermute x3, waiting for transfers between devices, passed_along(): return lax.ppermute(x, axis, pairs)  52.7 us
    pallas_call x1, Pallas kernels, short_chain(): pl.pallas_call(chain_kernel, grid=(steps,), in_specs=[pl.BlockSpec((rows,...  41.7 us
    gather x48, local copies, waits for them, and re-layouts  20.1 us
    pallas_call x1, Pallas kernels, long_conv_out(): pl.pallas_call(long_kernel, grid=(steps,), in_specs=[pl.BlockSpec(tss.sha...  16.9 us
    ppermute x3, starting transfers between devices, passed_along(): return lax.ppermute(x, axis, pairs)  7.5 us
    all_to_all x1, starting transfers between devices, local(): lax.all_to_all(z_two, 'seq', split_axis=0, concat_axis=0, tiled=True)  5.43 us
  transfers between devices with their start and end apart: 4, of which 2 were waited for; matrix products, arithmetic and copies ran while one was open for 8% of the time, Pallas kernels for 10%

profile of v3, /device:TPU:18, one launch (start us, length us, event | category | flops | bytes accessed | tf_op | source)
XLA Modules:
  0.0 165.1 jit_solution(16717268172665184764)
XLA Ops:
  0.7 1.2 slice.9
  1.9 1.9 %collective-permute-start = (bf16[18,12288]{1,0:T(8,128)(2,1)S(1)}, bf16[18,12288]{1,0:T(8,128)(2,1)S(1)}, u32[]{:S(2)}, u32[]{:S(2)}) collective-permute-start(bf16[18,12288]{1,0:T(8,128)(2,1)S(1)} %slice.9), channel_id=1, source_target_pairs={{0,1},{1,2},{2,3},{3,4},{4,5},{5,6},{6,7},{7,8},{8,9},{9,10},{10,1... | collective-permute-start | bytes 1327112 | tf_op jit(solution)/shard_map/ppermute | solution.py:14
  3.8 0.9 slice.10
  4.8 3.5 %collective-permute-start.1 = (bf16[6,8192]{1,0:T(8,128)(2,1)S(1)}, bf16[6,8192]{1,0:T(8,128)(2,1)S(1)}, u32[]{:S(2)}, u32[]{:S(2)}) collective-permute-start(bf16[6,8192]{1,0:T(8,128)(2,1)S(1)} %slice.10), channel_id=1, source_target_pairs={{0,1},{1,2},{2,3},{3,4},{4,5},{5,6},{6,7},{7,8},{8,9},{9,10},{10,1... | collective-permute-start | bytes 294920 | tf_op jit(solution)/shard_map/ppermute | solution.py:14
  8.3 0.7 convert_reduce_fusion
  9.1 1.7 %convert_element_type.30.fq.fk.fv = f32[7,12288]{1,0:T(8,128)} convert(bf16[7,12288]{1,0:T(8,128)(2,1)} %param.11) | non-fusion elementwise | flops 86016 | bytes 516096 | tf_op jit(solution)/shard_map/convert_element_type | solution.py:251
  10.8 1.0 broadcast_in_dim.108
  11.8 1.1 convert_element_type.32.filt
  12.9 0.8 convert_element_type.33.wq.wk.wv
  13.8 0.8 reshape_subtract_fusion.dist_ref
  14.6 0.8 collective-permute-done.1
  15.4 0.8 pad.11.gq_h.gk_h
  16.3 1.0 pad.10.hq.hk.hv
  17.3 41.7 %shard_map.104 = (bf16[16,256,256]{2,1,0:T(8,128)(2,1)}, f32[256,4096]{1,0:T(8,128)}) custom-call(s32[288,1]{1,0:T(8,128)} %reshape_subtract_fusion.dist_ref, bf16[256,12288]{1,0:T(8,128)(2,1)} %sv.1, bf16[256,12288]{1,0:T(8,128)(2,1)} %sv.1, bf16[256,12288]{1,0:T(8,128)(2,1)} %sv.1, bf16[32,12288]{1,0:T(8,128)(2,1)} %pad.10.hq.hk.hv, ...), custom_call_target="tpu_custom_call" | custom-call | tf_op jit(solution)/shard_map/pallas_call | solution.py:84
  59.0 5.4 %all-to-all-start = ((bf16[16,256,256]{2,1,0:T(8,128)(2,1)}), bf16[16,256,256]{2,1,0:T(8,128)(2,1)}, u32[]{:S(2)}, u32[]{:S(2)}) async-start(bf16[16,256,256]{2,1,0:T(8,128)(2,1)} %get-tuple-element.4.z_ref), calls=%async_computation | async-start | bytes 4194304 | tf_op jit(solution)/shard_map/all_to_all | solution.py:257
  65.0 1.0 slice.11
  66.0 2.0 %collective-permute-start.2 = (bf16[16,128,256]{2,1,0:T(8,128)(2,1)}, bf16[16,128,256]{2,1,0:T(8,128)(2,1)S(1)}, u32[]{:S(2)}, u32[]{:S(2)}) collective-permute-start(bf16[16,128,256]{2,1,0:T(8,128)(2,1)} %slice.11), channel_id=1, source_target_pairs={{0,1},{1,2},{2,3},{3,4},{4,5},{5,6},{6,7},{7,8},{8,9},{9,10},{10,1... | collective-permute-start | bytes 3145736 | tf_op jit(solution)/shard_map/ppermute | solution.py:14
  68.1 0.8 copy.27.tss_ref
  68.9 0.6 broadcast_in_dim.120
  69.9 0.6 iota_add_fusion.1.spos_ref
  70.6 0.8 maximum_maximum_fusion.u_ref
  71.4 51.9 %collective-permute-done.2.prev_ref = bf16[16,128,256]{2,1,0:T(8,128)(2,1)S(1)} collective-permute-done((bf16[16,128,256]{2,1,0:T(8,128)(2,1)}, bf16[16,128,256]{2,1,0:T(8,128)(2,1)S(1)}, u32[]{:S(2)}, u32[]{:S(2)}) %collective-permute-start.2) | collective-permute-done | bytes 1048608 | tf_op jit(solution)/shard_map/ppermute | solution.py:14
  123.4 1.1 copy-done.1
  124.4 16.9 %shard_map.105 = bf16[256,4096]{1,0:T(8,128)(2,1)} custom-call(s32[256,1]{1,0:T(8,128)} %copy.27.tss_ref, s32[1,384]{1,0:T(1,128)} %iota_add_fusion.1.spos_ref, bf16[16,128,256]{2,1,0:T(8,128)(2,1)} %copy-done.1, bf16[16,256,256]{2,1,0:T(8,128)(2,1)} %get-tuple-element.4.z_ref, f32[256,4096]{1,0:T(8,128)} %get-tuple-element.5.q2_ref, f32[1,4096]{1,0:T(1,128)} %bitcast.17, ...), custom_call_target="tpu_custom_call" | custom-call | tf_op jit(solution)/shard_map/pallas_call | solution.py:136
  141.4 1.7 %concatenate.10 = bf16[4224,256]{1,0:T(8,128)(2,1)S(1)} pad(bf16[4096,256]{1,0:T(8,128)(2,1)} %bitcast.3, bf16[]{:T(256)} %constant.20.clone.1), padding=128_0x0_0 | pad | bytes 4259842 | tf_op jit(solution)/shard_map/concatenate | solution.py:271
  143.1 20.5 %while.1 = (s32[]{:T(128)}, bf16[4224,256]{1,0:T(8,128)(2,1)S(1)}, s32[16,2]{0,1:T(2,128)S(1)}, bf16[16,127,256]{2,1,0:T(8,128)(2,1)S(1)}, s32[]{:T(128)}) while((s32[]{:T(128)}, bf16[4224,256]{1,0:T(8,128)(2,1)S(1)}, s32[16,2]{0,1:T(2,128)S(1)}, bf16[16,127,256]{2,1,0:T(8,128)(2,1)S(1)}, s32[]{:T(128)}) %tuple.26), condition=%wide.while_cond, body=%wide.while_body.sunk | while | flops 2 | bytes 131177 | solution.py:279
  143.2 0.5 slice.24
  143.7 0.7 bitcast_dynamic-update-slice_fusion.2
  144.5 0.5 slice.24
  145.0 0.7 bitcast_dynamic-update-slice_fusion.2
  145.7 0.5 slice.24
  146.3 0.7 bitcast_dynamic-update-slice_fusion.2
  147.0 0.5 slice.24
  147.5 0.7 bitcast_dynamic-update-slice_fusion.2
  148.3 0.5 slice.24
  148.8 0.7 bitcast_dynamic-update-slice_fusion.2
  150.1 0.7 bitcast_dynamic-update-slice_fusion.2
  151.4 0.7 bitcast_dynamic-update-slice_fusion.2
  152.7 0.7 bitcast_dynamic-update-slice_fusion.2
  153.9 0.7 bitcast_dynamic-update-slice_fusion.2
  155.2 0.7 bitcast_dynamic-update-slice_fusion.2
  156.5 0.7 bitcast_dynamic-update-slice_fusion.2
  157.8 0.7 bitcast_dynamic-update-slice_fusion.2
  159.1 0.7 bitcast_dynamic-update-slice_fusion.2
  160.3 0.7 bitcast_dynamic-update-slice_fusion.2
  161.6 0.7 bitcast_dynamic-update-slice_fusion.2
  162.9 0.7 bitcast_dynamic-update-slice_fusion.2
  163.6 1.5 copy_select_fusion
  (65 shorter events, 7.9 us)
Async XLA Ops:
  0.6 13.1 %copy-start.4 = (s32[16]{0:T(128)S(1)}, s32[16]{0:T(128)}, u32[]{:S(2)}) copy-start(s32[16]{0:T(128)} %param.16) | copy-start | bytes 196
  0.6 12.3 %copy-start.2 = (bf16[7,12288]{1,0:T(8,128)(2,1)S(1)}, bf16[7,12288]{1,0:T(8,128)(2,1)}, u32[]{:S(2)}) copy-start(bf16[7,12288]{1,0:T(8,128)(2,1)} %param.13) | copy-start | bytes 516100
  1.9 14.4 %collective-permute-start = (bf16[18,12288]{1,0:T(8,128)(2,1)S(1)}, bf16[18,12288]{1,0:T(8,128)(2,1)S(1)}, u32[]{:S(2)}, u32[]{:S(2)}) collective-permute-start(bf16[18,12288]{1,0:T(8,128)(2,1)S(1)} %slice.9), channel_id=1, source_target_pairs={{0,1},{1,2},{2,3},{3,4},{4,5},{5,6},{6,7},{7,8},{8,9},{9,10},{10,1... | collective-permute-start | bytes 1327112 | tf_op jit(solution)/shard_map/ppermute | solution.py:14
  4.8 10.6 %collective-permute-start.1 = (bf16[6,8192]{1,0:T(8,128)(2,1)S(1)}, bf16[6,8192]{1,0:T(8,128)(2,1)S(1)}, u32[]{:S(2)}, u32[]{:S(2)}) collective-permute-start(bf16[6,8192]{1,0:T(8,128)(2,1)S(1)} %slice.10), channel_id=1, source_target_pairs={{0,1},{1,2},{2,3},{3,4},{4,5},{5,6},{6,7},{7,8},{8,9},{9,10},{10,1... | collective-permute-start | bytes 294920 | tf_op jit(solution)/shard_map/ppermute | solution.py:14
  59.0 5.5 %copy-start.6 = (s32[16]{0:T(128)S(1)}, s32[16]{0:T(128)}, u32[]{:S(2)}) copy-start(s32[16]{0:T(128)} %param.17) | copy-start | bytes 196
  59.0 6.0 %copy-start = (bf16[16,256,256]{2,1,0:T(8,128)(2,1)S(1)}, bf16[16,256,256]{2,1,0:T(8,128)(2,1)}, u32[]{:S(2)}) copy-start(bf16[16,256,256]{2,1,0:T(8,128)(2,1)} %get-tuple-element.4.z_ref) | copy-start | bytes 6291460
  59.0 82.3 %all-to-all-start = ((bf16[16,256,256]{2,1,0:T(8,128)(2,1)}), bf16[16,256,256]{2,1,0:T(8,128)(2,1)}, u32[]{:S(2)}, u32[]{:S(2)}) async-start(bf16[16,256,256]{2,1,0:T(8,128)(2,1)} %get-tuple-element.4.z_ref), calls=%async_computation | async-start | bytes 4194304 | tf_op jit(solution)/shard_map/all_to_all | solution.py:257
  64.4 4.5 %copy-start.5 = (bf16[4096]{0:T(1024)(128)(2,1)S(1)}, bf16[4096]{0:T(1024)(128)(2,1)}, u32[]{:S(2)}) copy-start(bf16[4096]{0:T(1024)(128)(2,1)} %param.15) | copy-start | bytes 24580
  64.4 5.1 %copy-start.3 = (bf16[128,256]{1,0:T(8,128)(2,1)S(1)}, bf16[128,256]{1,0:T(8,128)(2,1)}, u32[]{:S(2)}) copy-start(bf16[128,256]{1,0:T(8,128)(2,1)} %param.14) | copy-start | bytes 196612
  66.0 57.3 %collective-permute-start.2 = (bf16[16,128,256]{2,1,0:T(8,128)(2,1)}, bf16[16,128,256]{2,1,0:T(8,128)(2,1)S(1)}, u32[]{:S(2)}, u32[]{:S(2)}) collective-permute-start(bf16[16,128,256]{2,1,0:T(8,128)(2,1)} %slice.11), channel_id=1, source_target_pairs={{0,1},{1,2},{2,3},{3,4},{4,5},{5,6},{6,7},{7,8},{8,9},{9,10},{10,1... | collective-permute-start | bytes 3145736 | tf_op jit(solution)/shard_map/ppermute | solution.py:14
  123.4 1.1 copy-start.1

commit v4 on v3

v4 whole, which is shorter than its diff:
```python
import jax
import jax.numpy as jnp
from jax import lax
from jax.sharding import PartitionSpec as P
from jax.experimental import pallas as pl
from jax.experimental.pallas import tpu as pltpu

ENDS_MAX = 4


def passed_along(x, axis, by):
    length = lax.axis_size(axis)
    pairs = [(i, i + by) for i in range(length) if 0 <= i + by < length]
    return lax.ppermute(x, axis, pairs)


def request_of(positions, req_ends):
    return jnp.sum((req_ends[None, :] < positions[:, None]).astype(jnp.int32), axis=1)


def short_conv(values, weights, segment):
    length = weights.shape[0]
    out_count = values.shape[0] - length + 1
    latest = length - 1
    current = segment[latest:]
    summed = values[latest:].astype(jnp.float32) * weights[0].astype(jnp.float32)
    for lag_step in range(1, length):
        earlier = values[latest - lag_step : latest - lag_step + out_count].astype(jnp.float32)
        same_req = segment[latest - lag_step : latest - lag_step + out_count] == current
        summed = summed + jnp.where(
            same_req[:, None], earlier * weights[lag_step].astype(jnp.float32), 0.0
        )
    return summed


HALO = 32
TILE = 512
GROUP_LANES = 128
WINDOW = 144


def short_conv_rows(x, w, first, dist_ref):
    rows = x.shape[0]
    dist = dist_ref[first:rows, :]
    acc = x[first:rows, :] * w[0:1, :].astype(jnp.float32)
    for lag in range(1, w.shape[0]):
        term = x[first - lag : rows - lag, :] * w[lag : lag + 1, :].astype(jnp.float32)
        acc = acc + jnp.where(dist >= lag, term, 0.0)
    return acc


def chain_kernel(dist_ref, sq, sk, sv, hq, hk, hv, mk, gk_h, fq, fk, fv, filt, wk, wv,
                 z2_ref, xq, xk, xv, xb, zs, ys):
    rows = xq.shape[0]
    for main, halo, x in ((sq, hq, xq), (sk, hk, xk), (sv, hv, xv), (mk, gk_h, xb)):
        reach = halo.shape[0]
        x[0 : HALO - reach, :] = jnp.zeros((HALO - reach, x.shape[1]), jnp.float32)
        x[HALO - reach : HALO, :] = halo[...].astype(jnp.float32)
        x[HALO:rows, :] = main[...].astype(jnp.float32)

    k1 = short_conv_rows(xk, fk, 16, dist_ref)
    v1 = short_conv_rows(xv, fv, 16, dist_ref)
    zs[16:rows, :] = (k1 * v1).astype(jnp.bfloat16).astype(jnp.float32)
    q1 = short_conv_rows(xq, fq, 24, dist_ref)
    c1 = short_conv_rows(zs, filt, 24, dist_ref)
    ys[24:rows, :] = (q1 * c1).astype(jnp.bfloat16).astype(jnp.float32)
    v2 = short_conv_rows(ys, wv, HALO, dist_ref)
    k2 = short_conv_rows(xb, wk, HALO, dist_ref)
    z2 = (k2 * v2).astype(jnp.bfloat16)
    chunk = z2_ref.shape[2]
    for i in range(z2_ref.shape[0]):
        z2_ref[i] = z2[:, i * chunk : (i + 1) * chunk]


def short_chain(dist, se_streams, se_halo, mr_gates, mr_halo, se_feat, se_filt, mr_feat, shards):
    tok_rows = se_streams.shape[0]
    channels = mr_gates.shape[1] // 2
    steps = channels // TILE
    rows = tok_rows + HALO
    taps = se_feat.shape[0]
    chunk = channels // shards

    def col(part):
        return lambda j: (0, j + part * steps)

    main = [pl.BlockSpec((tok_rows, TILE), col(p)) for p in range(3)]
    halo = [pl.BlockSpec((se_halo.shape[0], TILE), col(p)) for p in range(3)]
    mhalo = pl.BlockSpec((mr_halo.shape[0], TILE), col(1))
    wts = [pl.BlockSpec((taps, TILE), col(p)) for p in range(3)]
    return pl.pallas_call(
        chain_kernel,
        grid=(steps,),
        in_specs=[pl.BlockSpec((rows, 1), lambda j: (0, 0))] + main + halo + [main[1], mhalo] + wts
        + [wts[0], wts[1], wts[2]],
        out_specs=pl.BlockSpec((TILE // chunk, tok_rows, chunk), lambda j: (j, 0, 0)),
        out_shape=jax.ShapeDtypeStruct((shards, tok_rows, chunk), jnp.bfloat16),
        scratch_shapes=[pltpu.VMEM((rows, TILE), jnp.float32) for _ in range(6)],
    )(dist, se_streams, se_streams, se_streams, se_halo, se_halo, se_halo, mr_gates,
      mr_halo, se_feat, se_feat, se_feat, se_filt, mr_feat, mr_feat)


def long_kernel(dist_ref, tss_ref, spos_ref, mg_ref, mh_ref, wq_ref, prev_ref, z_ref, skip_ref, u_ref,
                out_ref, xa):
    rows = xa.shape[0]
    reach = mh_ref.shape[0]
    xa[HALO - reach : HALO, :] = mh_ref[...].astype(jnp.float32)
    xa[HALO:rows, :] = mg_ref[...].astype(jnp.float32)
    q2 = short_conv_rows(xa, wq_ref, HALO, dist_ref)
    blk = prev_ref.shape[1]
    tile = z_ref.shape[2]
    width = u_ref.shape[1]
    per_group = tile // u_ref.shape[0]
    z = z_ref[0]
    windows = (jnp.concatenate([prev_ref[0], z[:blk]], axis=0), z)
    masks = [
        spos_ref[:, b * blk : b * blk + width] >= tss_ref[b * blk : (b + 1) * blk, :] for b in range(2)
    ]
    lane_grp = lax.broadcasted_iota(jnp.int32, (1, GROUP_LANES), 1) // per_group
    halves = tile // GROUP_LANES
    groups_half = GROUP_LANES // per_group
    acc = [[jnp.zeros((blk, GROUP_LANES), jnp.float32) for _ in range(halves)] for _ in range(2)]
    for g in range(u_ref.shape[0]):
        half = g // groups_half
        row = jnp.broadcast_to(u_ref[g : g + 1, :], (blk, width))
        taps = pltpu.roll(row, 0, 1, stride=1, stride_axis=0)
        for b in range(2):
            mat = jnp.where(masks[b], taps, 0.0).astype(jnp.bfloat16)
            part = windows[b][:, half * GROUP_LANES : (half + 1) * GROUP_LANES]
            res = jnp.dot(mat, part, preferred_element_type=jnp.float32)
            acc[b][half] = jnp.where(lane_grp == g % groups_half, res, acc[b][half])
    conv = jnp.concatenate([jnp.concatenate(acc[b], axis=1) for b in range(2)], axis=0)
    mixed = (conv + skip_ref[...].astype(jnp.float32) * z.astype(jnp.float32)).astype(jnp.bfloat16)
    out_ref[...] = (q2 * mixed.astype(jnp.float32)).astype(jnp.bfloat16)


def long_conv_out(dist, tss, spos, mr_gates, mr_halo, mr_feat, prev_z, z_two, skip, taps_rows):
    steps, tok_rows, lanes = z_two.shape
    channels = steps * lanes
    blk = prev_z.shape[1]
    per_group = channels // taps_rows.shape[0]
    return pl.pallas_call(
        long_kernel,
        grid=(steps,),
        in_specs=[
            pl.BlockSpec(dist.shape, lambda j: (0, 0)),
            pl.BlockSpec(tss.shape, lambda j: (0, 0)),
            pl.BlockSpec(spos.shape, lambda j: (0, 0)),
            pl.BlockSpec((tok_rows, lanes), lambda j: (0, j)),
            pl.BlockSpec((mr_halo.shape[0], lanes), lambda j: (0, j)),
            pl.BlockSpec((mr_feat.shape[0], lanes), lambda j: (0, j)),
            pl.BlockSpec((1, blk, lanes), lambda j: (j, 0, 0)),
            pl.BlockSpec((1, tok_rows, lanes), lambda j: (j, 0, 0)),
            pl.BlockSpec((1, lanes), lambda j: (0, j)),
            pl.BlockSpec((lanes // per_group, taps_rows.shape[1]), lambda j: (j, 0)),
        ],
        out_specs=pl.BlockSpec((tok_rows, lanes), lambda j: (0, j)),
        out_shape=jax.ShapeDtypeStruct((tok_rows, channels), jnp.bfloat16),
        scratch_shapes=[pltpu.VMEM((tok_rows + HALO, lanes), jnp.float32)],
    )(dist, tss, spos, mr_gates, mr_halo, mr_feat, prev_z, z_two, skip, taps_rows)


def tail_kernel(begin_ref, first_ref, z_ref, out_ref):
    t = pl.program_id(0)
    begin = begin_ref[t]
    total = z_ref.shape[0]
    tail_len = out_ref.shape[1]
    start = jnp.clip((begin // 16) * 16, 0, total - WINDOW)
    shift = begin - start
    window = z_ref[pl.ds(pl.multiple_of(start, 16), WINDOW), :].astype(jnp.float32)
    moved = pltpu.roll(window, (WINDOW - shift) % WINDOW, 0)[:tail_len]
    pos = begin + lax.broadcasted_iota(jnp.int32, (tail_len, 1), 0)
    out_ref[0] = jnp.where(pos >= first_ref[t], moved, 0.0).astype(out_ref.dtype)


def cut_tails_all(z_all, begins, firsts, tail_len):
    total, lanes = z_all.shape
    count = begins.shape[0]
    return pl.pallas_call(
        tail_kernel,
        grid_spec=pltpu.PrefetchScalarGridSpec(
            num_scalar_prefetch=2,
            grid=(count,),
            in_specs=[pl.BlockSpec((total, lanes), lambda t, b, f: (0, 0))],
            out_specs=pl.BlockSpec((1, tail_len, lanes), lambda t, b, f: (t, 0, 0)),
        ),
        out_shape=jax.ShapeDtypeStruct((count, tail_len, lanes), z_all.dtype),
    )(begins, firsts, z_all)


def seg_start(positions, req_ends):
    seg = request_of(positions, req_ends)
    prev_end = jnp.where(seg > 0, pick_entries(req_ends, jnp.maximum(seg - 1, 0)), -1)
    return prev_end + 1


def pick_entries(lookup_table, indices):
    hits = indices[:, None] == jnp.arange(lookup_table.shape[0], dtype=jnp.int32)[None, :]
    return jnp.sum(jnp.where(hits, lookup_table[None, :], 0), axis=1)


def local(
    se_streams, mr_gates, se_feat, se_filter, mr_feat, mr_filter, mr_skip, req_ends, decode_row
):
    tok_rows = se_streams.shape[0]
    channels = mr_gates.shape[1] // 2
    shards = lax.axis_size("seq")
    device = lax.axis_index("seq")
    offset = device * tok_rows
    reach_rows = se_feat.shape[0] - 1
    tap_count = mr_filter.shape[0]
    tail_len = tap_count - 1
    group_ch = channels // se_filter.shape[1]
    total_req = req_ends.shape[0]
    slot_total = ENDS_MAX + 1
    rim_depth = 2 * reach_rows
    prev_se, prev_mr = passed_along(
        (se_streams[tok_rows - 3 * reach_rows :], mr_gates[tok_rows - reach_rows :]), "seq", 1
    )
    ext_pos = offset - HALO + jnp.arange(tok_rows + HALO, dtype=jnp.int32)
    dist = (ext_pos - seg_start(ext_pos, req_ends))[:, None]
    z_two = short_chain(
        dist,
        se_streams,
        prev_se,
        mr_gates,
        prev_mr,
        se_feat,
        jnp.repeat(se_filter, group_ch, axis=1),
        mr_feat,
        shards,
    )
    prev_z = passed_along(z_two[:, tok_rows - tap_count :], "seq", 1)
    received = lax.all_to_all(z_two, "seq", split_axis=0, concat_axis=0, tiled=True)
    tgt_pos = offset + jnp.arange(tok_rows, dtype=jnp.int32)
    tss = seg_start(tgt_pos, req_ends)[:, None]
    spos = (offset - tap_count + jnp.arange(tok_rows + tap_count, dtype=jnp.int32))[None, :]
    filt_t = mr_filter[::-1].T.astype(jnp.float32)
    filters = filt_t.shape[0]
    taps_rows = jnp.concatenate(
        [jnp.zeros((filters, 1), jnp.float32), filt_t, jnp.zeros((filters, tap_count - 1), jnp.float32)],
        axis=1,
    )
    hyena_out = long_conv_out(
        dist, tss, spos, mr_gates, prev_mr, mr_feat, prev_z, z_two, mr_skip[None, :], taps_rows
    )
    z_all = received.reshape(shards * tok_rows, received.shape[2])
    rows_ids = jnp.arange(total_req, dtype=jnp.int32)
    owner = jnp.sum(
        jnp.where(decode_row[None, :] == rows_ids[:, None], rows_ids[None, :], 0), axis=1
    )
    last_pos = pick_entries(req_ends, owner)
    first_pos = jnp.where(owner > 0, pick_entries(req_ends, jnp.maximum(owner - 1, 0)) + 1, 0)
    tail_cache = cut_tails_all(z_all, last_pos - tail_len + 1, first_pos, tail_len)
    return (hyena_out, tail_cache)


def solution(mesh):
    placed = (
        P(("groups", "seq"), None),
        P(("groups", "seq"), None),
        P(),
        P(),
        P(),
        P(),
        P(),
        P("groups"),
        P("groups"),
    )
    return jax.shard_map(
        local,
        mesh=mesh,
        in_specs=placed,
        out_specs=(P(("groups", "seq"), None), P("groups", None, "seq")),
        check_vma=False,
    )
```

time: 166 us -> 152 us (0.916)
  local copies, waits for them, and re-layouts: 31.4 us -> 10.9 us
  Pallas kernels: 58.6 us -> 65.7 us
  waiting for transfers between devices: 52.7 us -> 57.1 us
  other arithmetic: 8.2 us -> 4.09 us
    gather x48 -> x0, local copies, waits for them, and re-layouts: 20.1 us -> none
    pallas_call x1 -> x2, Pallas kernels: 16.9 us -> 29.3 us  [the longest x1 21.5 us: long_conv_out(): pl.pallas_call(long_kernel, grid=(steps,), in_specs=[pl.BlockSpec(dist.sh...]
    pallas_call x1, Pallas kernels: 41.7 us -> 36.4 us  [short_chain(): pl.pallas_call(chain_kernel, grid=(steps,), in_specs=[pl.BlockSpec((rows,...]
    ppermute x3, waiting for transfers between devices: 52.7 us -> 57.1 us  [passed_along(): return lax.ppermute(x, axis, pairs)]
    unnamed x15 -> x18, local copies, waits for them, and re-layouts: 1.21 us -> 4.7 us
    convert_element_type x2 -> x0, other arithmetic: 2.51 us -> none  [the longest x1 1.73 us: local(): se_feat.astype(jnp.float32)]
    pad x2 -> x0, local copies, waits for them, and re-layouts: 1.87 us -> none  [the longest x1 1.03 us: local(): se_halo = jnp.pad(prev_se, ((HALO - 3 * reach_rows, 0), (0, 0)))]
    concatenate x2 -> x0, local copies, waits for them, and re-layouts: 1.74 us -> none  [the longest x1 1.73 us: local(): jnp.concatenate([jnp.zeros((tap_count, z_all.shape[1]), z_all.dtype), z_a...]
  transfers between devices with their start and end apart: 4 -> 4, of which waited for: 2 -> 2; matrix products, arithmetic and copies ran while one was open for 8% -> 6% of each run, Pallas kernels for 10% -> 14%
where the time goes in v4:
time: 152 us; the launch traced here: 151 us
  Pallas kernels  65.7 us (43%)
  waiting for transfers between devices  57.1 us (38%)
  starting transfers between devices  12.9 us (8%)
  local copies, waits for them, and re-layouts  10.9 us (7%)
  other arithmetic  4.09 us (3%)
    ppermute x3, waiting for transfers between devices, passed_along(): return lax.ppermute(x, axis, pairs)  57.1 us
    pallas_call x1, Pallas kernels, short_chain(): pl.pallas_call(chain_kernel, grid=(steps,), in_specs=[pl.BlockSpec((rows,...  36.4 us
    pallas_call x1, Pallas kernels, long_conv_out(): pl.pallas_call(long_kernel, grid=(steps,), in_specs=[pl.BlockSpec(dist.sh...  21.5 us
    pallas_call x1, Pallas kernels, cut_tails_all(): pl.pallas_call(tail_kernel, grid_spec=pltpu.PrefetchScalarGridSpec(num_sc...  7.84 us
    ppermute x3, starting transfers between devices, passed_along(): return lax.ppermute(x, axis, pairs)  7.51 us
    all_to_all x1, starting transfers between devices, local(): lax.all_to_all(z_two, 'seq', split_axis=0, concat_axis=0, tiled=True)  5.43 us
    unnamed x18, local copies, waits for them, and re-layouts  4.7 us
  transfers between devices with their start and end apart: 4, of which 2 were waited for; matrix products, arithmetic and copies ran while one was open for 6% of the time, Pallas kernels for 14%

profile of v4, /device:TPU:18, one launch (start us, length us, event | category | flops | bytes accessed | tf_op | source)
XLA Modules:
  0.0 151.5 jit_solution(16224684740187806168)
XLA Ops:
  0.6 0.0 copy-start.5
  0.6 0.9 slice.9
  1.6 1.9 %collective-permute-start = (bf16[6,8192]{1,0:T(8,128)(2,1)S(1)}, bf16[6,8192]{1,0:T(8,128)(2,1)S(1)}, u32[]{:S(2)}, u32[]{:S(2)}) collective-permute-start(bf16[6,8192]{1,0:T(8,128)(2,1)S(1)} %slice.9), channel_id=1, source_target_pairs={{0,1},{1,2},{2,3},{3,4},{4,5},{5,6},{6,7},{7,8},{8,9},{9,10},{10,1... | collective-permute-start | bytes 294920 | tf_op jit(solution)/shard_map/ppermute | solution.py:14
  3.5 1.2 slice.10
  4.7 3.5 %collective-permute-start.1 = (bf16[18,12288]{1,0:T(8,128)(2,1)S(1)}, bf16[18,12288]{1,0:T(8,128)(2,1)S(1)}, u32[]{:S(2)}, u32[]{:S(2)}) collective-permute-start(bf16[18,12288]{1,0:T(8,128)(2,1)S(1)} %slice.10), channel_id=1, source_target_pairs={{0,1},{1,2},{2,3},{3,4},{4,5},{5,6},{6,7},{7,8},{8,9},{9,10},{10,1... | collective-permute-start | bytes 1327112 | tf_op jit(solution)/shard_map/ppermute | solution.py:14
  8.3 0.7 convert_reduce_fusion
  9.0 1.0 broadcast_in_dim.88
  10.0 1.2 reshape.94.filt
  11.2 0.0 copy-done.5
  11.2 0.1 select_reduce_fusion
  11.3 0.8 reshape_subtract_fusion.dist_ref
  12.1 0.0 collective-permute-done.gk_h.mh_ref
  12.1 0.0 copy-start.3
  12.1 4.7 %collective-permute-done.1.hq.hk.hv = bf16[18,12288]{1,0:T(8,128)(2,1)S(1)} collective-permute-done((bf16[18,12288]{1,0:T(8,128)(2,1)S(1)}, bf16[18,12288]{1,0:T(8,128)(2,1)S(1)}, u32[]{:S(2)}, u32[]{:S(2)}) %collective-permute-start.1) | collective-permute-done | bytes 442400 | tf_op jit(solution)/shard_map/ppermute | solution.py:14
  16.8 0.0 copy-done.3
  16.8 0.0 copy-start.1
  16.8 0.8 copy-done.1
  17.6 36.4 %shard_map.104.z_ref = bf16[16,256,256]{2,1,0:T(8,128)(2,1)} custom-call(s32[288,1]{1,0:T(8,128)} %reshape_subtract_fusion.dist_ref, bf16[256,12288]{1,0:T(8,128)(2,1)} %sv.1, bf16[256,12288]{1,0:T(8,128)(2,1)} %sv.1, bf16[256,12288]{1,0:T(8,128)(2,1)} %sv.1, bf16[18,12288]{1,0:T(8,128)(2,1)} %copy-done.1, bf16[18,12288]{1,0:T(8,128)(2,1)} %copy-done.1, ...), custom_call_target="tpu_custom_call" | custom-call | tf_op jit(solution)/shard_map/pallas_call | solution.py:90
  54.0 0.0 copy-start.7
  54.0 0.0 copy-start
  54.0 5.4 %all-to-all-start = ((bf16[16,256,256]{2,1,0:T(8,128)(2,1)}), bf16[16,256,256]{2,1,0:T(8,128)(2,1)}, u32[]{:S(2)}, u32[]{:S(2)}) async-start(bf16[16,256,256]{2,1,0:T(8,128)(2,1)} %shard_map.104.z_ref), calls=%async_computation | async-start | bytes 4194304 | tf_op jit(solution)/shard_map/all_to_all | solution.py:233
  59.5 0.0 copy-start.4
  59.5 0.0 copy-start.6
  59.5 0.0 copy-done.7
  59.5 0.1 select_reduce_fusion.4
  59.6 0.1 convert_reduce_fusion.1
  59.7 0.1 select_reduce_fusion.1
  59.8 0.0 copy-done
  59.8 0.1 slice.12
  59.9 2.1 %collective-permute-start.2 = (bf16[16,128,256]{2,1,0:T(8,128)(2,1)S(1)}, bf16[16,128,256]{2,1,0:T(8,128)(2,1)S(1)}, u32[]{:S(2)}, u32[]{:S(2)}) collective-permute-start(bf16[16,128,256]{2,1,0:T(8,128)(2,1)S(1)} %slice.12), channel_id=1, source_target_pairs={{0,1},{1,2},{2,3},{3,4},{4,5},{5,6},{6,7},{7,8},{8,9},{9,10},{10,1... | collective-permute-start | bytes 3145736 | tf_op jit(solution)/shard_map/ppermute | solution.py:14
  62.0 0.6 iota_add_fusion.1.spos_ref
  62.6 0.8 copy.19.tss_ref
  63.4 0.0 copy-done.4
  63.4 0.1 copy.18
  63.5 0.2 rev.3
  63.8 0.1 pad.2.clone
  63.8 0.0 copy-done.6
  63.8 0.6 broadcast_in_dim.89.skip_ref
  64.5 0.2 select_reduce_fusion.2
  64.6 0.5 compare_select_fusion
  65.2 0.8 maximum_maximum_fusion.u_ref
  66.0 52.4 %collective-permute-done.2.prev_ref = bf16[16,128,256]{2,1,0:T(8,128)(2,1)S(1)} collective-permute-done((bf16[16,128,256]{2,1,0:T(8,128)(2,1)S(1)}, bf16[16,128,256]{2,1,0:T(8,128)(2,1)S(1)}, u32[]{:S(2)}, u32[]{:S(2)}) %collective-permute-start.2) | collective-permute-done | bytes 1048608 | tf_op jit(solution)/shard_map/ppermute | solution.py:14
  118.4 0.0 copy-start.2
  118.4 1.0 copy-done.2
  119.4 21.5 %shard_map.105 = bf16[256,4096]{1,0:T(8,128)(2,1)} custom-call(s32[288,1]{1,0:T(8,128)} %reshape_subtract_fusion.dist_ref, s32[256,1]{1,0:T(8,128)} %copy.19.tss_ref, s32[1,384]{1,0:T(1,128)} %iota_add_fusion.1.spos_ref, bf16[256,8192]{1,0:T(8,128)(2,1)} %mg_ref.1, bf16[6,8192]{1,0:T(8,128)(2,1)} %copy-done.3, bf16[7,12288]{1,0:T(8,128)(2,1)} %wq_ref.1, ...), custom_call_target="tpu_custom_call" | custom-call | tf_op jit(solution)/shard_map/pallas_call | solution.py:141
  140.9 0.0 all-to-all-done
  140.9 7.8 %shard_map.106 = bf16[16,127,256]{2,1,0:T(8,128)(2,1)} custom-call(s32[16]{0:T(128)} %get-tuple-element.11.begin_ref, s32[16]{0:T(128)} %get-tuple-element.10.first_ref, bf16[4096,256]{1,0:T(8,128)(2,1)} %bitcast.2.z_ref), custom_call_target="tpu_custom_call" | custom-call | tf_op jit(solution)/shard_map/pallas_call | solution.py:178
  148.7 2.8 %copy.20 = bf16[16,127,256]{2,0,1:T(8,128)(2,1)} copy(bf16[16,127,256]{2,1,0:T(8,128)(2,1)} %shard_map.106) | data formatting | bytes 2080768
  (10 shorter events, 0.1 us)
Async XLA Ops:
  0.6 10.6 %copy-start.5 = (s32[16]{0:T(128)S(1)}, s32[16]{0:T(128)}, u32[]{:S(2)}) copy-start(s32[16]{0:T(128)} %param.16) | copy-start | bytes 196
  1.6 10.5 %collective-permute-start = (bf16[6,8192]{1,0:T(8,128)(2,1)S(1)}, bf16[6,8192]{1,0:T(8,128)(2,1)S(1)}, u32[]{:S(2)}, u32[]{:S(2)}) collective-permute-start(bf16[6,8192]{1,0:T(8,128)(2,1)S(1)} %slice.9), channel_id=1, source_target_pairs={{0,1},{1,2},{2,3},{3,4},{4,5},{5,6},{6,7},{7,8},{8,9},{9,10},{10,1... | collective-permute-start | bytes 294920 | tf_op jit(solution)/shard_map/ppermute | solution.py:14
  4.7 12.1 %collective-permute-start.1 = (bf16[18,12288]{1,0:T(8,128)(2,1)S(1)}, bf16[18,12288]{1,0:T(8,128)(2,1)S(1)}, u32[]{:S(2)}, u32[]{:S(2)}) collective-permute-start(bf16[18,12288]{1,0:T(8,128)(2,1)S(1)} %slice.10), channel_id=1, source_target_pairs={{0,1},{1,2},{2,3},{3,4},{4,5},{5,6},{6,7},{7,8},{8,9},{9,10},{10,1... | collective-permute-start | bytes 1327112 | tf_op jit(solution)/shard_map/ppermute | solution.py:14
  12.1 4.7 %copy-start.3 = (bf16[6,8192]{1,0:T(8,128)(2,1)}, bf16[6,8192]{1,0:T(8,128)(2,1)S(1)}, u32[]{:S(2)}) copy-start(bf16[6,8192]{1,0:T(8,128)(2,1)S(1)} %collective-permute-done.gk_h.mh_ref) | copy-start | bytes 294916
  16.8 0.8 copy-start.1
  54.0 5.5 %copy-start.7 = (s32[16]{0:T(128)S(1)}, s32[16]{0:T(128)}, u32[]{:S(2)}) copy-start(s32[16]{0:T(128)} %param.17) | copy-start | bytes 196
  54.0 5.8 %copy-start = (bf16[16,256,256]{2,1,0:T(8,128)(2,1)S(1)}, bf16[16,256,256]{2,1,0:T(8,128)(2,1)}, u32[]{:S(2)}) copy-start(bf16[16,256,256]{2,1,0:T(8,128)(2,1)} %shard_map.104.z_ref) | copy-start | bytes 6291460
  54.0 86.8 %all-to-all-start = ((bf16[16,256,256]{2,1,0:T(8,128)(2,1)}), bf16[16,256,256]{2,1,0:T(8,128)(2,1)}, u32[]{:S(2)}, u32[]{:S(2)}) async-start(bf16[16,256,256]{2,1,0:T(8,128)(2,1)} %shard_map.104.z_ref), calls=%async_computation | async-start | bytes 4194304 | tf_op jit(solution)/shard_map/all_to_all | solution.py:233
  59.5 3.9 %copy-start.4 = (bf16[128,256]{1,0:T(8,128)(2,1)S(1)}, bf16[128,256]{1,0:T(8,128)(2,1)}, u32[]{:S(2)}) copy-start(bf16[128,256]{1,0:T(8,128)(2,1)} %param.14) | copy-start | bytes 196612
  59.5 4.4 %copy-start.6 = (bf16[4096]{0:T(1024)(128)(2,1)S(1)}, bf16[4096]{0:T(1024)(128)(2,1)}, u32[]{:S(2)}) copy-start(bf16[4096]{0:T(1024)(128)(2,1)} %param.15) | copy-start | bytes 24580
  59.9 58.5 %collective-permute-start.2 = (bf16[16,128,256]{2,1,0:T(8,128)(2,1)S(1)}, bf16[16,128,256]{2,1,0:T(8,128)(2,1)S(1)}, u32[]{:S(2)}, u32[]{:S(2)}) collective-permute-start(bf16[16,128,256]{2,1,0:T(8,128)(2,1)S(1)} %slice.12), channel_id=1, source_target_pairs={{0,1},{1,2},{2,3},{3,4},{4,5},{5,6},{6,7},{7,8},{8,9},{9,10},{10,1... | collective-permute-start | bytes 3145736 | tf_op jit(solution)/shard_map/ppermute | solution.py:14
  118.4 1.0 copy-start.2

commit v5 on v4

--- a/solution.py
+++ b/solution.py
@@ -54,7 +54,8 @@
     rows = xq.shape[0]
     for main, halo, x in ((sq, hq, xq), (sk, hk, xk), (sv, hv, xv), (mk, gk_h, xb)):
         reach = halo.shape[0]
-        x[0 : HALO - reach, :] = jnp.zeros((HALO - reach, x.shape[1]), jnp.float32)
+        if reach < HALO:
+            x[0 : HALO - reach, :] = jnp.zeros((HALO - reach, x.shape[1]), jnp.float32)
         x[HALO - reach : HALO, :] = halo[...].astype(jnp.float32)
         x[HALO:rows, :] = main[...].astype(jnp.float32)
 
@@ -72,26 +73,30 @@
         z2_ref[i] = z2[:, i * chunk : (i + 1) * chunk]
 
 
-def short_chain(dist, se_streams, se_halo, mr_gates, mr_halo, se_feat, se_filt, mr_feat, shards):
-    tok_rows = se_streams.shape[0]
+def short_chain(dist, se_streams, se_halo, mr_gates, mr_halo, se_feat, se_filt, mr_feat, shards, half):
+    tok_rows = dist.shape[0] - HALO
     channels = mr_gates.shape[1] // 2
     steps = channels // TILE
     rows = tok_rows + HALO
     taps = se_feat.shape[0]
     chunk = channels // shards
 
-    def col(part):
-        return lambda j: (0, j + part * steps)
+    def col(part, row_block=half):
+        return lambda j: (row_block, j + part * steps)
+
+    def halo_spec(halo, part):
+        if halo.shape[0] < HALO:
+            return pl.BlockSpec((halo.shape[0], TILE), col(part, 0))
+        return pl.BlockSpec((HALO, TILE), col(part, half * tok_rows // HALO - 1))
 
     main = [pl.BlockSpec((tok_rows, TILE), col(p)) for p in range(3)]
-    halo = [pl.BlockSpec((se_halo.shape[0], TILE), col(p)) for p in range(3)]
-    mhalo = pl.BlockSpec((mr_halo.shape[0], TILE), col(1))
-    wts = [pl.BlockSpec((taps, TILE), col(p)) for p in range(3)]
+    halo = [halo_spec(se_halo, p) for p in range(3)]
+    wts = [pl.BlockSpec((taps, TILE), col(p, 0)) for p in range(3)]
     return pl.pallas_call(
         chain_kernel,
         grid=(steps,),
-        in_specs=[pl.BlockSpec((rows, 1), lambda j: (0, 0))] + main + halo + [main[1], mhalo] + wts
-        + [wts[0], wts[1], wts[2]],
+        in_specs=[pl.BlockSpec((rows, 1), lambda j: (0, 0))] + main + halo
+        + [main[1], halo_spec(mr_halo, 1)] + wts + [wts[0], wts[1], wts[2]],
         out_specs=pl.BlockSpec((TILE // chunk, tok_rows, chunk), lambda j: (j, 0, 0)),
         out_shape=jax.ShapeDtypeStruct((shards, tok_rows, chunk), jnp.bfloat16),
         scratch_shapes=[pltpu.VMEM((rows, TILE), jnp.float32) for _ in range(6)],
@@ -99,19 +104,20 @@
       mr_halo, se_feat, se_feat, se_feat, se_filt, mr_feat, mr_feat)
 
 
-def long_kernel(dist_ref, tss_ref, spos_ref, mg_ref, mh_ref, wq_ref, prev_ref, z_ref, skip_ref, u_ref,
-                out_ref, xa):
+def long_kernel(dist_ref, tss_ref, spos_ref, mg_ref, mh_ref, wq_ref, prev_ref, lo_ref, hi_ref, skip_ref,
+                u_ref, out_ref, xa):
     rows = xa.shape[0]
     reach = mh_ref.shape[0]
     xa[HALO - reach : HALO, :] = mh_ref[...].astype(jnp.float32)
     xa[HALO:rows, :] = mg_ref[...].astype(jnp.float32)
     q2 = short_conv_rows(xa, wq_ref, HALO, dist_ref)
-    blk = prev_ref.shape[1]
-    tile = z_ref.shape[2]
+    blk = lo_ref.shape[1]
+    tile = lo_ref.shape[2]
     width = u_ref.shape[1]
     per_group = tile // u_ref.shape[0]
-    z = z_ref[0]
-    windows = (jnp.concatenate([prev_ref[0], z[:blk]], axis=0), z)
+    lo = lo_ref[0]
+    hi = hi_ref[0]
+    windows = (jnp.concatenate([prev_ref[0], lo], axis=0), jnp.concatenate([lo, hi], axis=0))
     masks = [
         spos_ref[:, b * blk : b * blk + width] >= tss_ref[b * blk : (b + 1) * blk, :] for b in range(2)
     ]
@@ -129,15 +135,17 @@
             res = jnp.dot(mat, part, preferred_element_type=jnp.float32)
             acc[b][half] = jnp.where(lane_grp == g % groups_half, res, acc[b][half])
     conv = jnp.concatenate([jnp.concatenate(acc[b], axis=1) for b in range(2)], axis=0)
-    mixed = (conv + skip_ref[...].astype(jnp.float32) * z.astype(jnp.float32)).astype(jnp.bfloat16)
+    z = jnp.concatenate([lo, hi], axis=0).astype(jnp.float32)
+    mixed = (conv + skip_ref[...].astype(jnp.float32) * z).astype(jnp.bfloat16)
     out_ref[...] = (q2 * mixed.astype(jnp.float32)).astype(jnp.bfloat16)
 
 
-def long_conv_out(dist, tss, spos, mr_gates, mr_halo, mr_feat, prev_z, z_two, skip, taps_rows):
-    steps, tok_rows, lanes = z_two.shape
+def long_conv_out(dist, tss, spos, mr_gates, mr_halo, mr_feat, prev_z, z_lo, z_hi, skip, taps_rows):
+    steps, blk, lanes = z_lo.shape
+    tok_rows = 2 * blk
     channels = steps * lanes
-    blk = prev_z.shape[1]
     per_group = channels // taps_rows.shape[0]
+    piece = pl.BlockSpec((1, blk, lanes), lambda j: (j, 0, 0))
     return pl.pallas_call(
         long_kernel,
         grid=(steps,),
@@ -148,43 +156,48 @@
             pl.BlockSpec((tok_rows, lanes), lambda j: (0, j)),
             pl.BlockSpec((mr_halo.shape[0], lanes), lambda j: (0, j)),
             pl.BlockSpec((mr_feat.shape[0], lanes), lambda j: (0, j)),
-            pl.BlockSpec((1, blk, lanes), lambda j: (j, 0, 0)),
-            pl.BlockSpec((1, tok_rows, lanes), lambda j: (j, 0, 0)),
+            piece,
+            piece,
+            piece,
             pl.BlockSpec((1, lanes), lambda j: (0, j)),
             pl.BlockSpec((lanes // per_group, taps_rows.shape[1]), lambda j: (j, 0)),
         ],
         out_specs=pl.BlockSpec((tok_rows, lanes), lambda j: (0, j)),
         out_shape=jax.ShapeDtypeStruct((tok_rows, channels), jnp.bfloat16),
         scratch_shapes=[pltpu.VMEM((tok_rows + HALO, lanes), jnp.float32)],
-    )(dist, tss, spos, mr_gates, mr_halo, mr_feat, prev_z, z_two, skip, taps_rows)
-
-
-def tail_kernel(begin_ref, first_ref, z_ref, out_ref):
-    t = pl.program_id(0)
-    begin = begin_ref[t]
-    total = z_ref.shape[0]
-    tail_len = out_ref.shape[1]
-    start = jnp.clip((begin // 16) * 16, 0, total - WINDOW)
-    shift = begin - start
-    window = z_ref[pl.ds(pl.multiple_of(start, 16), WINDOW), :].astype(jnp.float32)
-    moved = pltpu.roll(window, (WINDOW - shift) % WINDOW, 0)[:tail_len]
-    pos = begin + lax.broadcasted_iota(jnp.int32, (tail_len, 1), 0)
-    out_ref[0] = jnp.where(pos >= first_ref[t], moved, 0.0).astype(out_ref.dtype)
-
-
-def cut_tails_all(z_all, begins, firsts, tail_len):
-    total, lanes = z_all.shape
+    )(dist, tss, spos, mr_gates, mr_halo, mr_feat, prev_z, z_lo, z_hi, skip, taps_rows)
+
+
+def tail_kernel(begin_ref, first_ref, lo_ref, hi_ref, out_ref, z_all):
+    shards, blk, lanes = lo_ref.shape
+    tail_len = out_ref.shape[0]
+    total = z_all.shape[0]
+    for src in range(shards):
+        z_all[2 * src * blk : (2 * src + 1) * blk, :] = lo_ref[src].astype(jnp.float32)
+        z_all[(2 * src + 1) * blk : (2 * src + 2) * blk, :] = hi_ref[src].astype(jnp.float32)
+    for t in range(out_ref.shape[1]):
+        begin = begin_ref[t]
+        start = jnp.clip((begin // 16) * 16, 0, total - WINDOW)
+        shift = begin - start
+        window = z_all[pl.ds(pl.multiple_of(start, 16), WINDOW), :]
+        moved = pltpu.roll(window, (WINDOW - shift) % WINDOW, 0)[:tail_len]
+        pos = begin + lax.broadcasted_iota(jnp.int32, (tail_len, 1), 0)
+        out_ref[:, t, :] = jnp.where(pos >= first_ref[t], moved, 0.0).astype(out_ref.dtype)
+
+
+def cut_tails_all(z_lo, z_hi, begins, firsts, tail_len):
+    shards, blk, lanes = z_lo.shape
     count = begins.shape[0]
-    return pl.pallas_call(
+    smem = pl.BlockSpec(memory_space=pltpu.SMEM)
+    vmem = pl.BlockSpec(memory_space=pltpu.VMEM)
+    out = pl.pallas_call(
         tail_kernel,
-        grid_spec=pltpu.PrefetchScalarGridSpec(
-            num_scalar_prefetch=2,
-            grid=(count,),
-            in_specs=[pl.BlockSpec((total, lanes), lambda t, b, f: (0, 0))],
-            out_specs=pl.BlockSpec((1, tail_len, lanes), lambda t, b, f: (t, 0, 0)),
-        ),
-        out_shape=jax.ShapeDtypeStruct((count, tail_len, lanes), z_all.dtype),
-    )(begins, firsts, z_all)
+        in_specs=[smem, smem, vmem, vmem],
+        out_specs=vmem,
+        out_shape=jax.ShapeDtypeStruct((tail_len, count, lanes), z_lo.dtype),
+        scratch_shapes=[pltpu.VMEM((2 * shards * blk, lanes), jnp.float32)],
+    )(begins, firsts, z_lo, z_hi)
+    return jnp.transpose(out, (1, 0, 2))
 
 
 def seg_start(positions, req_ends):
@@ -216,41 +229,47 @@
     prev_se, prev_mr = passed_along(
         (se_streams[tok_rows - 3 * reach_rows :], mr_gates[tok_rows - reach_rows :]), "seq", 1
     )
-    ext_pos = offset - HALO + jnp.arange(tok_rows + HALO, dtype=jnp.int32)
-    dist = (ext_pos - seg_start(ext_pos, req_ends))[:, None]
-    z_two = short_chain(
-        dist,
-        se_streams,
-        prev_se,
-        mr_gates,
-        prev_mr,
-        se_feat,
-        jnp.repeat(se_filter, group_ch, axis=1),
-        mr_feat,
-        shards,
-    )
-    prev_z = passed_along(z_two[:, tok_rows - tap_count :], "seq", 1)
-    received = lax.all_to_all(z_two, "seq", split_axis=0, concat_axis=0, tiled=True)
-    tgt_pos = offset + jnp.arange(tok_rows, dtype=jnp.int32)
-    tss = seg_start(tgt_pos, req_ends)[:, None]
-    spos = (offset - tap_count + jnp.arange(tok_rows + tap_count, dtype=jnp.int32))[None, :]
+    blk = tok_rows // 2
+    se_filt = jnp.repeat(se_filter, group_ch, axis=1)
+
+    def dist_of(half):
+        ext_pos = offset + half * blk - HALO + jnp.arange(blk + HALO, dtype=jnp.int32)
+        return (ext_pos - seg_start(ext_pos, req_ends))[:, None]
+
+    dists = [dist_of(0), dist_of(1)]
+    z_hi = short_chain(
+        dists[1], se_streams, se_streams, mr_gates, mr_gates, se_feat, se_filt, mr_feat, shards, 1
+    )
+    prev_z = passed_along(z_hi, "seq", 1)
+    z_hi, prev_se, prev_mr = lax.optimization_barrier((z_hi, prev_se, prev_mr))
+    recv_hi = lax.all_to_all(z_hi, "seq", split_axis=0, concat_axis=0, tiled=True)
+    z_lo = short_chain(
+        dists[0], se_streams, prev_se, mr_gates, prev_mr, se_feat, se_filt, mr_feat, shards, 0
+    )
+    z_lo, recv_hi = lax.optimization_barrier((z_lo, recv_hi))
+    recv_lo = lax.all_to_all(z_lo, "seq", split_axis=0, concat_axis=0, tiled=True)
     filt_t = mr_filter[::-1].T.astype(jnp.float32)
     filters = filt_t.shape[0]
     taps_rows = jnp.concatenate(
         [jnp.zeros((filters, 1), jnp.float32), filt_t, jnp.zeros((filters, tap_count - 1), jnp.float32)],
         axis=1,
     )
+
+    tgt_pos = offset + jnp.arange(tok_rows, dtype=jnp.int32)
+    tss = seg_start(tgt_pos, req_ends)[:, None]
+    spos = (offset - blk + jnp.arange(tok_rows + blk, dtype=jnp.int32))[None, :]
+    ext_pos = offset - HALO + jnp.arange(tok_rows + HALO, dtype=jnp.int32)
+    dist = (ext_pos - seg_start(ext_pos, req_ends))[:, None]
     hyena_out = long_conv_out(
-        dist, tss, spos, mr_gates, prev_mr, mr_feat, prev_z, z_two, mr_skip[None, :], taps_rows
-    )
-    z_all = received.reshape(shards * tok_rows, received.shape[2])
+        dist, tss, spos, mr_gates, prev_mr, mr_feat, prev_z, z_lo, z_hi, mr_skip[None, :], taps_rows
+    )
     rows_ids = jnp.arange(total_req, dtype=jnp.int32)
     owner = jnp.sum(
         jnp.where(decode_row[None, :] == rows_ids[:, None], rows_ids[None, :], 0), axis=1
     )
     last_pos = pick_entries(req_ends, owner)
     first_pos = jnp.where(owner > 0, pick_entries(req_ends, jnp.maximum(owner - 1, 0)) + 1, 0)
-    tail_cache = cut_tails_all(z_all, last_pos - tail_len + 1, first_pos, tail_len)
+    tail_cache = cut_tails_all(recv_lo, recv_hi, last_pos - tail_len + 1, first_pos, tail_len)
     return (hyena_out, tail_cache)
 
 

time: 152 us -> 118 us (0.78)
  waiting for transfers between devices: 57.1 us -> 18.4 us
  starting transfers between devices: 12.9 us -> 17 us
  local copies, waits for them, and re-layouts: 10.9 us -> 7.4 us
  other arithmetic: 4.09 us -> 6.28 us
  Pallas kernels: 65.7 us -> 67.7 us
    ppermute x3, waiting for transfers between devices: 57.1 us -> 16 us  [passed_along(): return lax.ppermute(x, axis, pairs)]
    pallas_call x1 -> x2, Pallas kernels: 36.4 us -> 40.5 us  [short_chain(): pl.pallas_call(chain_kernel, grid=(steps,), in_specs=[pl.BlockSpec((rows,...]
    all_to_all x1 -> x2, starting transfers between devices: 5.43 us -> 9.46 us  [the longest x1 5.24 us: local(): lax.all_to_all(z_hi, 'seq', split_axis=0, concat_axis=0, tiled=True)]
    unnamed x18 -> x17, local copies, waits for them, and re-layouts: 4.7 us -> 1.12 us
    all_to_all x1 -> x2, waiting for transfers between devices: 0.01 us -> 2.4 us  [the longest x1 2.39 us: local(): lax.all_to_all(z_hi, 'seq', split_axis=0, concat_axis=0, tiled=True)]
    pallas_call x1, Pallas kernels: 7.84 us -> 5.65 us  [cut_tails_all(): pl.pallas_call(tail_kernel, in_specs=[smem, smem, vmem, vmem], out_specs=...]
  transfers between devices with their start and end apart: 4 -> 5, of which waited for: 2 -> 2; matrix products, arithmetic and copies ran while one was open for 6% -> 10% of each run, Pallas kernels for 14% -> 53%
where the time goes in v5:
time: 118 us
  Pallas kernels  67.7 us (57%)
  waiting for transfers between devices  18.4 us (16%)
  starting transfers between devices  17 us (14%)
  local copies, waits for them, and re-layouts  7.4 us (6%)
  other arithmetic  6.28 us (5%)
    pallas_call x2, Pallas kernels, short_chain(): pl.pallas_call(chain_kernel, grid=(steps,), in_specs=[pl.BlockSpec((rows,...  40.5 us
    pallas_call x1, Pallas kernels, long_conv_out(): pl.pallas_call(long_kernel, grid=(steps,), in_specs=[pl.BlockSpec(dist.sh...  21.5 us
    ppermute x3, waiting for transfers between devices, passed_along(): return lax.ppermute(x, axis, pairs)  16 us
    ppermute x3, starting transfers between devices, passed_along(): return lax.ppermute(x, axis, pairs)  7.5 us
    pallas_call x1, Pallas kernels, cut_tails_all(): pl.pallas_call(tail_kernel, in_specs=[smem, smem, vmem, vmem], out_specs=...  5.65 us
    all_to_all x1, starting transfers between devices, local(): lax.all_to_all(z_hi, 'seq', split_axis=0, concat_axis=0, tiled=True)  5.24 us
    all_to_all x1, starting transfers between devices, local(): lax.all_to_all(z_lo, 'seq', split_axis=0, concat_axis=0, tiled=True)  4.22 us
    all_to_all x1, waiting for transfers between devices, local(): lax.all_to_all(z_hi, 'seq', split_axis=0, concat_axis=0, tiled=True)  2.39 us
  transfers between devices with their start and end apart: 5, of which 2 were waited for; matrix products, arithmetic and copies ran while one was open for 10% of the time, Pallas kernels for 53%

profile of v5, /device:TPU:18, one launch (start us, length us, event | category | flops | bytes accessed | tf_op | source)
XLA Modules:
  0.0 117.6 jit_solution(1607016423690090830)
XLA Ops:
  0.6 0.9 slice.7
  1.6 1.9 %collective-permute-start.1 = (bf16[6,8192]{1,0:T(8,128)(2,1)S(1)}, bf16[6,8192]{1,0:T(8,128)(2,1)S(1)}, u32[]{:S(2)}, u32[]{:S(2)}) collective-permute-start(bf16[6,8192]{1,0:T(8,128)(2,1)S(1)} %slice.7), channel_id=1, source_target_pairs={{0,1},{1,2},{2,3},{3,4},{4,5},{5,6},{6,7},{7,8},{8,9},{9,10},{10,1... | collective-permute-start | bytes 294920 | tf_op jit(solution)/shard_map/ppermute | solution.py:14
  3.5 1.2 %slice.6 = bf16[18,12288]{1,0:T(8,128)(2,1)S(1)} slice(bf16[256,12288]{1,0:T(8,128)(2,1)} %sv.3), slice={[238:256], [0:12288]} | slice | bytes 884736 | tf_op jit(solution)/shard_map/slice | solution.py:230
  4.7 3.5 %collective-permute-start = (bf16[18,12288]{1,0:T(8,128)(2,1)S(1)}, bf16[18,12288]{1,0:T(8,128)(2,1)S(1)}, u32[]{:S(2)}, u32[]{:S(2)}) collective-permute-start(bf16[18,12288]{1,0:T(8,128)(2,1)S(1)} %slice.6), channel_id=1, source_target_pairs={{0,1},{1,2},{2,3},{3,4},{4,5},{5,6},{6,7},{7,8},{8,9},{9,10},{10,1... | collective-permute-start | bytes 1327112 | tf_op jit(solution)/shard_map/ppermute | solution.py:14
  8.3 0.7 convert_reduce_fusion.1
  9.0 0.7 select_reduce_fusion.1
  9.8 0.1 copy.25
  9.9 0.7 add_subtract_fusion.1.dist_ref
  10.6 1.0 broadcast_in_dim.118
  11.6 1.2 %reshape.169.filt = bf16[7,4096]{1,0:T(8,128)(2,1)} reshape(bf16[7,256,16]{2,1,0:T(8,128)(2,1)S(1)} %broadcast_in_dim.118) | data formatting | bytes 114688 | tf_op jit(solution)/shard_map/reshape | solution.py:233
  12.8 20.2 %shard_map.104.hi_ref = bf16[16,128,256]{2,1,0:T(8,128)(2,1)} custom-call(s32[160,1]{1,0:T(8,128)} %add_subtract_fusion.1.dist_ref, bf16[256,12288]{1,0:T(8,128)(2,1)} %sv.3, bf16[256,12288]{1,0:T(8,128)(2,1)} %sv.3, bf16[256,12288]{1,0:T(8,128)(2,1)} %sv.3, bf16[256,12288]{1,0:T(8,128)(2,1)} %sv.3, bf16[256,12288]{1,0:T(8,128)(2,1)} %sv.3, ...), custom_call_target="tpu_custom_call" | custom-call | tf_op jit(solution)/shard_map/pallas_call | solution.py:95
  33.0 0.0 collective-permute-done.1.gk_h.mh_ref
  33.0 0.0 copy-start.3
  33.0 0.0 collective-permute-done.hq.hk.hv
  33.0 0.0 copy-start
  33.0 5.2 %all-to-all-start = ((bf16[16,128,256]{2,1,0:T(8,128)(2,1)}), bf16[16,128,256]{2,1,0:T(8,128)(2,1)S(1)}, u32[]{:S(2)}, u32[]{:S(2)}) async-start(bf16[16,128,256]{2,1,0:T(8,128)(2,1)} %shard_map.104.hi_ref), calls=%async_computation | async-start | bytes 2097152 | tf_op jit(solution)/shard_map/all_to_all | solution.py:245
  38.3 2.0 %collective-permute-start.2 = (bf16[16,128,256]{2,1,0:T(8,128)(2,1)}, bf16[16,128,256]{2,1,0:T(8,128)(2,1)}, u32[]{:S(2)}, u32[]{:S(2)}) collective-permute-start(bf16[16,128,256]{2,1,0:T(8,128)(2,1)} %shard_map.104.hi_ref), channel_id=1, source_target_pairs={{0,1},{1,2},{2,3},{3,4},{4,5},{5,6},{6,7},{7,8},{8,9},{9,10},{10,1... | collective-permute-start | bytes 3145736 | tf_op jit(solution)/shard_map/ppermute | solution.py:14
  40.3 0.1 copy.27
  40.5 0.0 copy-done.5
  40.5 0.1 convert_reduce_fusion.3
  40.6 0.1 convert_reduce_fusion
  40.7 0.6 add_subtract_fusion.dist_ref
  41.3 0.0 copy-done.3
  41.3 0.0 copy-done
  41.3 0.0 copy-start.4
  41.4 20.3 %shard_map.105.lo_ref = bf16[16,128,256]{2,1,0:T(8,128)(2,1)} custom-call(s32[160,1]{1,0:T(8,128)} %add_subtract_fusion.dist_ref, bf16[256,12288]{1,0:T(8,128)(2,1)} %sv.3, bf16[256,12288]{1,0:T(8,128)(2,1)} %sv.3, bf16[256,12288]{1,0:T(8,128)(2,1)} %sv.3, bf16[18,12288]{1,0:T(8,128)(2,1)} %copy-done, bf16[18,12288]{1,0:T(8,128)(2,1)} %copy-done, ...), custom_call_target="tpu_custom_call" | custom-call | tf_op jit(solution)/shard_map/pallas_call | solution.py:95
  61.6 2.4 %all-to-all-done.hi_ref = bf16[16,128,256]{2,1,0:T(8,128)(2,1)S(1)} async-done(((bf16[16,128,256]{2,1,0:T(8,128)(2,1)}), bf16[16,128,256]{2,1,0:T(8,128)(2,1)S(1)}, u32[]{:S(2)}, u32[]{:S(2)}) %all-to-all-start) | async-done | bytes 1048608 | tf_op jit(solution)/shard_map/all_to_all | solution.py:245
  64.0 4.2 %all-to-all-start.1 = ((bf16[16,128,256]{2,1,0:T(8,128)(2,1)}), bf16[16,128,256]{2,1,0:T(8,128)(2,1)S(1)}, u32[]{:S(2)}, u32[]{:S(2)}) async-start(bf16[16,128,256]{2,1,0:T(8,128)(2,1)} %shard_map.105.lo_ref), calls=%async_computation.1 | async-start | bytes 2097152 | tf_op jit(solution)/shard_map/all_to_all | solution.py:250
  68.2 0.0 copy-done.7
  68.2 0.1 select_reduce_fusion.6
  68.4 0.1 select_reduce_fusion.3
  68.4 0.1 select_reduce_fusion
  68.5 0.2 select_reduce_fusion.4
  68.7 0.6 iota_add_fusion.1.spos_ref
  69.3 0.1 pad.2.clone
  69.4 0.6 broadcast_in_dim.119.skip_ref
  70.0 0.1 copy.28
  70.1 0.2 rev.3
  70.4 0.8 copy.29.tss_ref
  71.2 0.8 reshape_subtract_fusion.dist_ref
  71.9 0.6 compare_select_fusion
  72.5 0.8 maximum_maximum_fusion.u_ref
  73.4 16.0 %collective-permute-done.2.prev_ref = bf16[16,128,256]{2,1,0:T(8,128)(2,1)} collective-permute-done((bf16[16,128,256]{2,1,0:T(8,128)(2,1)}, bf16[16,128,256]{2,1,0:T(8,128)(2,1)}, u32[]{:S(2)}, u32[]{:S(2)}) %collective-permute-start.2) | collective-permute-done | bytes 1048608 | tf_op jit(solution)/shard_map/ppermute | solution.py:14
  89.4 21.5 %shard_map.106 = bf16[256,4096]{1,0:T(8,128)(2,1)} custom-call(s32[288,1]{1,0:T(8,128)} %reshape_subtract_fusion.dist_ref, s32[256,1]{1,0:T(8,128)} %copy.29.tss_ref, s32[1,384]{1,0:T(1,128)} %iota_add_fusion.1.spos_ref, bf16[256,8192]{1,0:T(8,128)(2,1)} %mg_ref.1, bf16[6,8192]{1,0:T(8,128)(2,1)} %copy-done.3, bf16[7,12288]{1,0:T(8,128)(2,1)} %wq_ref.1, ...), custom_call_target="tpu_custom_call" | custom-call | tf_op jit(solution)/shard_map/pallas_call | solution.py:149
  110.9 0.0 copy-done.1
  110.9 0.0 all-to-all-done.1.lo_ref
  111.0 1.0 copy-done.2
  111.9 5.6 %shard_map.107 = bf16[127,16,256]{2,1,0:T(8,128)(2,1)} custom-call(s32[16]{0:T(128)} %get-tuple-element.21.begin_ref, s32[16]{0:T(128)} %get-tuple-element.20.first_ref, bf16[16,128,256]{2,1,0:T(8,128)(2,1)} %copy-done.2, bf16[16,128,256]{2,1,0:T(8,128)(2,1)} %copy-done.1), custom_call_target="tpu_custom_call" | custom-call | tf_op jit(solution)/shard_map/pallas_call | solution.py:193
  (22 shorter events, 0.1 us)
Async XLA Ops:
  1.6 31.4 %collective-permute-start.1 = (bf16[6,8192]{1,0:T(8,128)(2,1)S(1)}, bf16[6,8192]{1,0:T(8,128)(2,1)S(1)}, u32[]{:S(2)}, u32[]{:S(2)}) collective-permute-start(bf16[6,8192]{1,0:T(8,128)(2,1)S(1)} %slice.7), channel_id=1, source_target_pairs={{0,1},{1,2},{2,3},{3,4},{4,5},{5,6},{6,7},{7,8},{8,9},{9,10},{10,1... | collective-permute-start | bytes 294920 | tf_op jit(solution)/shard_map/ppermute | solution.py:14
  4.7 28.3 %collective-permute-start = (bf16[18,12288]{1,0:T(8,128)(2,1)S(1)}, bf16[18,12288]{1,0:T(8,128)(2,1)S(1)}, u32[]{:S(2)}, u32[]{:S(2)}) collective-permute-start(bf16[18,12288]{1,0:T(8,128)(2,1)S(1)} %slice.6), channel_id=1, source_target_pairs={{0,1},{1,2},{2,3},{3,4},{4,5},{5,6},{6,7},{7,8},{8,9},{9,10},{10,1... | collective-permute-start | bytes 1327112 | tf_op jit(solution)/shard_map/ppermute | solution.py:14
  12.8 27.7 %copy-start.5 = (s32[16]{0:T(128)S(1)}, s32[16]{0:T(128)}, u32[]{:S(2)}) copy-start(s32[16]{0:T(128)} %param.16) | copy-start | bytes 196
  33.0 8.3 %copy-start.3 = (bf16[6,8192]{1,0:T(8,128)(2,1)}, bf16[6,8192]{1,0:T(8,128)(2,1)S(1)}, u32[]{:S(2)}) copy-start(bf16[6,8192]{1,0:T(8,128)(2,1)S(1)} %collective-permute-done.1.gk_h.mh_ref) | copy-start | bytes 294916
  33.0 8.3 %copy-start = (bf16[18,12288]{1,0:T(8,128)(2,1)}, bf16[18,12288]{1,0:T(8,128)(2,1)S(1)}, u32[]{:S(2)}) copy-start(bf16[18,12288]{1,0:T(8,128)(2,1)S(1)} %collective-permute-done.hq.hk.hv) | copy-start | bytes 1327108
  33.0 31.0 %all-to-all-start = ((bf16[16,128,256]{2,1,0:T(8,128)(2,1)}), bf16[16,128,256]{2,1,0:T(8,128)(2,1)S(1)}, u32[]{:S(2)}, u32[]{:S(2)}) async-start(bf16[16,128,256]{2,1,0:T(8,128)(2,1)} %shard_map.104.hi_ref), calls=%async_computation | async-start | bytes 2097152 | tf_op jit(solution)/shard_map/all_to_all | solution.py:245
  38.3 51.1 %collective-permute-start.2 = (bf16[16,128,256]{2,1,0:T(8,128)(2,1)}, bf16[16,128,256]{2,1,0:T(8,128)(2,1)}, u32[]{:S(2)}, u32[]{:S(2)}) collective-permute-start(bf16[16,128,256]{2,1,0:T(8,128)(2,1)} %shard_map.104.hi_ref), channel_id=1, source_target_pairs={{0,1},{1,2},{2,3},{3,4},{4,5},{5,6},{6,7},{7,8},{8,9},{9,10},{10,1... | collective-permute-start | bytes 3145736 | tf_op jit(solution)/shard_map/ppermute | solution.py:14
  41.3 26.9 %copy-start.7 = (s32[16]{0:T(128)S(1)}, s32[16]{0:T(128)}, u32[]{:S(2)}) copy-start(s32[16]{0:T(128)} %param.17) | copy-start | bytes 196
  41.3 28.1 %copy-start.6 = (bf16[4096]{0:T(1024)(128)(2,1)S(1)}, bf16[4096]{0:T(1024)(128)(2,1)}, u32[]{:S(2)}) copy-start(bf16[4096]{0:T(1024)(128)(2,1)} %param.15) | copy-start | bytes 24580
  41.3 28.7 %copy-start.4 = (bf16[128,256]{1,0:T(8,128)(2,1)S(1)}, bf16[128,256]{1,0:T(8,128)(2,1)}, u32[]{:S(2)}) copy-start(bf16[128,256]{1,0:T(8,128)(2,1)} %param.14) | copy-start | bytes 196612
  64.0 46.9 %copy-start.1 = (bf16[16,128,256]{2,1,0:T(8,128)(2,1)}, bf16[16,128,256]{2,1,0:T(8,128)(2,1)S(1)}, u32[]{:S(2)}) copy-start(bf16[16,128,256]{2,1,0:T(8,128)(2,1)S(1)} %all-to-all-done.hi_ref) | copy-start | bytes 3145732
  64.0 46.9 %all-to-all-start.1 = ((bf16[16,128,256]{2,1,0:T(8,128)(2,1)}), bf16[16,128,256]{2,1,0:T(8,128)(2,1)S(1)}, u32[]{:S(2)}, u32[]{:S(2)}) async-start(bf16[16,128,256]{2,1,0:T(8,128)(2,1)} %shard_map.105.lo_ref), calls=%async_computation.1 | async-start | bytes 2097152 | tf_op jit(solution)/shard_map/all_to_all | solution.py:250
  111.0 1.0 copy-start.2

commit v6 on v5

--- a/solution.py
+++ b/solution.py
@@ -34,7 +34,7 @@
 
 
 HALO = 32
-TILE = 512
+TILE = 1024
 GROUP_LANES = 128
 WINDOW = 144
 

time: 118 us -> 118 us (level)
  waiting for transfers between devices: 18.4 us -> 17 us
  Pallas kernels: 67.7 us -> 69 us
    pallas_call x2, Pallas kernels: 40.5 us -> 41.8 us  [short_chain(): pl.pallas_call(chain_kernel, grid=(steps,), in_specs=[pl.BlockSpec((rows,...]
  transfers between devices with their start and end apart: 5 -> 5, of which waited for: 2 -> 2; matrix products, arithmetic and copies ran while one was open for 10% -> 10% of each run, Pallas kernels for 53% -> 54%
where the time goes in v6:
time: 118 us
  Pallas kernels  69 us (58%)
  starting transfers between devices  17.4 us (15%)
  waiting for transfers between devices  17 us (14%)
  local copies, waits for them, and re-layouts  7.4 us (6%)
  other arithmetic  6.28 us (5%)
    pallas_call x2, Pallas kernels, short_chain(): pl.pallas_call(chain_kernel, grid=(steps,), in_specs=[pl.BlockSpec((rows,...  41.8 us
    pallas_call x1, Pallas kernels, long_conv_out(): pl.pallas_call(long_kernel, grid=(steps,), in_specs=[pl.BlockSpec(dist.sh...  21.6 us
    ppermute x3, waiting for transfers between devices, passed_along(): return lax.ppermute(x, axis, pairs)  15.2 us
    ppermute x3, starting transfers between devices, passed_along(): return lax.ppermute(x, axis, pairs)  7.5 us
    pallas_call x1, Pallas kernels, cut_tails_all(): pl.pallas_call(tail_kernel, in_specs=[smem, smem, vmem, vmem], out_specs=...  5.65 us
    all_to_all x1, starting transfers between devices, local(): lax.all_to_all(z_hi, 'seq', split_axis=0, concat_axis=0, tiled=True)  5.24 us
    all_to_all x1, starting transfers between devices, local(): lax.all_to_all(z_lo, 'seq', split_axis=0, concat_axis=0, tiled=True)  4.61 us
  transfers between devices with their start and end apart: 5, of which 2 were waited for; matrix products, arithmetic and copies ran while one was open for 10% of the time, Pallas kernels for 54%

profile of v6, /device:TPU:18, one launch (start us, length us, event | category | flops | bytes accessed | tf_op | source)
XLA Modules:
  0.0 117.9 jit_solution(1909889768489950786)
XLA Ops:
  0.6 0.9 slice.7
  1.6 1.9 %collective-permute-start.1 = (bf16[6,8192]{1,0:T(8,128)(2,1)S(1)}, bf16[6,8192]{1,0:T(8,128)(2,1)S(1)}, u32[]{:S(2)}, u32[]{:S(2)}) collective-permute-start(bf16[6,8192]{1,0:T(8,128)(2,1)S(1)} %slice.7), channel_id=1, source_target_pairs={{0,1},{1,2},{2,3},{3,4},{4,5},{5,6},{6,7},{7,8},{8,9},{9,10},{10,1... | collective-permute-start | bytes 294920 | tf_op jit(solution)/shard_map/ppermute | solution.py:14
  3.5 1.2 %slice.6 = bf16[18,12288]{1,0:T(8,128)(2,1)S(1)} slice(bf16[256,12288]{1,0:T(8,128)(2,1)} %sv.3), slice={[238:256], [0:12288]} | slice | bytes 884736 | tf_op jit(solution)/shard_map/slice | solution.py:230
  4.7 3.5 %collective-permute-start = (bf16[18,12288]{1,0:T(8,128)(2,1)S(1)}, bf16[18,12288]{1,0:T(8,128)(2,1)S(1)}, u32[]{:S(2)}, u32[]{:S(2)}) collective-permute-start(bf16[18,12288]{1,0:T(8,128)(2,1)S(1)} %slice.6), channel_id=1, source_target_pairs={{0,1},{1,2},{2,3},{3,4},{4,5},{5,6},{6,7},{7,8},{8,9},{9,10},{10,1... | collective-permute-start | bytes 1327112 | tf_op jit(solution)/shard_map/ppermute | solution.py:14
  8.3 0.7 convert_reduce_fusion.1
  9.0 0.7 select_reduce_fusion.1
  9.8 0.1 copy.25
  9.9 0.7 add_subtract_fusion.1.dist_ref
  10.6 1.0 broadcast_in_dim.118
  11.6 1.2 %reshape.169.filt = bf16[7,4096]{1,0:T(8,128)(2,1)} reshape(bf16[7,256,16]{2,1,0:T(8,128)(2,1)S(1)} %broadcast_in_dim.118) | data formatting | bytes 114688 | tf_op jit(solution)/shard_map/reshape | solution.py:233
  12.8 20.9 %shard_map.104.hi_ref = bf16[16,128,256]{2,1,0:T(8,128)(2,1)} custom-call(s32[160,1]{1,0:T(8,128)} %add_subtract_fusion.1.dist_ref, bf16[256,12288]{1,0:T(8,128)(2,1)} %sv.3, bf16[256,12288]{1,0:T(8,128)(2,1)} %sv.3, bf16[256,12288]{1,0:T(8,128)(2,1)} %sv.3, bf16[256,12288]{1,0:T(8,128)(2,1)} %sv.3, bf16[256,12288]{1,0:T(8,128)(2,1)} %sv.3, ...), custom_call_target="tpu_custom_call" | custom-call | tf_op jit(solution)/shard_map/pallas_call | solution.py:95
  33.7 0.0 collective-permute-done.1.gk_h.mh_ref
  33.7 0.0 copy-start.3
  33.7 0.0 collective-permute-done.hq.hk.hv
  33.7 0.0 copy-start
  33.7 5.2 %all-to-all-start = ((bf16[16,128,256]{2,1,0:T(8,128)(2,1)}), bf16[16,128,256]{2,1,0:T(8,128)(2,1)S(1)}, u32[]{:S(2)}, u32[]{:S(2)}) async-start(bf16[16,128,256]{2,1,0:T(8,128)(2,1)} %shard_map.104.hi_ref), calls=%async_computation | async-start | bytes 2097152 | tf_op jit(solution)/shard_map/all_to_all | solution.py:245
  38.9 2.0 %collective-permute-start.2 = (bf16[16,128,256]{2,1,0:T(8,128)(2,1)}, bf16[16,128,256]{2,1,0:T(8,128)(2,1)}, u32[]{:S(2)}, u32[]{:S(2)}) collective-permute-start(bf16[16,128,256]{2,1,0:T(8,128)(2,1)} %shard_map.104.hi_ref), channel_id=1, source_target_pairs={{0,1},{1,2},{2,3},{3,4},{4,5},{5,6},{6,7},{7,8},{8,9},{9,10},{10,1... | collective-permute-start | bytes 3145736 | tf_op jit(solution)/shard_map/ppermute | solution.py:14
  41.0 0.1 copy.27
  41.1 0.0 copy-done.5
  41.1 0.1 convert_reduce_fusion.3
  41.2 0.1 convert_reduce_fusion
  41.3 0.6 add_subtract_fusion.dist_ref
  42.0 0.0 copy-done.3
  42.0 0.0 copy-start.4
  42.0 20.9 %shard_map.105.lo_ref = bf16[16,128,256]{2,1,0:T(8,128)(2,1)} custom-call(s32[160,1]{1,0:T(8,128)} %add_subtract_fusion.dist_ref, bf16[256,12288]{1,0:T(8,128)(2,1)} %sv.3, bf16[256,12288]{1,0:T(8,128)(2,1)} %sv.3, bf16[256,12288]{1,0:T(8,128)(2,1)} %sv.3, bf16[18,12288]{1,0:T(8,128)(2,1)} %copy-done, bf16[18,12288]{1,0:T(8,128)(2,1)} %copy-done, ...), custom_call_target="tpu_custom_call" | custom-call | tf_op jit(solution)/shard_map/pallas_call | solution.py:95
  62.9 1.7 %all-to-all-done.hi_ref = bf16[16,128,256]{2,1,0:T(8,128)(2,1)S(1)} async-done(((bf16[16,128,256]{2,1,0:T(8,128)(2,1)}), bf16[16,128,256]{2,1,0:T(8,128)(2,1)S(1)}, u32[]{:S(2)}, u32[]{:S(2)}) %all-to-all-start) | async-done | bytes 1048608 | tf_op jit(solution)/shard_map/all_to_all | solution.py:245
  64.7 4.6 %all-to-all-start.1 = ((bf16[16,128,256]{2,1,0:T(8,128)(2,1)}), bf16[16,128,256]{2,1,0:T(8,128)(2,1)S(1)}, u32[]{:S(2)}, u32[]{:S(2)}) async-start(bf16[16,128,256]{2,1,0:T(8,128)(2,1)} %shard_map.105.lo_ref), calls=%async_computation.1 | async-start | bytes 2097152 | tf_op jit(solution)/shard_map/all_to_all | solution.py:250
  69.3 0.0 copy-done.7
  69.3 0.1 select_reduce_fusion.6
  69.4 0.1 select_reduce_fusion.3
  69.5 0.1 select_reduce_fusion
  69.6 0.2 select_reduce_fusion.4
  69.8 0.6 iota_add_fusion.1.spos_ref
  70.4 0.1 pad.2.clone
  70.5 0.0 copy-done.6
  70.5 0.6 broadcast_in_dim.119.skip_ref
  71.1 0.1 copy.28
  71.2 0.2 rev.3
  71.4 0.8 copy.29.tss_ref
  72.2 0.8 reshape_subtract_fusion.dist_ref
  73.0 0.6 compare_select_fusion
  73.6 0.8 maximum_maximum_fusion.u_ref
  74.4 15.2 %collective-permute-done.2.prev_ref = bf16[16,128,256]{2,1,0:T(8,128)(2,1)} collective-permute-done((bf16[16,128,256]{2,1,0:T(8,128)(2,1)}, bf16[16,128,256]{2,1,0:T(8,128)(2,1)}, u32[]{:S(2)}, u32[]{:S(2)}) %collective-permute-start.2) | collective-permute-done | bytes 1048608 | tf_op jit(solution)/shard_map/ppermute | solution.py:14
  89.7 21.6 %shard_map.106 = bf16[256,4096]{1,0:T(8,128)(2,1)} custom-call(s32[288,1]{1,0:T(8,128)} %reshape_subtract_fusion.dist_ref, s32[256,1]{1,0:T(8,128)} %copy.29.tss_ref, s32[1,384]{1,0:T(1,128)} %iota_add_fusion.1.spos_ref, bf16[256,8192]{1,0:T(8,128)(2,1)} %mg_ref.1, bf16[6,8192]{1,0:T(8,128)(2,1)} %copy-done.3, bf16[7,12288]{1,0:T(8,128)(2,1)} %wq_ref.1, ...), custom_call_target="tpu_custom_call" | custom-call | tf_op jit(solution)/shard_map/pallas_call | solution.py:149
  111.2 0.0 copy-done.1
  111.2 0.0 all-to-all-done.1.lo_ref
  111.2 1.0 copy-done.2
  112.2 5.6 %shard_map.107 = bf16[127,16,256]{2,1,0:T(8,128)(2,1)} custom-call(s32[16]{0:T(128)} %get-tuple-element.21.begin_ref, s32[16]{0:T(128)} %get-tuple-element.20.first_ref, bf16[16,128,256]{2,1,0:T(8,128)(2,1)} %copy-done.2, bf16[16,128,256]{2,1,0:T(8,128)(2,1)} %copy-done.1), custom_call_target="tpu_custom_call" | custom-call | tf_op jit(solution)/shard_map/pallas_call | solution.py:193
  (22 shorter events, 0.1 us)
Async XLA Ops:
  1.6 32.1 %collective-permute-start.1 = (bf16[6,8192]{1,0:T(8,128)(2,1)S(1)}, bf16[6,8192]{1,0:T(8,128)(2,1)S(1)}, u32[]{:S(2)}, u32[]{:S(2)}) collective-permute-start(bf16[6,8192]{1,0:T(8,128)(2,1)S(1)} %slice.7), channel_id=1, source_target_pairs={{0,1},{1,2},{2,3},{3,4},{4,5},{5,6},{6,7},{7,8},{8,9},{9,10},{10,1... | collective-permute-start | bytes 294920 | tf_op jit(solution)/shard_map/ppermute | solution.py:14
  4.7 29.0 %collective-permute-start = (bf16[18,12288]{1,0:T(8,128)(2,1)S(1)}, bf16[18,12288]{1,0:T(8,128)(2,1)S(1)}, u32[]{:S(2)}, u32[]{:S(2)}) collective-permute-start(bf16[18,12288]{1,0:T(8,128)(2,1)S(1)} %slice.6), channel_id=1, source_target_pairs={{0,1},{1,2},{2,3},{3,4},{4,5},{5,6},{6,7},{7,8},{8,9},{9,10},{10,1... | collective-permute-start | bytes 1327112 | tf_op jit(solution)/shard_map/ppermute | solution.py:14
  12.8 28.4 %copy-start.5 = (s32[16]{0:T(128)S(1)}, s32[16]{0:T(128)}, u32[]{:S(2)}) copy-start(s32[16]{0:T(128)} %param.16) | copy-start | bytes 196
  33.7 8.3 %copy-start.3 = (bf16[6,8192]{1,0:T(8,128)(2,1)}, bf16[6,8192]{1,0:T(8,128)(2,1)S(1)}, u32[]{:S(2)}) copy-start(bf16[6,8192]{1,0:T(8,128)(2,1)S(1)} %collective-permute-done.1.gk_h.mh_ref) | copy-start | bytes 294916
  33.7 8.3 %copy-start = (bf16[18,12288]{1,0:T(8,128)(2,1)}, bf16[18,12288]{1,0:T(8,128)(2,1)S(1)}, u32[]{:S(2)}) copy-start(bf16[18,12288]{1,0:T(8,128)(2,1)S(1)} %collective-permute-done.hq.hk.hv) | copy-start | bytes 1327108
  33.7 31.0 %all-to-all-start = ((bf16[16,128,256]{2,1,0:T(8,128)(2,1)}), bf16[16,128,256]{2,1,0:T(8,128)(2,1)S(1)}, u32[]{:S(2)}, u32[]{:S(2)}) async-start(bf16[16,128,256]{2,1,0:T(8,128)(2,1)} %shard_map.104.hi_ref), calls=%async_computation | async-start | bytes 2097152 | tf_op jit(solution)/shard_map/all_to_all | solution.py:245
  38.9 50.7 %collective-permute-start.2 = (bf16[16,128,256]{2,1,0:T(8,128)(2,1)}, bf16[16,128,256]{2,1,0:T(8,128)(2,1)}, u32[]{:S(2)}, u32[]{:S(2)}) collective-permute-start(bf16[16,128,256]{2,1,0:T(8,128)(2,1)} %shard_map.104.hi_ref), channel_id=1, source_target_pairs={{0,1},{1,2},{2,3},{3,4},{4,5},{5,6},{6,7},{7,8},{8,9},{9,10},{10,1... | collective-permute-start | bytes 3145736 | tf_op jit(solution)/shard_map/ppermute | solution.py:14
  42.0 27.3 %copy-start.7 = (s32[16]{0:T(128)S(1)}, s32[16]{0:T(128)}, u32[]{:S(2)}) copy-start(s32[16]{0:T(128)} %param.17) | copy-start | bytes 196
  42.0 28.5 %copy-start.6 = (bf16[4096]{0:T(1024)(128)(2,1)S(1)}, bf16[4096]{0:T(1024)(128)(2,1)}, u32[]{:S(2)}) copy-start(bf16[4096]{0:T(1024)(128)(2,1)} %param.15) | copy-start | bytes 24580
  42.0 29.1 %copy-start.4 = (bf16[128,256]{1,0:T(8,128)(2,1)S(1)}, bf16[128,256]{1,0:T(8,128)(2,1)}, u32[]{:S(2)}) copy-start(bf16[128,256]{1,0:T(8,128)(2,1)} %param.14) | copy-start | bytes 196612
  64.7 46.5 %copy-start.1 = (bf16[16,128,256]{2,1,0:T(8,128)(2,1)}, bf16[16,128,256]{2,1,0:T(8,128)(2,1)S(1)}, u32[]{:S(2)}) copy-start(bf16[16,128,256]{2,1,0:T(8,128)(2,1)S(1)} %all-to-all-done.hi_ref) | copy-start | bytes 3145732
  64.7 46.5 %all-to-all-start.1 = ((bf16[16,128,256]{2,1,0:T(8,128)(2,1)}), bf16[16,128,256]{2,1,0:T(8,128)(2,1)S(1)}, u32[]{:S(2)}, u32[]{:S(2)}) async-start(bf16[16,128,256]{2,1,0:T(8,128)(2,1)} %shard_map.105.lo_ref), calls=%async_computation.1 | async-start | bytes 2097152 | tf_op jit(solution)/shard_map/all_to_all | solution.py:250
  111.2 1.0 copy-start.2

commit v7 on v5

--- a/solution.py
+++ b/solution.py
@@ -1,3 +1,5 @@
+import functools
+
 import jax
 import jax.numpy as jnp
 from jax import lax
@@ -49,9 +51,13 @@
     return acc
 
 
-def chain_kernel(dist_ref, sq, sk, sv, hq, hk, hv, mk, gk_h, fq, fk, fv, filt, wk, wv,
-                 z2_ref, xq, xk, xv, xb, zs, ys):
-    rows = xq.shape[0]
+def chain_kernel(dist_ref, sq, sk, sv, hq, hk, hv, mk, gk_h, fq, fk, fv, filt_ref, wk, wv,
+                 z2_ref, xq, xk, xv, xb, zs, ys, group_ch):
+    rows, tile = xq.shape
+    filters = filt_ref.shape[1]
+    lane_ch = pl.program_id(0) * tile + lax.broadcasted_iota(jnp.int32, (filters, tile), 1)
+    spread = (lane_ch // group_ch == lax.broadcasted_iota(jnp.int32, (filters, tile), 0))
+    filt = jnp.dot(filt_ref[...], spread.astype(filt_ref.dtype), preferred_element_type=jnp.float32)
     for main, halo, x in ((sq, hq, xq), (sk, hk, xk), (sv, hv, xv), (mk, gk_h, xb)):
         reach = halo.shape[0]
         if reach < HALO:
@@ -93,10 +99,11 @@
     halo = [halo_spec(se_halo, p) for p in range(3)]
     wts = [pl.BlockSpec((taps, TILE), col(p, 0)) for p in range(3)]
     return pl.pallas_call(
-        chain_kernel,
+        functools.partial(chain_kernel, group_ch=channels // se_filt.shape[1]),
         grid=(steps,),
         in_specs=[pl.BlockSpec((rows, 1), lambda j: (0, 0))] + main + halo
-        + [main[1], halo_spec(mr_halo, 1)] + wts + [wts[0], wts[1], wts[2]],
+        + [main[1], halo_spec(mr_halo, 1)] + wts
+        + [pl.BlockSpec(se_filt.shape, lambda j: (0, 0)), wts[1], wts[2]],
         out_specs=pl.BlockSpec((TILE // chunk, tok_rows, chunk), lambda j: (j, 0, 0)),
         out_shape=jax.ShapeDtypeStruct((shards, tok_rows, chunk), jnp.bfloat16),
         scratch_shapes=[pltpu.VMEM((rows, TILE), jnp.float32) for _ in range(6)],
@@ -230,7 +237,7 @@
         (se_streams[tok_rows - 3 * reach_rows :], mr_gates[tok_rows - reach_rows :]), "seq", 1
     )
     blk = tok_rows // 2
-    se_filt = jnp.repeat(se_filter, group_ch, axis=1)
+    se_filt = se_filter
 
     def dist_of(half):
         ext_pos = offset + half * blk - HALO + jnp.arange(blk + HALO, dtype=jnp.int32)

time: 118 us -> 116 us (0.983)
  local copies, waits for them, and re-layouts: 7.4 us -> 5.24 us
    reshape x1 -> x0, local copies, waits for them, and re-layouts: 1.22 us -> none  [local(): se_filt = jnp.repeat(se_filter, group_ch, axis=1)]
  transfers between devices with their start and end apart: 5 -> 5, of which waited for: 2 -> 2; matrix products, arithmetic and copies ran while one was open for 10% -> 8% of each run, Pallas kernels for 53% -> 54%
where the time goes in v7:
time: 116 us
  Pallas kernels  68.4 us (59%)
  waiting for transfers between devices  18 us (16%)
  starting transfers between devices  17 us (15%)
  other arithmetic  6.28 us (5%)
  local copies, waits for them, and re-layouts  5.24 us (5%)
    pallas_call x2, Pallas kernels, short_chain(): pl.pallas_call(functools.partial(chain_kernel, group_ch=channels // se_fi...  41.2 us
    pallas_call x1, Pallas kernels, long_conv_out(): pl.pallas_call(long_kernel, grid=(steps,), in_specs=[pl.BlockSpec(dist.sh...  21.6 us
    ppermute x3, waiting for transfers between devices, passed_along(): return lax.ppermute(x, axis, pairs)  16 us
    ppermute x3, starting transfers between devices, passed_along(): return lax.ppermute(x, axis, pairs)  7.5 us
    pallas_call x1, Pallas kernels, cut_tails_all(): pl.pallas_call(tail_kernel, in_specs=[smem, smem, vmem, vmem], out_specs=...  5.65 us
    all_to_all x1, starting transfers between devices, local(): lax.all_to_all(z_hi, 'seq', split_axis=0, concat_axis=0, tiled=True)  5.24 us
    all_to_all x1, starting transfers between devices, local(): lax.all_to_all(z_lo, 'seq', split_axis=0, concat_axis=0, tiled=True)  4.22 us
  transfers between devices with their start and end apart: 5, of which 2 were waited for; matrix products, arithmetic and copies ran while one was open for 8% of the time, Pallas kernels for 54%

profile of v7, /device:TPU:18, one launch (start us, length us, event | category | flops | bytes accessed | tf_op | source)
XLA Modules:
  0.0 115.8 jit_solution(1218267459407949422)
XLA Ops:
  0.6 0.9 slice.7
  1.6 1.9 %collective-permute-start.1 = (bf16[6,8192]{1,0:T(8,128)(2,1)S(1)}, bf16[6,8192]{1,0:T(8,128)(2,1)S(1)}, u32[]{:S(2)}, u32[]{:S(2)}) collective-permute-start(bf16[6,8192]{1,0:T(8,128)(2,1)S(1)} %slice.7), channel_id=1, source_target_pairs={{0,1},{1,2},{2,3},{3,4},{4,5},{5,6},{6,7},{7,8},{8,9},{9,10},{10,1... | collective-permute-start | bytes 294920 | tf_op jit(solution)/shard_map/ppermute | solution.py:16
  3.5 1.2 %slice.6 = bf16[18,12288]{1,0:T(8,128)(2,1)S(1)} slice(bf16[256,12288]{1,0:T(8,128)(2,1)} %sv.3), slice={[238:256], [0:12288]} | slice | bytes 884736 | tf_op jit(solution)/shard_map/slice | solution.py:237
  4.7 3.5 %collective-permute-start = (bf16[18,12288]{1,0:T(8,128)(2,1)S(1)}, bf16[18,12288]{1,0:T(8,128)(2,1)S(1)}, u32[]{:S(2)}, u32[]{:S(2)}) collective-permute-start(bf16[18,12288]{1,0:T(8,128)(2,1)S(1)} %slice.6), channel_id=1, source_target_pairs={{0,1},{1,2},{2,3},{3,4},{4,5},{5,6},{6,7},{7,8},{8,9},{9,10},{10,1... | collective-permute-start | bytes 1327112 | tf_op jit(solution)/shard_map/ppermute | solution.py:16
  8.3 0.7 convert_reduce_fusion.1
  9.0 0.7 select_reduce_fusion.1
  9.8 0.1 copy.25
  9.9 0.7 add_subtract_fusion.1.dist_ref
  10.6 20.5 %shard_map.104.hi_ref = bf16[16,128,256]{2,1,0:T(8,128)(2,1)} custom-call(s32[160,1]{1,0:T(8,128)} %add_subtract_fusion.1.dist_ref, bf16[256,12288]{1,0:T(8,128)(2,1)} %sv.3, bf16[256,12288]{1,0:T(8,128)(2,1)} %sv.3, bf16[256,12288]{1,0:T(8,128)(2,1)} %sv.3, bf16[256,12288]{1,0:T(8,128)(2,1)} %sv.3, bf16[256,12288]{1,0:T(8,128)(2,1)} %sv.3, ...), custom_call_target="tpu_custom_call" | custom-call | tf_op jit(solution)/shard_map/pallas_call | solution.py:101
  31.1 0.0 collective-permute-done.1.gk_h.mh_ref
  31.1 0.0 copy-start.3
  31.1 0.0 collective-permute-done.hq.hk.hv
  31.2 0.0 copy-start
  31.2 5.2 %all-to-all-start = ((bf16[16,128,256]{2,1,0:T(8,128)(2,1)}), bf16[16,128,256]{2,1,0:T(8,128)(2,1)S(1)}, u32[]{:S(2)}, u32[]{:S(2)}) async-start(bf16[16,128,256]{2,1,0:T(8,128)(2,1)} %shard_map.104.hi_ref), calls=%async_computation | async-start | bytes 2097152 | tf_op jit(solution)/shard_map/all_to_all | solution.py:252
  36.4 2.0 %collective-permute-start.2 = (bf16[16,128,256]{2,1,0:T(8,128)(2,1)}, bf16[16,128,256]{2,1,0:T(8,128)(2,1)}, u32[]{:S(2)}, u32[]{:S(2)}) collective-permute-start(bf16[16,128,256]{2,1,0:T(8,128)(2,1)} %shard_map.104.hi_ref), channel_id=1, source_target_pairs={{0,1},{1,2},{2,3},{3,4},{4,5},{5,6},{6,7},{7,8},{8,9},{9,10},{10,1... | collective-permute-start | bytes 3145736 | tf_op jit(solution)/shard_map/ppermute | solution.py:16
  38.5 0.1 copy.27
  38.6 0.0 copy-done.5
  38.6 0.1 convert_reduce_fusion.3
  38.7 0.1 convert_reduce_fusion
  38.8 0.6 add_subtract_fusion.dist_ref
  39.5 0.0 copy-done.3
  39.5 0.0 copy-done
  39.5 0.0 copy-start.4
  39.5 20.7 %shard_map.105.lo_ref = bf16[16,128,256]{2,1,0:T(8,128)(2,1)} custom-call(s32[160,1]{1,0:T(8,128)} %add_subtract_fusion.dist_ref, bf16[256,12288]{1,0:T(8,128)(2,1)} %sv.3, bf16[256,12288]{1,0:T(8,128)(2,1)} %sv.3, bf16[256,12288]{1,0:T(8,128)(2,1)} %sv.3, bf16[18,12288]{1,0:T(8,128)(2,1)} %copy-done, bf16[18,12288]{1,0:T(8,128)(2,1)} %copy-done, ...), custom_call_target="tpu_custom_call" | custom-call | tf_op jit(solution)/shard_map/pallas_call | solution.py:101
  60.2 2.0 %all-to-all-done.hi_ref = bf16[16,128,256]{2,1,0:T(8,128)(2,1)S(1)} async-done(((bf16[16,128,256]{2,1,0:T(8,128)(2,1)}), bf16[16,128,256]{2,1,0:T(8,128)(2,1)S(1)}, u32[]{:S(2)}, u32[]{:S(2)}) %all-to-all-start) | async-done | bytes 1048608 | tf_op jit(solution)/shard_map/all_to_all | solution.py:252
  62.1 4.2 %all-to-all-start.1 = ((bf16[16,128,256]{2,1,0:T(8,128)(2,1)}), bf16[16,128,256]{2,1,0:T(8,128)(2,1)S(1)}, u32[]{:S(2)}, u32[]{:S(2)}) async-start(bf16[16,128,256]{2,1,0:T(8,128)(2,1)} %shard_map.105.lo_ref), calls=%async_computation.1 | async-start | bytes 2097152 | tf_op jit(solution)/shard_map/all_to_all | solution.py:257
  66.4 0.0 copy-done.7
  66.4 0.1 select_reduce_fusion.6
  66.5 0.1 select_reduce_fusion.3
  66.6 0.1 select_reduce_fusion
  66.7 0.2 select_reduce_fusion.4
  66.9 0.6 iota_add_fusion.1.spos_ref
  67.4 0.1 pad.2.clone
  67.5 0.0 copy-done.6
  67.5 0.6 broadcast_in_dim.115.skip_ref
  68.1 0.0 copy-done.4
  68.1 0.1 copy.28
  68.3 0.2 rev.3
  68.5 0.8 copy.29.tss_ref
  69.3 0.8 reshape_subtract_fusion.dist_ref
  70.1 0.6 compare_select_fusion
  70.7 0.8 maximum_maximum_fusion.u_ref
  71.5 16.0 %collective-permute-done.2.prev_ref = bf16[16,128,256]{2,1,0:T(8,128)(2,1)} collective-permute-done((bf16[16,128,256]{2,1,0:T(8,128)(2,1)}, bf16[16,128,256]{2,1,0:T(8,128)(2,1)}, u32[]{:S(2)}, u32[]{:S(2)}) %collective-permute-start.2) | collective-permute-done | bytes 1048608 | tf_op jit(solution)/shard_map/ppermute | solution.py:16
  87.5 21.6 %shard_map.106 = bf16[256,4096]{1,0:T(8,128)(2,1)} custom-call(s32[288,1]{1,0:T(8,128)} %reshape_subtract_fusion.dist_ref, s32[256,1]{1,0:T(8,128)} %copy.29.tss_ref, s32[1,384]{1,0:T(1,128)} %iota_add_fusion.1.spos_ref, bf16[256,8192]{1,0:T(8,128)(2,1)} %mg_ref.1, bf16[6,8192]{1,0:T(8,128)(2,1)} %copy-done.3, bf16[7,12288]{1,0:T(8,128)(2,1)} %wq_ref.1, ...), custom_call_target="tpu_custom_call" | custom-call | tf_op jit(solution)/shard_map/pallas_call | solution.py:156
  109.1 0.0 copy-done.1
  109.1 0.0 all-to-all-done.1.lo_ref
  109.1 1.0 copy-done.2
  110.1 5.6 %shard_map.107 = bf16[127,16,256]{2,1,0:T(8,128)(2,1)} custom-call(s32[16]{0:T(128)} %get-tuple-element.21.begin_ref, s32[16]{0:T(128)} %get-tuple-element.20.first_ref, bf16[16,128,256]{2,1,0:T(8,128)(2,1)} %copy-done.2, bf16[16,128,256]{2,1,0:T(8,128)(2,1)} %copy-done.1), custom_call_target="tpu_custom_call" | custom-call | tf_op jit(solution)/shard_map/pallas_call | solution.py:200
  (20 shorter events, 0.1 us)
Async XLA Ops:
  1.6 29.6 %collective-permute-start.1 = (bf16[6,8192]{1,0:T(8,128)(2,1)S(1)}, bf16[6,8192]{1,0:T(8,128)(2,1)S(1)}, u32[]{:S(2)}, u32[]{:S(2)}) collective-permute-start(bf16[6,8192]{1,0:T(8,128)(2,1)S(1)} %slice.7), channel_id=1, source_target_pairs={{0,1},{1,2},{2,3},{3,4},{4,5},{5,6},{6,7},{7,8},{8,9},{9,10},{10,1... | collective-permute-start | bytes 294920 | tf_op jit(solution)/shard_map/ppermute | solution.py:16
  4.7 26.4 %collective-permute-start = (bf16[18,12288]{1,0:T(8,128)(2,1)S(1)}, bf16[18,12288]{1,0:T(8,128)(2,1)S(1)}, u32[]{:S(2)}, u32[]{:S(2)}) collective-permute-start(bf16[18,12288]{1,0:T(8,128)(2,1)S(1)} %slice.6), channel_id=1, source_target_pairs={{0,1},{1,2},{2,3},{3,4},{4,5},{5,6},{6,7},{7,8},{8,9},{9,10},{10,1... | collective-permute-start | bytes 1327112 | tf_op jit(solution)/shard_map/ppermute | solution.py:16
  10.6 28.0 %copy-start.5 = (s32[16]{0:T(128)S(1)}, s32[16]{0:T(128)}, u32[]{:S(2)}) copy-start(s32[16]{0:T(128)} %param.16) | copy-start | bytes 196
  31.1 8.3 %copy-start.3 = (bf16[6,8192]{1,0:T(8,128)(2,1)}, bf16[6,8192]{1,0:T(8,128)(2,1)S(1)}, u32[]{:S(2)}) copy-start(bf16[6,8192]{1,0:T(8,128)(2,1)S(1)} %collective-permute-done.1.gk_h.mh_ref) | copy-start | bytes 294916
  31.2 8.3 %copy-start = (bf16[18,12288]{1,0:T(8,128)(2,1)}, bf16[18,12288]{1,0:T(8,128)(2,1)S(1)}, u32[]{:S(2)}) copy-start(bf16[18,12288]{1,0:T(8,128)(2,1)S(1)} %collective-permute-done.hq.hk.hv) | copy-start | bytes 1327108
  31.2 31.0 %all-to-all-start = ((bf16[16,128,256]{2,1,0:T(8,128)(2,1)}), bf16[16,128,256]{2,1,0:T(8,128)(2,1)S(1)}, u32[]{:S(2)}, u32[]{:S(2)}) async-start(bf16[16,128,256]{2,1,0:T(8,128)(2,1)} %shard_map.104.hi_ref), calls=%async_computation | async-start | bytes 2097152 | tf_op jit(solution)/shard_map/all_to_all | solution.py:252
  36.4 51.1 %collective-permute-start.2 = (bf16[16,128,256]{2,1,0:T(8,128)(2,1)}, bf16[16,128,256]{2,1,0:T(8,128)(2,1)}, u32[]{:S(2)}, u32[]{:S(2)}) collective-permute-start(bf16[16,128,256]{2,1,0:T(8,128)(2,1)} %shard_map.104.hi_ref), channel_id=1, source_target_pairs={{0,1},{1,2},{2,3},{3,4},{4,5},{5,6},{6,7},{7,8},{8,9},{9,10},{10,1... | collective-permute-start | bytes 3145736 | tf_op jit(solution)/shard_map/ppermute | solution.py:16
  39.5 26.9 %copy-start.7 = (s32[16]{0:T(128)S(1)}, s32[16]{0:T(128)}, u32[]{:S(2)}) copy-start(s32[16]{0:T(128)} %param.17) | copy-start | bytes 196
  39.5 28.1 %copy-start.6 = (bf16[4096]{0:T(1024)(128)(2,1)S(1)}, bf16[4096]{0:T(1024)(128)(2,1)}, u32[]{:S(2)}) copy-start(bf16[4096]{0:T(1024)(128)(2,1)} %param.15) | copy-start | bytes 24580
  39.5 28.7 %copy-start.4 = (bf16[128,256]{1,0:T(8,128)(2,1)S(1)}, bf16[128,256]{1,0:T(8,128)(2,1)}, u32[]{:S(2)}) copy-start(bf16[128,256]{1,0:T(8,128)(2,1)} %param.14) | copy-start | bytes 196612
  62.1 46.9 %copy-start.1 = (bf16[16,128,256]{2,1,0:T(8,128)(2,1)}, bf16[16,128,256]{2,1,0:T(8,128)(2,1)S(1)}, u32[]{:S(2)}) copy-start(bf16[16,128,256]{2,1,0:T(8,128)(2,1)S(1)} %all-to-all-done.hi_ref) | copy-start | bytes 3145732
  62.1 46.9 %all-to-all-start.1 = ((bf16[16,128,256]{2,1,0:T(8,128)(2,1)}), bf16[16,128,256]{2,1,0:T(8,128)(2,1)S(1)}, u32[]{:S(2)}, u32[]{:S(2)}) async-start(bf16[16,128,256]{2,1,0:T(8,128)(2,1)} %shard_map.105.lo_ref), calls=%async_computation.1 | async-start | bytes 2097152 | tf_op jit(solution)/shard_map/all_to_all | solution.py:257
  109.1 1.0 copy-start.2

commit v8 on v7

--- a/solution.py
+++ b/solution.py
@@ -41,9 +41,9 @@
 WINDOW = 144
 
 
-def short_conv_rows(x, w, first, dist_ref):
+def short_conv_rows(x, w, first, dist_all):
     rows = x.shape[0]
-    dist = dist_ref[first:rows, :]
+    dist = dist_all[first:rows, :]
     acc = x[first:rows, :] * w[0:1, :].astype(jnp.float32)
     for lag in range(1, w.shape[0]):
         term = x[first - lag : rows - lag, :] * w[lag : lag + 1, :].astype(jnp.float32)
@@ -51,9 +51,15 @@
     return acc
 
 
-def chain_kernel(dist_ref, sq, sk, sv, hq, hk, hv, mk, gk_h, fq, fk, fv, filt_ref, wk, wv,
-                 z2_ref, xq, xk, xv, xb, zs, ys, group_ch):
+def rel_dist(rel_ref, base, count):
+    index = base + lax.broadcasted_iota(jnp.int32, (count, 1), 0)
+    return index - rel_ref[base : base + count, :]
+
+
+def chain_kernel(rel_ref, sq, sk, sv, hq, hk, hv, mk, gk_h, fq, fk, fv, filt_ref, wk, wv,
+                 z2_ref, xq, xk, xv, xb, zs, ys, group_ch, base):
     rows, tile = xq.shape
+    dist_ref = rel_dist(rel_ref, base, rows)
     filters = filt_ref.shape[1]
     lane_ch = pl.program_id(0) * tile + lax.broadcasted_iota(jnp.int32, (filters, tile), 1)
     spread = (lane_ch // group_ch == lax.broadcasted_iota(jnp.int32, (filters, tile), 0))
@@ -79,8 +85,8 @@
         z2_ref[i] = z2[:, i * chunk : (i + 1) * chunk]
 
 
-def short_chain(dist, se_streams, se_halo, mr_gates, mr_halo, se_feat, se_filt, mr_feat, shards, half):
-    tok_rows = dist.shape[0] - HALO
+def short_chain(rel, se_streams, se_halo, mr_gates, mr_halo, se_feat, se_filt, mr_feat, shards, half):
+    tok_rows = se_streams.shape[0] // 2
     channels = mr_gates.shape[1] // 2
     steps = channels // TILE
     rows = tok_rows + HALO
@@ -99,25 +105,28 @@
     halo = [halo_spec(se_halo, p) for p in range(3)]
     wts = [pl.BlockSpec((taps, TILE), col(p, 0)) for p in range(3)]
     return pl.pallas_call(
-        functools.partial(chain_kernel, group_ch=channels // se_filt.shape[1]),
+        functools.partial(
+            chain_kernel, group_ch=channels // se_filt.shape[1], base=half * tok_rows + tok_rows - HALO
+        ),
         grid=(steps,),
-        in_specs=[pl.BlockSpec((rows, 1), lambda j: (0, 0))] + main + halo
+        in_specs=[pl.BlockSpec(rel.shape, lambda j: (0, 0))] + main + halo
         + [main[1], halo_spec(mr_halo, 1)] + wts
         + [pl.BlockSpec(se_filt.shape, lambda j: (0, 0)), wts[1], wts[2]],
         out_specs=pl.BlockSpec((TILE // chunk, tok_rows, chunk), lambda j: (j, 0, 0)),
         out_shape=jax.ShapeDtypeStruct((shards, tok_rows, chunk), jnp.bfloat16),
         scratch_shapes=[pltpu.VMEM((rows, TILE), jnp.float32) for _ in range(6)],
-    )(dist, se_streams, se_streams, se_streams, se_halo, se_halo, se_halo, mr_gates,
+    )(rel, se_streams, se_streams, se_streams, se_halo, se_halo, se_halo, mr_gates,
       mr_halo, se_feat, se_feat, se_feat, se_filt, mr_feat, mr_feat)
 
 
-def long_kernel(dist_ref, tss_ref, spos_ref, mg_ref, mh_ref, wq_ref, prev_ref, lo_ref, hi_ref, skip_ref,
+def long_kernel(rel_ref, mg_ref, mh_ref, wq_ref, prev_ref, lo_ref, hi_ref, skip_ref,
                 u_ref, out_ref, xa):
     rows = xa.shape[0]
     reach = mh_ref.shape[0]
     xa[HALO - reach : HALO, :] = mh_ref[...].astype(jnp.float32)
     xa[HALO:rows, :] = mg_ref[...].astype(jnp.float32)
-    q2 = short_conv_rows(xa, wq_ref, HALO, dist_ref)
+    blk = lo_ref.shape[1]
+    q2 = short_conv_rows(xa, wq_ref, HALO, rel_dist(rel_ref, blk - HALO, rows))
     blk = lo_ref.shape[1]
     tile = lo_ref.shape[2]
     width = u_ref.shape[1]
@@ -126,7 +135,8 @@
     hi = hi_ref[0]
     windows = (jnp.concatenate([prev_ref[0], lo], axis=0), jnp.concatenate([lo, hi], axis=0))
     masks = [
-        spos_ref[:, b * blk : b * blk + width] >= tss_ref[b * blk : (b + 1) * blk, :] for b in range(2)
+        lax.broadcasted_iota(jnp.int32, (1, width), 1) + b * blk >= rel_ref[(b + 1) * blk : (b + 2) * blk, :]
+        for b in range(2)
     ]
     lane_grp = lax.broadcasted_iota(jnp.int32, (1, GROUP_LANES), 1) // per_group
     halves = tile // GROUP_LANES
@@ -147,7 +157,7 @@
     out_ref[...] = (q2 * mixed.astype(jnp.float32)).astype(jnp.bfloat16)
 
 
-def long_conv_out(dist, tss, spos, mr_gates, mr_halo, mr_feat, prev_z, z_lo, z_hi, skip, taps_rows):
+def long_conv_out(rel, mr_gates, mr_halo, mr_feat, prev_z, z_lo, z_hi, skip, taps_rows):
     steps, blk, lanes = z_lo.shape
     tok_rows = 2 * blk
     channels = steps * lanes
@@ -157,9 +167,7 @@
         long_kernel,
         grid=(steps,),
         in_specs=[
-            pl.BlockSpec(dist.shape, lambda j: (0, 0)),
-            pl.BlockSpec(tss.shape, lambda j: (0, 0)),
-            pl.BlockSpec(spos.shape, lambda j: (0, 0)),
+            pl.BlockSpec(rel.shape, lambda j: (0, 0)),
             pl.BlockSpec((tok_rows, lanes), lambda j: (0, j)),
             pl.BlockSpec((mr_halo.shape[0], lanes), lambda j: (0, j)),
             pl.BlockSpec((mr_feat.shape[0], lanes), lambda j: (0, j)),
@@ -172,7 +180,7 @@
         out_specs=pl.BlockSpec((tok_rows, lanes), lambda j: (0, j)),
         out_shape=jax.ShapeDtypeStruct((tok_rows, channels), jnp.bfloat16),
         scratch_shapes=[pltpu.VMEM((tok_rows + HALO, lanes), jnp.float32)],
-    )(dist, tss, spos, mr_gates, mr_halo, mr_feat, prev_z, z_lo, z_hi, skip, taps_rows)
+    )(rel, mr_gates, mr_halo, mr_feat, prev_z, z_lo, z_hi, skip, taps_rows)
 
 
 def tail_kernel(begin_ref, first_ref, lo_ref, hi_ref, out_ref, z_all):
@@ -239,19 +247,16 @@
     blk = tok_rows // 2
     se_filt = se_filter
 
-    def dist_of(half):
-        ext_pos = offset + half * blk - HALO + jnp.arange(blk + HALO, dtype=jnp.int32)
-        return (ext_pos - seg_start(ext_pos, req_ends))[:, None]
-
-    dists = [dist_of(0), dist_of(1)]
+    window_pos = offset - blk + jnp.arange(tok_rows + blk, dtype=jnp.int32)
+    rel = (seg_start(window_pos, req_ends) - (offset - blk))[:, None]
     z_hi = short_chain(
-        dists[1], se_streams, se_streams, mr_gates, mr_gates, se_feat, se_filt, mr_feat, shards, 1
+        rel, se_streams, se_streams, mr_gates, mr_gates, se_feat, se_filt, mr_feat, shards, 1
     )
     prev_z = passed_along(z_hi, "seq", 1)
     z_hi, prev_se, prev_mr = lax.optimization_barrier((z_hi, prev_se, prev_mr))
     recv_hi = lax.all_to_all(z_hi, "seq", split_axis=0, concat_axis=0, tiled=True)
     z_lo = short_chain(
-        dists[0], se_streams, prev_se, mr_gates, prev_mr, se_feat, se_filt, mr_feat, shards, 0
+        rel, se_streams, prev_se, mr_gates, prev_mr, se_feat, se_filt, mr_feat, shards, 0
     )
     z_lo, recv_hi = lax.optimization_barrier((z_lo, recv_hi))
     recv_lo = lax.all_to_all(z_lo, "seq", split_axis=0, concat_axis=0, tiled=True)
@@ -262,13 +267,8 @@
         axis=1,
     )
 
-    tgt_pos = offset + jnp.arange(tok_rows, dtype=jnp.int32)
-    tss = seg_start(tgt_pos, req_ends)[:, None]
-    spos = (offset - blk + jnp.arange(tok_rows + blk, dtype=jnp.int32))[None, :]
-    ext_pos = offset - HALO + jnp.arange(tok_rows + HALO, dtype=jnp.int32)
-    dist = (ext_pos - seg_start(ext_pos, req_ends))[:, None]
     hyena_out = long_conv_out(
-        dist, tss, spos, mr_gates, prev_mr, mr_feat, prev_z, z_lo, z_hi, mr_skip[None, :], taps_rows
+        rel, mr_gates, prev_mr, mr_feat, prev_z, z_lo, z_hi, mr_skip[None, :], taps_rows
     )
     rows_ids = jnp.arange(total_req, dtype=jnp.int32)
     owner = jnp.sum(

time: 116 us -> 132 us (1.14)
  waiting for transfers between devices: 18 us -> 35.3 us
  other arithmetic: 6.28 us -> 3.26 us
  Pallas kernels: 68.4 us -> 70.3 us
    ppermute x3, waiting for transfers between devices: 16 us -> 31.7 us  [passed_along(): return lax.ppermute(x, axis, pairs)]
    sub x3 -> x1, other arithmetic: 2.07 us -> 0.01 us  [local(): rel = (seg_start(window_pos, req_ends) - (offset - blk))[:, None]]
    pallas_call x2, Pallas kernels: 41.2 us -> 42.9 us  [short_chain(): pl.pallas_call(functools.partial(chain_kernel, group_ch=channels // se_fi...]
    all_to_all x1, waiting for transfers between devices: 1.97 us -> 3.63 us  [local(): lax.all_to_all(z_hi, 'seq', split_axis=0, concat_axis=0, tiled=True)]
  transfers between devices with their start and end apart: 5 -> 5, of which waited for: 2 -> 2; matrix products, arithmetic and copies ran while one was open for 8% -> 5% of each run, Pallas kernels for 54% -> 49%
where the time goes in v8:
time: 132 us; the launch traced here: 131 us
  Pallas kernels  70.3 us (53%)
  waiting for transfers between devices  35.3 us (27%)
  starting transfers between devices  17.4 us (13%)
  local copies, waits for them, and re-layouts  4.01 us (3%)
  other arithmetic  3.26 us (2%)
    pallas_call x2, Pallas kernels, short_chain(): pl.pallas_call(functools.partial(chain_kernel, group_ch=channels // se_fi...  42.9 us
    ppermute x3, waiting for transfers between devices, passed_along(): return lax.ppermute(x, axis, pairs)  31.7 us
    pallas_call x1, Pallas kernels, long_conv_out(): pl.pallas_call(long_kernel, grid=(steps,), in_specs=[pl.BlockSpec(rel.sha...  21.7 us
    ppermute x3, starting transfers between devices, passed_along(): return lax.ppermute(x, axis, pairs)  7.51 us
    pallas_call x1, Pallas kernels, cut_tails_all(): pl.pallas_call(tail_kernel, in_specs=[smem, smem, vmem, vmem], out_specs=...  5.65 us
    all_to_all x1, starting transfers between devices, local(): lax.all_to_all(z_hi, 'seq', split_axis=0, concat_axis=0, tiled=True)  5.24 us
    all_to_all x1, starting transfers between devices, local(): lax.all_to_all(z_lo, 'seq', split_axis=0, concat_axis=0, tiled=True)  4.64 us
    all_to_all x1, waiting for transfers between devices, local(): lax.all_to_all(z_hi, 'seq', split_axis=0, concat_axis=0, tiled=True)  3.63 us
  transfers between devices with their start and end apart: 5, of which 2 were waited for; matrix products, arithmetic and copies ran while one was open for 5% of the time, Pallas kernels for 49%

profile of v8, /device:TPU:18, one launch (start us, length us, event | category | flops | bytes accessed | tf_op | source)
XLA Modules:
  0.0 131.1 jit_solution(13352672212635116149)
XLA Ops:
  0.6 0.9 slice.7
  1.6 1.9 %collective-permute-start.1 = (bf16[6,8192]{1,0:T(8,128)(2,1)S(1)}, bf16[6,8192]{1,0:T(8,128)(2,1)S(1)}, u32[]{:S(2)}, u32[]{:S(2)}) collective-permute-start(bf16[6,8192]{1,0:T(8,128)(2,1)S(1)} %slice.7), channel_id=1, source_target_pairs={{0,1},{1,2},{2,3},{3,4},{4,5},{5,6},{6,7},{7,8},{8,9},{9,10},{10,1... | collective-permute-start | bytes 294920 | tf_op jit(solution)/shard_map/ppermute | solution.py:16
  3.5 1.2 slice.6
  4.7 3.5 %collective-permute-start = (bf16[18,12288]{1,0:T(8,128)(2,1)S(1)}, bf16[18,12288]{1,0:T(8,128)(2,1)S(1)}, u32[]{:S(2)}, u32[]{:S(2)}) collective-permute-start(bf16[18,12288]{1,0:T(8,128)(2,1)S(1)} %slice.6), channel_id=1, source_target_pairs={{0,1},{1,2},{2,3},{3,4},{4,5},{5,6},{6,7},{7,8},{8,9},{9,10},{10,1... | collective-permute-start | bytes 1327112 | tf_op jit(solution)/shard_map/ppermute | solution.py:16
  8.3 0.7 convert_reduce_fusion
  9.0 0.7 select_reduce_fusion
  9.8 0.8 sub.30.rel_ref
  10.6 21.4 %shard_map.104.hi_ref = bf16[16,128,256]{2,1,0:T(8,128)(2,1)} custom-call(s32[384,1]{1,0:T(8,128)} %sub.30.rel_ref, bf16[256,12288]{1,0:T(8,128)(2,1)} %sv.3, bf16[256,12288]{1,0:T(8,128)(2,1)} %sv.3, bf16[256,12288]{1,0:T(8,128)(2,1)} %sv.3, bf16[256,12288]{1,0:T(8,128)(2,1)} %sv.3, bf16[256,12288]{1,0:T(8,128)(2,1)} %sv.3, bf16[256,12288]{1,0:T(8,128)(2,1)} %sv.3, ...), custom_call_target="tpu_custom_call" | custom-call | tf_op jit(solution)/shard_map/pallas_call | solution.py:107
  32.0 0.0 collective-permute-done.1.gk_h.mh_ref
  32.0 0.0 copy-start.3
  32.0 0.0 collective-permute-done.hq.hk.hv
  32.0 0.0 copy-start.1
  32.0 5.2 %all-to-all-start = ((bf16[16,128,256]{2,1,0:T(8,128)(2,1)}), bf16[16,128,256]{2,1,0:T(8,128)(2,1)S(1)}, u32[]{:S(2)}, u32[]{:S(2)}) async-start(bf16[16,128,256]{2,1,0:T(8,128)(2,1)} %shard_map.104.hi_ref), calls=%async_computation | async-start | bytes 2097152 | tf_op jit(solution)/shard_map/all_to_all | solution.py:257
  37.3 0.0 copy-done.3
  37.3 0.0 copy-done.1
  37.3 0.0 copy-start
  37.3 0.0 copy-start.7
  37.3 0.0 copy-start.5
  37.3 0.0 copy-start.4
  37.3 0.0 copy-start.6
  37.3 21.5 %shard_map.105.lo_ref = bf16[16,128,256]{2,1,0:T(8,128)(2,1)} custom-call(s32[384,1]{1,0:T(8,128)} %sub.30.rel_ref, bf16[256,12288]{1,0:T(8,128)(2,1)} %sv.3, bf16[256,12288]{1,0:T(8,128)(2,1)} %sv.3, bf16[256,12288]{1,0:T(8,128)(2,1)} %sv.3, bf16[18,12288]{1,0:T(8,128)(2,1)} %copy-done.1, bf16[18,12288]{1,0:T(8,128)(2,1)} %copy-done.1, ...), custom_call_target="tpu_custom_call" | custom-call | tf_op jit(solution)/shard_map/pallas_call | solution.py:107
  58.8 3.6 %all-to-all-done.hi_ref = bf16[16,128,256]{2,1,0:T(8,128)(2,1)S(1)} async-done(((bf16[16,128,256]{2,1,0:T(8,128)(2,1)}), bf16[16,128,256]{2,1,0:T(8,128)(2,1)S(1)}, u32[]{:S(2)}, u32[]{:S(2)}) %all-to-all-start) | async-done | bytes 1048608 | tf_op jit(solution)/shard_map/all_to_all | solution.py:257
  62.4 0.0 copy-start.2
  62.4 4.6 %all-to-all-start.1 = ((bf16[16,128,256]{2,1,0:T(8,128)(2,1)}), bf16[16,128,256]{2,1,0:T(8,128)(2,1)}, u32[]{:S(2)}, u32[]{:S(2)}) async-start(bf16[16,128,256]{2,1,0:T(8,128)(2,1)} %shard_map.105.lo_ref), calls=%async_computation.1 | async-start | bytes 2097152 | tf_op jit(solution)/shard_map/all_to_all | solution.py:262
  67.1 0.0 copy-done
  67.1 2.1 %collective-permute-start.2 = (bf16[16,128,256]{2,1,0:T(8,128)(2,1)S(1)}, bf16[16,128,256]{2,1,0:T(8,128)(2,1)}, u32[]{:S(2)}, u32[]{:S(2)}) collective-permute-start(bf16[16,128,256]{2,1,0:T(8,128)(2,1)S(1)} %copy-done), channel_id=1, source_target_pairs={{0,1},{1,2},{2,3},{3,4},{4,5},{5,6},{6,7},{7,8},{8,9},{9,10},{10,1... | collective-permute-start | bytes 3145736 | tf_op jit(solution)/shard_map/ppermute | solution.py:16
  69.2 0.0 copy-done.7
  69.2 0.1 select_reduce_fusion.3
  69.3 0.1 pad.2.clone
  69.4 0.0 copy-done.5
  69.4 0.6 broadcast_in_dim.65.skip_ref
  70.0 0.0 copy-done.4
  70.0 0.1 copy.18
  70.1 0.2 rev.3
  70.3 0.0 copy-done.6
  70.3 0.2 select_reduce_fusion.1
  70.5 0.6 compare_select_fusion
  71.1 0.8 maximum_maximum_fusion.u_ref
  72.0 31.7 %collective-permute-done.2.prev_ref = bf16[16,128,256]{2,1,0:T(8,128)(2,1)} collective-permute-done((bf16[16,128,256]{2,1,0:T(8,128)(2,1)S(1)}, bf16[16,128,256]{2,1,0:T(8,128)(2,1)}, u32[]{:S(2)}, u32[]{:S(2)}) %collective-permute-start.2) | collective-permute-done | bytes 1048608 | tf_op jit(solution)/shard_map/ppermute | solution.py:16
  103.7 21.7 %shard_map.106 = bf16[256,4096]{1,0:T(8,128)(2,1)} custom-call(s32[384,1]{1,0:T(8,128)} %sub.30.rel_ref, bf16[256,8192]{1,0:T(8,128)(2,1)} %mg_ref.1, bf16[6,8192]{1,0:T(8,128)(2,1)} %copy-done.3, bf16[7,12288]{1,0:T(8,128)(2,1)} %wq_ref.1, bf16[16,128,256]{2,1,0:T(8,128)(2,1)} %collective-permute-done.2.prev_ref, bf16[16,128,256]{2,1,0:T(8,128)(2,1)} %shard_map.105.lo_ref, ...), custom_call_target="tpu_custom_call" | custom-call | tf_op jit(solution)/shard_map/pallas_call | solution.py:166
  125.4 0.0 copy-done.2
  125.4 0.0 all-to-all-done.1.lo_ref
  125.4 5.7 %shard_map.107 = bf16[127,16,256]{2,1,0:T(8,128)(2,1)} custom-call(s32[16]{0:T(128)} %get-tuple-element.15.begin_ref, s32[16]{0:T(128)} %get-tuple-element.14.first_ref, bf16[16,128,256]{2,1,0:T(8,128)(2,1)} %all-to-all-done.1.lo_ref, bf16[16,128,256]{2,1,0:T(8,128)(2,1)} %copy-done.2), custom_call_target="tpu_custom_call" | custom-call | tf_op jit(solution)/shard_map/pallas_call | solution.py:208
  (7 shorter events, 0.0 us)
Async XLA Ops:
  1.6 30.4 %collective-permute-start.1 = (bf16[6,8192]{1,0:T(8,128)(2,1)S(1)}, bf16[6,8192]{1,0:T(8,128)(2,1)S(1)}, u32[]{:S(2)}, u32[]{:S(2)}) collective-permute-start(bf16[6,8192]{1,0:T(8,128)(2,1)S(1)} %slice.7), channel_id=1, source_target_pairs={{0,1},{1,2},{2,3},{3,4},{4,5},{5,6},{6,7},{7,8},{8,9},{9,10},{10,1... | collective-permute-start | bytes 294920 | tf_op jit(solution)/shard_map/ppermute | solution.py:16
  4.7 27.3 %collective-permute-start = (bf16[18,12288]{1,0:T(8,128)(2,1)S(1)}, bf16[18,12288]{1,0:T(8,128)(2,1)S(1)}, u32[]{:S(2)}, u32[]{:S(2)}) collective-permute-start(bf16[18,12288]{1,0:T(8,128)(2,1)S(1)} %slice.6), channel_id=1, source_target_pairs={{0,1},{1,2},{2,3},{3,4},{4,5},{5,6},{6,7},{7,8},{8,9},{9,10},{10,1... | collective-permute-start | bytes 1327112 | tf_op jit(solution)/shard_map/ppermute | solution.py:16
  32.0 5.3 %copy-start.3 = (bf16[6,8192]{1,0:T(8,128)(2,1)}, bf16[6,8192]{1,0:T(8,128)(2,1)S(1)}, u32[]{:S(2)}) copy-start(bf16[6,8192]{1,0:T(8,128)(2,1)S(1)} %collective-permute-done.1.gk_h.mh_ref) | copy-start | bytes 294916
  32.0 5.3 %copy-start.1 = (bf16[18,12288]{1,0:T(8,128)(2,1)}, bf16[18,12288]{1,0:T(8,128)(2,1)S(1)}, u32[]{:S(2)}) copy-start(bf16[18,12288]{1,0:T(8,128)(2,1)S(1)} %collective-permute-done.hq.hk.hv) | copy-start | bytes 1327108
  32.0 30.4 %all-to-all-start = ((bf16[16,128,256]{2,1,0:T(8,128)(2,1)}), bf16[16,128,256]{2,1,0:T(8,128)(2,1)S(1)}, u32[]{:S(2)}, u32[]{:S(2)}) async-start(bf16[16,128,256]{2,1,0:T(8,128)(2,1)} %shard_map.104.hi_ref), calls=%async_computation | async-start | bytes 2097152 | tf_op jit(solution)/shard_map/all_to_all | solution.py:257
  37.3 29.8 %copy-start = (bf16[16,128,256]{2,1,0:T(8,128)(2,1)S(1)}, bf16[16,128,256]{2,1,0:T(8,128)(2,1)}, u32[]{:S(2)}) copy-start(bf16[16,128,256]{2,1,0:T(8,128)(2,1)} %shard_map.104.hi_ref) | copy-start | bytes 3145732
  37.3 31.9 %copy-start.7 = (s32[16]{0:T(128)S(1)}, s32[16]{0:T(128)}, u32[]{:S(2)}) copy-start(s32[16]{0:T(128)} %param.17) | copy-start | bytes 196
  37.3 32.1 %copy-start.5 = (bf16[4096]{0:T(1024)(128)(2,1)S(1)}, bf16[4096]{0:T(1024)(128)(2,1)}, u32[]{:S(2)}) copy-start(bf16[4096]{0:T(1024)(128)(2,1)} %param.15) | copy-start | bytes 24580
  37.3 32.7 %copy-start.4 = (bf16[128,256]{1,0:T(8,128)(2,1)S(1)}, bf16[128,256]{1,0:T(8,128)(2,1)}, u32[]{:S(2)}) copy-start(bf16[128,256]{1,0:T(8,128)(2,1)} %param.14) | copy-start | bytes 196612
  37.3 33.0 %copy-start.6 = (s32[16]{0:T(128)S(1)}, s32[16]{0:T(128)}, u32[]{:S(2)}) copy-start(s32[16]{0:T(128)} %param.16) | copy-start | bytes 196
  62.4 63.0 %copy-start.2 = (bf16[16,128,256]{2,1,0:T(8,128)(2,1)}, bf16[16,128,256]{2,1,0:T(8,128)(2,1)S(1)}, u32[]{:S(2)}) copy-start(bf16[16,128,256]{2,1,0:T(8,128)(2,1)S(1)} %all-to-all-done.hi_ref) | copy-start | bytes 3145732
  62.4 63.0 %all-to-all-start.1 = ((bf16[16,128,256]{2,1,0:T(8,128)(2,1)}), bf16[16,128,256]{2,1,0:T(8,128)(2,1)}, u32[]{:S(2)}, u32[]{:S(2)}) async-start(bf16[16,128,256]{2,1,0:T(8,128)(2,1)} %shard_map.105.lo_ref), calls=%async_computation.1 | async-start | bytes 2097152 | tf_op jit(solution)/shard_map/all_to_all | solution.py:262
  67.1 36.6 %collective-permute-start.2 = (bf16[16,128,256]{2,1,0:T(8,128)(2,1)S(1)}, bf16[16,128,256]{2,1,0:T(8,128)(2,1)}, u32[]{:S(2)}, u32[]{:S(2)}) collective-permute-start(bf16[16,128,256]{2,1,0:T(8,128)(2,1)S(1)} %copy-done), channel_id=1, source_target_pairs={{0,1},{1,2},{2,3},{3,4},{4,5},{5,6},{6,7},{7,8},{8,9},{9,10},{10,1... | collective-permute-start | bytes 3145736 | tf_op jit(solution)/shard_map/ppermute | solution.py:16

commit v9 on v8

--- a/solution.py
+++ b/solution.py
@@ -258,7 +258,7 @@
     z_lo = short_chain(
         rel, se_streams, prev_se, mr_gates, prev_mr, se_feat, se_filt, mr_feat, shards, 0
     )
-    z_lo, recv_hi = lax.optimization_barrier((z_lo, recv_hi))
+    z_lo, recv_hi, prev_z = lax.optimization_barrier((z_lo, recv_hi, prev_z))
     recv_lo = lax.all_to_all(z_lo, "seq", split_axis=0, concat_axis=0, tiled=True)
     filt_t = mr_filter[::-1].T.astype(jnp.float32)
     filters = filt_t.shape[0]

time: 132 us -> 112 us (0.85)
  waiting for transfers between devices: 35.3 us -> 13.4 us
  local copies, waits for them, and re-layouts: 4.01 us -> 5.93 us
    ppermute x3, waiting for transfers between devices: 31.7 us -> 12.8 us  [passed_along(): return lax.ppermute(x, axis, pairs)]
    all_to_all x1, waiting for transfers between devices: 3.63 us -> 0.01 us  [local(): lax.all_to_all(z_hi, 'seq', split_axis=0, concat_axis=0, tiled=True)]
    unnamed x17 -> x19, local copies, waits for them, and re-layouts: 0.15 us -> 2.1 us
  transfers between devices with their start and end apart: 5 -> 5, of which waited for: 2 -> 2; matrix products, arithmetic and copies ran while one was open for 5% -> 5% of each run, Pallas kernels for 49% -> 58%
where the time goes in v9:
time: 112 us; the launch traced here: 111 us
  Pallas kernels  70.3 us (63%)
  starting transfers between devices  17.1 us (15%)
  waiting for transfers between devices  13.4 us (12%)
  local copies, waits for them, and re-layouts  5.93 us (5%)
  other arithmetic  3.25 us (3%)
    pallas_call x2, Pallas kernels, short_chain(): pl.pallas_call(functools.partial(chain_kernel, group_ch=channels // se_fi...  42.9 us
    pallas_call x1, Pallas kernels, long_conv_out(): pl.pallas_call(long_kernel, grid=(steps,), in_specs=[pl.BlockSpec(rel.sha...  21.8 us
    ppermute x3, waiting for transfers between devices, passed_along(): return lax.ppermute(x, axis, pairs)  12.8 us
    ppermute x3, starting transfers between devices, passed_along(): return lax.ppermute(x, axis, pairs)  7.64 us
    pallas_call x1, Pallas kernels, cut_tails_all(): pl.pallas_call(tail_kernel, in_specs=[smem, smem, vmem, vmem], out_specs=...  5.65 us
    all_to_all x1, starting transfers between devices, local(): lax.all_to_all(z_hi, 'seq', split_axis=0, concat_axis=0, tiled=True)  5.24 us
    all_to_all x1, starting transfers between devices, local(): lax.all_to_all(z_lo, 'seq', split_axis=0, concat_axis=0, tiled=True)  4.22 us
  transfers between devices with their start and end apart: 5, of which 2 were waited for; matrix products, arithmetic and copies ran while one was open for 5% of the time, Pallas kernels for 58%

profile of v9, /device:TPU:18, one launch (start us, length us, event | category | flops | bytes accessed | tf_op | source)
XLA Modules:
  0.0 110.7 jit_solution(8237879942019104259)
XLA Ops:
  0.6 1.2 %slice.6 = bf16[18,12288]{1,0:T(8,128)(2,1)S(1)} slice(bf16[256,12288]{1,0:T(8,128)(2,1)} %sv.3), slice={[238:256], [0:12288]} | slice | bytes 884736 | tf_op jit(solution)/shard_map/slice | solution.py:245
  1.8 1.9 %collective-permute-start = (bf16[18,12288]{1,0:T(8,128)(2,1)S(1)}, bf16[18,12288]{1,0:T(8,128)(2,1)S(1)}, u32[]{:S(2)}, u32[]{:S(2)}) collective-permute-start(bf16[18,12288]{1,0:T(8,128)(2,1)S(1)} %slice.6), channel_id=1, source_target_pairs={{0,1},{1,2},{2,3},{3,4},{4,5},{5,6},{6,7},{7,8},{8,9},{9,10},{10,1... | collective-permute-start | bytes 1327112 | tf_op jit(solution)/shard_map/ppermute | solution.py:16
  3.8 0.9 slice.7
  4.7 3.5 %collective-permute-start.1 = (bf16[6,8192]{1,0:T(8,128)(2,1)S(1)}, bf16[6,8192]{1,0:T(8,128)(2,1)S(1)}, u32[]{:S(2)}, u32[]{:S(2)}) collective-permute-start(bf16[6,8192]{1,0:T(8,128)(2,1)S(1)} %slice.7), channel_id=1, source_target_pairs={{0,1},{1,2},{2,3},{3,4},{4,5},{5,6},{6,7},{7,8},{8,9},{9,10},{10,1... | collective-permute-start | bytes 294920 | tf_op jit(solution)/shard_map/ppermute | solution.py:16
  8.3 0.7 convert_reduce_fusion
  9.0 0.7 select_reduce_fusion
  9.8 0.8 sub.30.rel_ref
  10.6 21.4 %shard_map.104.hi_ref = bf16[16,128,256]{2,1,0:T(8,128)(2,1)} custom-call(s32[384,1]{1,0:T(8,128)} %sub.30.rel_ref, bf16[256,12288]{1,0:T(8,128)(2,1)} %sv.3, bf16[256,12288]{1,0:T(8,128)(2,1)} %sv.3, bf16[256,12288]{1,0:T(8,128)(2,1)} %sv.3, bf16[256,12288]{1,0:T(8,128)(2,1)} %sv.3, bf16[256,12288]{1,0:T(8,128)(2,1)} %sv.3, bf16[256,12288]{1,0:T(8,128)(2,1)} %sv.3, ...), custom_call_target="tpu_custom_call" | custom-call | tf_op jit(solution)/shard_map/pallas_call | solution.py:107
  32.0 0.0 collective-permute-done.1.gk_h.mh_ref
  32.0 0.0 copy-start.4
  32.0 0.0 collective-permute-done.hq.hk.hv
  32.0 0.0 copy-start
  32.0 5.2 %all-to-all-start = ((bf16[16,128,256]{2,1,0:T(8,128)(2,1)}), bf16[16,128,256]{2,1,0:T(8,128)(2,1)S(1)}, u32[]{:S(2)}, u32[]{:S(2)}) async-start(bf16[16,128,256]{2,1,0:T(8,128)(2,1)} %shard_map.104.hi_ref), calls=%async_computation | async-start | bytes 2097152 | tf_op jit(solution)/shard_map/all_to_all | solution.py:257
  37.3 0.0 copy-start.5
  37.3 0.0 copy-start.6
  37.3 0.0 copy-start.8
  37.3 0.0 copy-start.7
  37.3 2.2 %collective-permute-start.2 = (bf16[16,128,256]{2,1,0:T(8,128)(2,1)}, bf16[16,128,256]{2,1,0:T(8,128)(2,1)S(1)}, u32[]{:S(2)}, u32[]{:S(2)}) collective-permute-start(bf16[16,128,256]{2,1,0:T(8,128)(2,1)} %shard_map.104.hi_ref), channel_id=1, source_target_pairs={{0,1},{1,2},{2,3},{3,4},{4,5},{5,6},{6,7},{7,8},{8,9},{9,10},{10,1... | collective-permute-start | bytes 3145736 | tf_op jit(solution)/shard_map/ppermute | solution.py:16
  39.5 0.0 copy-done.4
  39.5 0.0 copy-done
  39.5 21.5 %shard_map.105.lo_ref = bf16[16,128,256]{2,1,0:T(8,128)(2,1)} custom-call(s32[384,1]{1,0:T(8,128)} %sub.30.rel_ref, bf16[256,12288]{1,0:T(8,128)(2,1)} %sv.3, bf16[256,12288]{1,0:T(8,128)(2,1)} %sv.3, bf16[256,12288]{1,0:T(8,128)(2,1)} %sv.3, bf16[18,12288]{1,0:T(8,128)(2,1)} %copy-done, bf16[18,12288]{1,0:T(8,128)(2,1)} %copy-done, ...), custom_call_target="tpu_custom_call" | custom-call | tf_op jit(solution)/shard_map/pallas_call | solution.py:107
  61.0 12.8 %collective-permute-done.2.prev_ref = bf16[16,128,256]{2,1,0:T(8,128)(2,1)S(1)} collective-permute-done((bf16[16,128,256]{2,1,0:T(8,128)(2,1)}, bf16[16,128,256]{2,1,0:T(8,128)(2,1)S(1)}, u32[]{:S(2)}, u32[]{:S(2)}) %collective-permute-start.2) | collective-permute-done | bytes 1048608 | tf_op jit(solution)/shard_map/ppermute | solution.py:16
  73.7 0.0 copy-start.3
  73.8 0.0 all-to-all-done.hi_ref
  73.8 0.0 copy-start.1
  73.8 1.0 copy-done.3
  74.7 4.2 %all-to-all-start.1 = ((bf16[16,128,256]{2,1,0:T(8,128)(2,1)}), bf16[16,128,256]{2,1,0:T(8,128)(2,1)S(1)}, u32[]{:S(2)}, u32[]{:S(2)}) async-start(bf16[16,128,256]{2,1,0:T(8,128)(2,1)} %shard_map.105.lo_ref), calls=%async_computation.1 | async-start | bytes 2097152 | tf_op jit(solution)/shard_map/all_to_all | solution.py:262
  79.0 0.0 copy-done.5
  79.0 0.1 copy.18
  79.1 0.2 rev.3
  79.3 0.1 pad.2.clone
  79.4 0.0 copy-done.6
  79.4 0.6 broadcast_in_dim.65.skip_ref
  80.0 0.0 copy-done.8
  80.0 0.1 select_reduce_fusion.3
  80.1 0.0 copy-done.7
  80.1 0.2 select_reduce_fusion.1
  80.3 0.6 compare_select_fusion
  80.9 0.8 maximum_maximum_fusion.u_ref
  81.8 21.8 %shard_map.106 = bf16[256,4096]{1,0:T(8,128)(2,1)} custom-call(s32[384,1]{1,0:T(8,128)} %sub.30.rel_ref, bf16[256,8192]{1,0:T(8,128)(2,1)} %mg_ref.1, bf16[6,8192]{1,0:T(8,128)(2,1)} %copy-done.4, bf16[7,12288]{1,0:T(8,128)(2,1)} %wq_ref.1, bf16[16,128,256]{2,1,0:T(8,128)(2,1)} %copy-done.3, bf16[16,128,256]{2,1,0:T(8,128)(2,1)} %shard_map.105.lo_ref, ...), custom_call_target="tpu_custom_call" | custom-call | tf_op jit(solution)/shard_map/pallas_call | solution.py:166
  103.5 0.0 copy-done.1
  103.5 0.6 all-to-all-done.1.lo_ref
  104.1 0.0 copy-start.2
  104.1 1.0 copy-done.2
  105.1 5.6 %shard_map.107 = bf16[127,16,256]{2,1,0:T(8,128)(2,1)} custom-call(s32[16]{0:T(128)} %get-tuple-element.17.begin_ref, s32[16]{0:T(128)} %get-tuple-element.16.first_ref, bf16[16,128,256]{2,1,0:T(8,128)(2,1)} %copy-done.2, bf16[16,128,256]{2,1,0:T(8,128)(2,1)} %copy-done.1), custom_call_target="tpu_custom_call" | custom-call | tf_op jit(solution)/shard_map/pallas_call | solution.py:208
  (7 shorter events, 0.0 us)
Async XLA Ops:
  1.8 30.2 %collective-permute-start = (bf16[18,12288]{1,0:T(8,128)(2,1)S(1)}, bf16[18,12288]{1,0:T(8,128)(2,1)S(1)}, u32[]{:S(2)}, u32[]{:S(2)}) collective-permute-start(bf16[18,12288]{1,0:T(8,128)(2,1)S(1)} %slice.6), channel_id=1, source_target_pairs={{0,1},{1,2},{2,3},{3,4},{4,5},{5,6},{6,7},{7,8},{8,9},{9,10},{10,1... | collective-permute-start | bytes 1327112 | tf_op jit(solution)/shard_map/ppermute | solution.py:16
  4.7 27.3 %collective-permute-start.1 = (bf16[6,8192]{1,0:T(8,128)(2,1)S(1)}, bf16[6,8192]{1,0:T(8,128)(2,1)S(1)}, u32[]{:S(2)}, u32[]{:S(2)}) collective-permute-start(bf16[6,8192]{1,0:T(8,128)(2,1)S(1)} %slice.7), channel_id=1, source_target_pairs={{0,1},{1,2},{2,3},{3,4},{4,5},{5,6},{6,7},{7,8},{8,9},{9,10},{10,1... | collective-permute-start | bytes 294920 | tf_op jit(solution)/shard_map/ppermute | solution.py:16
  32.0 7.5 %copy-start.4 = (bf16[6,8192]{1,0:T(8,128)(2,1)}, bf16[6,8192]{1,0:T(8,128)(2,1)S(1)}, u32[]{:S(2)}) copy-start(bf16[6,8192]{1,0:T(8,128)(2,1)S(1)} %collective-permute-done.1.gk_h.mh_ref) | copy-start | bytes 294916
  32.0 7.5 %copy-start = (bf16[18,12288]{1,0:T(8,128)(2,1)}, bf16[18,12288]{1,0:T(8,128)(2,1)S(1)}, u32[]{:S(2)}) copy-start(bf16[18,12288]{1,0:T(8,128)(2,1)S(1)} %collective-permute-done.hq.hk.hv) | copy-start | bytes 1327108
  32.0 41.7 %all-to-all-start = ((bf16[16,128,256]{2,1,0:T(8,128)(2,1)}), bf16[16,128,256]{2,1,0:T(8,128)(2,1)S(1)}, u32[]{:S(2)}, u32[]{:S(2)}) async-start(bf16[16,128,256]{2,1,0:T(8,128)(2,1)} %shard_map.104.hi_ref), calls=%async_computation | async-start | bytes 2097152 | tf_op jit(solution)/shard_map/all_to_all | solution.py:257
  37.3 41.7 %copy-start.5 = (bf16[128,256]{1,0:T(8,128)(2,1)S(1)}, bf16[128,256]{1,0:T(8,128)(2,1)}, u32[]{:S(2)}) copy-start(bf16[128,256]{1,0:T(8,128)(2,1)} %param.14) | copy-start | bytes 196612
  37.3 42.1 %copy-start.6 = (bf16[4096]{0:T(1024)(128)(2,1)S(1)}, bf16[4096]{0:T(1024)(128)(2,1)}, u32[]{:S(2)}) copy-start(bf16[4096]{0:T(1024)(128)(2,1)} %param.15) | copy-start | bytes 24580
  37.3 42.7 %copy-start.8 = (s32[16]{0:T(128)S(1)}, s32[16]{0:T(128)}, u32[]{:S(2)}) copy-start(s32[16]{0:T(128)} %param.17) | copy-start | bytes 196
  37.3 42.8 %copy-start.7 = (s32[16]{0:T(128)S(1)}, s32[16]{0:T(128)}, u32[]{:S(2)}) copy-start(s32[16]{0:T(128)} %param.16) | copy-start | bytes 196
  37.3 36.5 %collective-permute-start.2 = (bf16[16,128,256]{2,1,0:T(8,128)(2,1)}, bf16[16,128,256]{2,1,0:T(8,128)(2,1)S(1)}, u32[]{:S(2)}, u32[]{:S(2)}) collective-permute-start(bf16[16,128,256]{2,1,0:T(8,128)(2,1)} %shard_map.104.hi_ref), channel_id=1, source_target_pairs={{0,1},{1,2},{2,3},{3,4},{4,5},{5,6},{6,7},{7,8},{8,9},{9,10},{10,1... | collective-permute-start | bytes 3145736 | tf_op jit(solution)/shard_map/ppermute | solution.py:16
  73.7 1.0 copy-start.3
  73.8 29.8 %copy-start.1 = (bf16[16,128,256]{2,1,0:T(8,128)(2,1)}, bf16[16,128,256]{2,1,0:T(8,128)(2,1)S(1)}, u32[]{:S(2)}) copy-start(bf16[16,128,256]{2,1,0:T(8,128)(2,1)S(1)} %all-to-all-done.hi_ref) | copy-start | bytes 3145732
  74.7 29.4 %all-to-all-start.1 = ((bf16[16,128,256]{2,1,0:T(8,128)(2,1)}), bf16[16,128,256]{2,1,0:T(8,128)(2,1)S(1)}, u32[]{:S(2)}, u32[]{:S(2)}) async-start(bf16[16,128,256]{2,1,0:T(8,128)(2,1)} %shard_map.105.lo_ref), calls=%async_computation.1 | async-start | bytes 2097152 | tf_op jit(solution)/shard_map/all_to_all | solution.py:262
  104.1 1.0 copy-start.2

commit v10 on v9

--- a/solution.py
+++ b/solution.py
@@ -120,7 +120,7 @@
 
 
 def long_kernel(rel_ref, mg_ref, mh_ref, wq_ref, prev_ref, lo_ref, hi_ref, skip_ref,
-                u_ref, out_ref, xa):
+                filt_ref, out_ref, xa, group_ch):
     rows = xa.shape[0]
     reach = mh_ref.shape[0]
     xa[HALO - reach : HALO, :] = mh_ref[...].astype(jnp.float32)
@@ -129,8 +129,21 @@
     q2 = short_conv_rows(xa, wq_ref, HALO, rel_dist(rel_ref, blk - HALO, rows))
     blk = lo_ref.shape[1]
     tile = lo_ref.shape[2]
-    width = u_ref.shape[1]
-    per_group = tile // u_ref.shape[0]
+    taps_n, filters = filt_ref.shape
+    width = 2 * taps_n
+    local_groups = tile // group_ch
+    pick = lax.broadcasted_iota(jnp.int32, (local_groups, filters), 1) == (
+        pl.program_id(0) * local_groups + lax.broadcasted_iota(jnp.int32, (local_groups, filters), 0)
+    )
+    cols = lax.dot_general(
+        pick.astype(filt_ref.dtype), filt_ref[...], (((1,), (1,)), ((), ())),
+        preferred_element_type=jnp.float32,
+    ).astype(filt_ref.dtype)
+    flip = lax.broadcasted_iota(jnp.int32, (taps_n, width), 1) == (
+        taps_n - lax.broadcasted_iota(jnp.int32, (taps_n, width), 0)
+    )
+    u_val = jnp.dot(cols, flip.astype(filt_ref.dtype), preferred_element_type=jnp.float32)
+    per_group = tile // local_groups
     lo = lo_ref[0]
     hi = hi_ref[0]
     windows = (jnp.concatenate([prev_ref[0], lo], axis=0), jnp.concatenate([lo, hi], axis=0))
@@ -142,9 +155,9 @@
     halves = tile // GROUP_LANES
     groups_half = GROUP_LANES // per_group
     acc = [[jnp.zeros((blk, GROUP_LANES), jnp.float32) for _ in range(halves)] for _ in range(2)]
-    for g in range(u_ref.shape[0]):
+    for g in range(local_groups):
         half = g // groups_half
-        row = jnp.broadcast_to(u_ref[g : g + 1, :], (blk, width))
+        row = jnp.broadcast_to(u_val[g : g + 1, :], (blk, width))
         taps = pltpu.roll(row, 0, 1, stride=1, stride_axis=0)
         for b in range(2):
             mat = jnp.where(masks[b], taps, 0.0).astype(jnp.bfloat16)
@@ -157,14 +170,13 @@
     out_ref[...] = (q2 * mixed.astype(jnp.float32)).astype(jnp.bfloat16)
 
 
-def long_conv_out(rel, mr_gates, mr_halo, mr_feat, prev_z, z_lo, z_hi, skip, taps_rows):
+def long_conv_out(rel, mr_gates, mr_halo, mr_feat, prev_z, z_lo, z_hi, skip, mr_filter):
     steps, blk, lanes = z_lo.shape
     tok_rows = 2 * blk
     channels = steps * lanes
-    per_group = channels // taps_rows.shape[0]
     piece = pl.BlockSpec((1, blk, lanes), lambda j: (j, 0, 0))
     return pl.pallas_call(
-        long_kernel,
+        functools.partial(long_kernel, group_ch=channels // mr_filter.shape[1]),
         grid=(steps,),
         in_specs=[
             pl.BlockSpec(rel.shape, lambda j: (0, 0)),
@@ -175,12 +187,12 @@
             piece,
             piece,
             pl.BlockSpec((1, lanes), lambda j: (0, j)),
-            pl.BlockSpec((lanes // per_group, taps_rows.shape[1]), lambda j: (j, 0)),
+            pl.BlockSpec(mr_filter.shape, lambda j: (0, 0)),
         ],
         out_specs=pl.BlockSpec((tok_rows, lanes), lambda j: (0, j)),
         out_shape=jax.ShapeDtypeStruct((tok_rows, channels), jnp.bfloat16),
         scratch_shapes=[pltpu.VMEM((tok_rows + HALO, lanes), jnp.float32)],
-    )(rel, mr_gates, mr_halo, mr_feat, prev_z, z_lo, z_hi, skip, taps_rows)
+    )(rel, mr_gates, mr_halo, mr_feat, prev_z, z_lo, z_hi, skip, mr_filter)
 
 
 def tail_kernel(begin_ref, first_ref, lo_ref, hi_ref, out_ref, z_all):
@@ -260,15 +272,8 @@
     )
     z_lo, recv_hi, prev_z = lax.optimization_barrier((z_lo, recv_hi, prev_z))
     recv_lo = lax.all_to_all(z_lo, "seq", split_axis=0, concat_axis=0, tiled=True)
-    filt_t = mr_filter[::-1].T.astype(jnp.float32)
-    filters = filt_t.shape[0]
-    taps_rows = jnp.concatenate(
-        [jnp.zeros((filters, 1), jnp.float32), filt_t, jnp.zeros((filters, tap_count - 1), jnp.float32)],
-        axis=1,
-    )
-
     hyena_out = long_conv_out(
-        rel, mr_gates, prev_mr, mr_feat, prev_z, z_lo, z_hi, mr_skip[None, :], taps_rows
+        rel, mr_gates, prev_mr, mr_feat, prev_z, z_lo, z_hi, mr_skip[None, :], mr_filter
     )
     rows_ids = jnp.arange(total_req, dtype=jnp.int32)
     owner = jnp.sum(

time: 112 us -> 112 us (level)
  Pallas kernels: 70.3 us -> 71.8 us
    pallas_call x1, Pallas kernels: 21.8 us -> 23.2 us  [long_conv_out(): pl.pallas_call(functools.partial(long_kernel, group_ch=channels // mr_fil...]
  transfers between devices with their start and end apart: 5 -> 5, of which waited for: 2 -> 2; matrix products, arithmetic and copies ran while one was open for 5% -> 4% of each run, Pallas kernels for 58% -> 60%
where the time goes in v10:
time: 112 us; the launch traced here: 111 us
  Pallas kernels  71.8 us (64%)
  starting transfers between devices  17.1 us (15%)
  waiting for transfers between devices  13.2 us (12%)
  local copies, waits for them, and re-layouts  5.51 us (5%)
  other arithmetic  2.41 us (2%)
    pallas_call x2, Pallas kernels, short_chain(): pl.pallas_call(functools.partial(chain_kernel, group_ch=channels // se_fi...  42.9 us
    pallas_call x1, Pallas kernels, long_conv_out(): pl.pallas_call(functools.partial(long_kernel, group_ch=channels // mr_fil...  23.2 us
    ppermute x3, waiting for transfers between devices, passed_along(): return lax.ppermute(x, axis, pairs)  12.8 us
    ppermute x3, starting transfers between devices, passed_along(): return lax.ppermute(x, axis, pairs)  7.64 us
    pallas_call x1, Pallas kernels, cut_tails_all(): pl.pallas_call(tail_kernel, in_specs=[smem, smem, vmem, vmem], out_specs=...  5.65 us
    all_to_all x1, starting transfers between devices, local(): lax.all_to_all(z_hi, 'seq', split_axis=0, concat_axis=0, tiled=True)  5.24 us
    all_to_all x1, starting transfers between devices, local(): lax.all_to_all(z_lo, 'seq', split_axis=0, concat_axis=0, tiled=True)  4.22 us
  transfers between devices with their start and end apart: 5, of which 2 were waited for; matrix products, arithmetic and copies ran while one was open for 4% of the time, Pallas kernels for 60%

profile of v10, /device:TPU:18, one launch (start us, length us, event | category | flops | bytes accessed | tf_op | source)
XLA Modules:
  0.0 110.7 jit_solution(12354923745977470710)
XLA Ops:
  0.6 1.2 %slice.6 = bf16[18,12288]{1,0:T(8,128)(2,1)S(1)} slice(bf16[256,12288]{1,0:T(8,128)(2,1)} %sv.3), slice={[238:256], [0:12288]} | slice | bytes 884736 | tf_op jit(solution)/shard_map/slice | solution.py:257
  1.8 1.9 %collective-permute-start = (bf16[18,12288]{1,0:T(8,128)(2,1)S(1)}, bf16[18,12288]{1,0:T(8,128)(2,1)S(1)}, u32[]{:S(2)}, u32[]{:S(2)}) collective-permute-start(bf16[18,12288]{1,0:T(8,128)(2,1)S(1)} %slice.6), channel_id=1, source_target_pairs={{0,1},{1,2},{2,3},{3,4},{4,5},{5,6},{6,7},{7,8},{8,9},{9,10},{10,1... | collective-permute-start | bytes 1327112 | tf_op jit(solution)/shard_map/ppermute | solution.py:16
  3.8 0.9 slice.7
  4.7 3.5 %collective-permute-start.1 = (bf16[6,8192]{1,0:T(8,128)(2,1)S(1)}, bf16[6,8192]{1,0:T(8,128)(2,1)S(1)}, u32[]{:S(2)}, u32[]{:S(2)}) collective-permute-start(bf16[6,8192]{1,0:T(8,128)(2,1)S(1)} %slice.7), channel_id=1, source_target_pairs={{0,1},{1,2},{2,3},{3,4},{4,5},{5,6},{6,7},{7,8},{8,9},{9,10},{10,1... | collective-permute-start | bytes 294920 | tf_op jit(solution)/shard_map/ppermute | solution.py:16
  8.3 0.7 convert_reduce_fusion
  9.0 0.7 select_reduce_fusion
  9.8 0.8 sub.30.rel_ref
  10.5 21.4 %shard_map.104.hi_ref = bf16[16,128,256]{2,1,0:T(8,128)(2,1)} custom-call(s32[384,1]{1,0:T(8,128)} %sub.30.rel_ref, bf16[256,12288]{1,0:T(8,128)(2,1)} %sv.3, bf16[256,12288]{1,0:T(8,128)(2,1)} %sv.3, bf16[256,12288]{1,0:T(8,128)(2,1)} %sv.3, bf16[256,12288]{1,0:T(8,128)(2,1)} %sv.3, bf16[256,12288]{1,0:T(8,128)(2,1)} %sv.3, bf16[256,12288]{1,0:T(8,128)(2,1)} %sv.3, ...), custom_call_target="tpu_custom_call" | custom-call | tf_op jit(solution)/shard_map/pallas_call | solution.py:107
  32.0 0.0 collective-permute-done.1.gk_h.mh_ref
  32.0 0.0 copy-start.4
  32.0 0.0 collective-permute-done.hq.hk.hv
  32.0 0.0 copy-start
  32.0 5.2 %all-to-all-start = ((bf16[16,128,256]{2,1,0:T(8,128)(2,1)}), bf16[16,128,256]{2,1,0:T(8,128)(2,1)S(1)}, u32[]{:S(2)}, u32[]{:S(2)}) async-start(bf16[16,128,256]{2,1,0:T(8,128)(2,1)} %shard_map.104.hi_ref), calls=%async_computation | async-start | bytes 2097152 | tf_op jit(solution)/shard_map/all_to_all | solution.py:269
  37.3 0.0 copy-start.5
  37.3 0.0 copy-start.7
  37.3 0.0 copy-start.6
  37.3 2.2 %collective-permute-start.2 = (bf16[16,128,256]{2,1,0:T(8,128)(2,1)}, bf16[16,128,256]{2,1,0:T(8,128)(2,1)S(1)}, u32[]{:S(2)}, u32[]{:S(2)}) collective-permute-start(bf16[16,128,256]{2,1,0:T(8,128)(2,1)} %shard_map.104.hi_ref), channel_id=1, source_target_pairs={{0,1},{1,2},{2,3},{3,4},{4,5},{5,6},{6,7},{7,8},{8,9},{9,10},{10,1... | collective-permute-start | bytes 3145736 | tf_op jit(solution)/shard_map/ppermute | solution.py:16
  39.5 0.0 copy-done.4
  39.5 0.0 copy-done
  39.5 21.5 %shard_map.105.lo_ref = bf16[16,128,256]{2,1,0:T(8,128)(2,1)} custom-call(s32[384,1]{1,0:T(8,128)} %sub.30.rel_ref, bf16[256,12288]{1,0:T(8,128)(2,1)} %sv.3, bf16[256,12288]{1,0:T(8,128)(2,1)} %sv.3, bf16[256,12288]{1,0:T(8,128)(2,1)} %sv.3, bf16[18,12288]{1,0:T(8,128)(2,1)} %copy-done, bf16[18,12288]{1,0:T(8,128)(2,1)} %copy-done, ...), custom_call_target="tpu_custom_call" | custom-call | tf_op jit(solution)/shard_map/pallas_call | solution.py:107
  61.0 12.8 %collective-permute-done.2.prev_ref = bf16[16,128,256]{2,1,0:T(8,128)(2,1)S(1)} collective-permute-done((bf16[16,128,256]{2,1,0:T(8,128)(2,1)}, bf16[16,128,256]{2,1,0:T(8,128)(2,1)S(1)}, u32[]{:S(2)}, u32[]{:S(2)}) %collective-permute-start.2) | collective-permute-done | bytes 1048608 | tf_op jit(solution)/shard_map/ppermute | solution.py:16
  73.8 0.0 copy-start.3
  73.8 0.0 all-to-all-done.hi_ref
  73.8 0.0 copy-start.1
  73.8 1.0 copy-done.3
  74.7 4.2 %all-to-all-start.1 = ((bf16[16,128,256]{2,1,0:T(8,128)(2,1)}), bf16[16,128,256]{2,1,0:T(8,128)(2,1)S(1)}, u32[]{:S(2)}, u32[]{:S(2)}) async-start(bf16[16,128,256]{2,1,0:T(8,128)(2,1)} %shard_map.105.lo_ref), calls=%async_computation.1 | async-start | bytes 2097152 | tf_op jit(solution)/shard_map/all_to_all | solution.py:274
  78.9 0.0 copy-done.5
  78.9 0.6 broadcast_in_dim.59.skip_ref
  79.6 0.0 copy-done.7
  79.6 0.1 select_reduce_fusion.3
  79.7 0.0 copy-done.6
  79.7 0.2 select_reduce_fusion.1
  79.9 0.6 compare_select_fusion
  80.5 23.2 %shard_map.106 = bf16[256,4096]{1,0:T(8,128)(2,1)} custom-call(s32[384,1]{1,0:T(8,128)} %sub.30.rel_ref, bf16[256,8192]{1,0:T(8,128)(2,1)} %mg_ref.1, bf16[6,8192]{1,0:T(8,128)(2,1)} %copy-done.4, bf16[7,12288]{1,0:T(8,128)(2,1)} %wq_ref.1, bf16[16,128,256]{2,1,0:T(8,128)(2,1)} %copy-done.3, bf16[16,128,256]{2,1,0:T(8,128)(2,1)} %shard_map.105.lo_ref, ...), custom_call_target="tpu_custom_call" | custom-call | tf_op jit(solution)/shard_map/pallas_call | solution.py:178
  103.7 0.0 copy-done.1
  103.7 0.4 all-to-all-done.1.lo_ref
  104.1 0.0 copy-start.2
  104.1 1.0 copy-done.2
  105.1 5.6 %shard_map.107 = bf16[127,16,256]{2,1,0:T(8,128)(2,1)} custom-call(s32[16]{0:T(128)} %get-tuple-element.17.begin_ref, s32[16]{0:T(128)} %get-tuple-element.16.first_ref, bf16[16,128,256]{2,1,0:T(8,128)(2,1)} %copy-done.2, bf16[16,128,256]{2,1,0:T(8,128)(2,1)} %copy-done.1), custom_call_target="tpu_custom_call" | custom-call | tf_op jit(solution)/shard_map/pallas_call | solution.py:220
  (4 shorter events, 0.0 us)
Async XLA Ops:
  1.8 30.2 %collective-permute-start = (bf16[18,12288]{1,0:T(8,128)(2,1)S(1)}, bf16[18,12288]{1,0:T(8,128)(2,1)S(1)}, u32[]{:S(2)}, u32[]{:S(2)}) collective-permute-start(bf16[18,12288]{1,0:T(8,128)(2,1)S(1)} %slice.6), channel_id=1, source_target_pairs={{0,1},{1,2},{2,3},{3,4},{4,5},{5,6},{6,7},{7,8},{8,9},{9,10},{10,1... | collective-permute-start | bytes 1327112 | tf_op jit(solution)/shard_map/ppermute | solution.py:16
  4.7 27.3 %collective-permute-start.1 = (bf16[6,8192]{1,0:T(8,128)(2,1)S(1)}, bf16[6,8192]{1,0:T(8,128)(2,1)S(1)}, u32[]{:S(2)}, u32[]{:S(2)}) collective-permute-start(bf16[6,8192]{1,0:T(8,128)(2,1)S(1)} %slice.7), channel_id=1, source_target_pairs={{0,1},{1,2},{2,3},{3,4},{4,5},{5,6},{6,7},{7,8},{8,9},{9,10},{10,1... | collective-permute-start | bytes 294920 | tf_op jit(solution)/shard_map/ppermute | solution.py:16
  32.0 7.5 %copy-start.4 = (bf16[6,8192]{1,0:T(8,128)(2,1)}, bf16[6,8192]{1,0:T(8,128)(2,1)S(1)}, u32[]{:S(2)}) copy-start(bf16[6,8192]{1,0:T(8,128)(2,1)S(1)} %collective-permute-done.1.gk_h.mh_ref) | copy-start | bytes 294916
  32.0 7.5 %copy-start = (bf16[18,12288]{1,0:T(8,128)(2,1)}, bf16[18,12288]{1,0:T(8,128)(2,1)S(1)}, u32[]{:S(2)}) copy-start(bf16[18,12288]{1,0:T(8,128)(2,1)S(1)} %collective-permute-done.hq.hk.hv) | copy-start | bytes 1327108
  32.0 41.7 %all-to-all-start = ((bf16[16,128,256]{2,1,0:T(8,128)(2,1)}), bf16[16,128,256]{2,1,0:T(8,128)(2,1)S(1)}, u32[]{:S(2)}, u32[]{:S(2)}) async-start(bf16[16,128,256]{2,1,0:T(8,128)(2,1)} %shard_map.104.hi_ref), calls=%async_computation | async-start | bytes 2097152 | tf_op jit(solution)/shard_map/all_to_all | solution.py:269
  37.3 41.7 %copy-start.5 = (bf16[4096]{0:T(1024)(128)(2,1)S(1)}, bf16[4096]{0:T(1024)(128)(2,1)}, u32[]{:S(2)}) copy-start(bf16[4096]{0:T(1024)(128)(2,1)} %param.15) | copy-start | bytes 24580
  37.3 42.3 %copy-start.7 = (s32[16]{0:T(128)S(1)}, s32[16]{0:T(128)}, u32[]{:S(2)}) copy-start(s32[16]{0:T(128)} %param.17) | copy-start | bytes 196
  37.3 42.4 %copy-start.6 = (s32[16]{0:T(128)S(1)}, s32[16]{0:T(128)}, u32[]{:S(2)}) copy-start(s32[16]{0:T(128)} %param.16) | copy-start | bytes 196
  37.3 36.5 %collective-permute-start.2 = (bf16[16,128,256]{2,1,0:T(8,128)(2,1)}, bf16[16,128,256]{2,1,0:T(8,128)(2,1)S(1)}, u32[]{:S(2)}, u32[]{:S(2)}) collective-permute-start(bf16[16,128,256]{2,1,0:T(8,128)(2,1)} %shard_map.104.hi_ref), channel_id=1, source_target_pairs={{0,1},{1,2},{2,3},{3,4},{4,5},{5,6},{6,7},{7,8},{8,9},{9,10},{10,1... | collective-permute-start | bytes 3145736 | tf_op jit(solution)/shard_map/ppermute | solution.py:16
  73.8 1.0 copy-start.3
  73.8 29.9 %copy-start.1 = (bf16[16,128,256]{2,1,0:T(8,128)(2,1)}, bf16[16,128,256]{2,1,0:T(8,128)(2,1)S(1)}, u32[]{:S(2)}) copy-start(bf16[16,128,256]{2,1,0:T(8,128)(2,1)S(1)} %all-to-all-done.hi_ref) | copy-start | bytes 3145732
  74.7 29.4 %all-to-all-start.1 = ((bf16[16,128,256]{2,1,0:T(8,128)(2,1)}), bf16[16,128,256]{2,1,0:T(8,128)(2,1)S(1)}, u32[]{:S(2)}, u32[]{:S(2)}) async-start(bf16[16,128,256]{2,1,0:T(8,128)(2,1)} %shard_map.105.lo_ref), calls=%async_computation.1 | async-start | bytes 2097152 | tf_op jit(solution)/shard_map/all_to_all | solution.py:274
  104.1 1.0 copy-start.2

commit v11 on v9

--- a/solution.py
+++ b/solution.py
@@ -188,13 +188,13 @@
     tail_len = out_ref.shape[0]
     total = z_all.shape[0]
     for src in range(shards):
-        z_all[2 * src * blk : (2 * src + 1) * blk, :] = lo_ref[src].astype(jnp.float32)
-        z_all[(2 * src + 1) * blk : (2 * src + 2) * blk, :] = hi_ref[src].astype(jnp.float32)
+        z_all[2 * src * blk : (2 * src + 1) * blk, :] = lo_ref[src]
+        z_all[(2 * src + 1) * blk : (2 * src + 2) * blk, :] = hi_ref[src]
     for t in range(out_ref.shape[1]):
         begin = begin_ref[t]
         start = jnp.clip((begin // 16) * 16, 0, total - WINDOW)
         shift = begin - start
-        window = z_all[pl.ds(pl.multiple_of(start, 16), WINDOW), :]
+        window = z_all[pl.ds(pl.multiple_of(start, 16), WINDOW), :].astype(jnp.float32)
         moved = pltpu.roll(window, (WINDOW - shift) % WINDOW, 0)[:tail_len]
         pos = begin + lax.broadcasted_iota(jnp.int32, (tail_len, 1), 0)
         out_ref[:, t, :] = jnp.where(pos >= first_ref[t], moved, 0.0).astype(out_ref.dtype)
@@ -210,7 +210,7 @@
         in_specs=[smem, smem, vmem, vmem],
         out_specs=vmem,
         out_shape=jax.ShapeDtypeStruct((tail_len, count, lanes), z_lo.dtype),
-        scratch_shapes=[pltpu.VMEM((2 * shards * blk, lanes), jnp.float32)],
+        scratch_shapes=[pltpu.VMEM((2 * shards * blk, lanes), z_lo.dtype)],
     )(begins, firsts, z_lo, z_hi)
     return jnp.transpose(out, (1, 0, 2))
 

time: 112 us -> 112 us (level)
  no operation moved by 1% of the time
where the time goes in v11:
time: 112 us; the launch traced here: 111 us
  Pallas kernels  70.2 us (63%)
  starting transfers between devices  17.1 us (15%)
  waiting for transfers between devices  13.4 us (12%)
  local copies, waits for them, and re-layouts  5.93 us (5%)
  other arithmetic  3.25 us (3%)
    pallas_call x2, Pallas kernels, short_chain(): pl.pallas_call(functools.partial(chain_kernel, group_ch=channels // se_fi...  42.9 us
    pallas_call x1, Pallas kernels, long_conv_out(): pl.pallas_call(long_kernel, grid=(steps,), in_specs=[pl.BlockSpec(rel.sha...  21.8 us
    ppermute x3, waiting for transfers between devices, passed_along(): return lax.ppermute(x, axis, pairs)  12.8 us
    ppermute x3, starting transfers between devices, passed_along(): return lax.ppermute(x, axis, pairs)  7.64 us
    pallas_call x1, Pallas kernels, cut_tails_all(): pl.pallas_call(tail_kernel, in_specs=[smem, smem, vmem, vmem], out_specs=...  5.55 us
    all_to_all x1, starting transfers between devices, local(): lax.all_to_all(z_hi, 'seq', split_axis=0, concat_axis=0, tiled=True)  5.24 us
    all_to_all x1, starting transfers between devices, local(): lax.all_to_all(z_lo, 'seq', split_axis=0, concat_axis=0, tiled=True)  4.22 us
  transfers between devices with their start and end apart: 5, of which 2 were waited for; matrix products, arithmetic and copies ran while one was open for 5% of the time, Pallas kernels for 58%

profile of v11, /device:TPU:18, one launch (start us, length us, event | category | flops | bytes accessed | tf_op | source)
XLA Modules:
  0.0 110.6 jit_solution(13118195939604973977)
XLA Ops:
  0.6 1.2 %slice.6 = bf16[18,12288]{1,0:T(8,128)(2,1)S(1)} slice(bf16[256,12288]{1,0:T(8,128)(2,1)} %sv.3), slice={[238:256], [0:12288]} | slice | bytes 884736 | tf_op jit(solution)/shard_map/slice | solution.py:245
  1.8 1.9 %collective-permute-start = (bf16[18,12288]{1,0:T(8,128)(2,1)S(1)}, bf16[18,12288]{1,0:T(8,128)(2,1)S(1)}, u32[]{:S(2)}, u32[]{:S(2)}) collective-permute-start(bf16[18,12288]{1,0:T(8,128)(2,1)S(1)} %slice.6), channel_id=1, source_target_pairs={{0,1},{1,2},{2,3},{3,4},{4,5},{5,6},{6,7},{7,8},{8,9},{9,10},{10,1... | collective-permute-start | bytes 1327112 | tf_op jit(solution)/shard_map/ppermute | solution.py:16
  3.8 0.9 slice.7
  4.7 3.5 %collective-permute-start.1 = (bf16[6,8192]{1,0:T(8,128)(2,1)S(1)}, bf16[6,8192]{1,0:T(8,128)(2,1)S(1)}, u32[]{:S(2)}, u32[]{:S(2)}) collective-permute-start(bf16[6,8192]{1,0:T(8,128)(2,1)S(1)} %slice.7), channel_id=1, source_target_pairs={{0,1},{1,2},{2,3},{3,4},{4,5},{5,6},{6,7},{7,8},{8,9},{9,10},{10,1... | collective-permute-start | bytes 294920 | tf_op jit(solution)/shard_map/ppermute | solution.py:16
  8.3 0.7 convert_reduce_fusion
  9.0 0.7 select_reduce_fusion
  9.8 0.8 sub.30.rel_ref
  10.6 21.4 %shard_map.104.hi_ref = bf16[16,128,256]{2,1,0:T(8,128)(2,1)} custom-call(s32[384,1]{1,0:T(8,128)} %sub.30.rel_ref, bf16[256,12288]{1,0:T(8,128)(2,1)} %sv.3, bf16[256,12288]{1,0:T(8,128)(2,1)} %sv.3, bf16[256,12288]{1,0:T(8,128)(2,1)} %sv.3, bf16[256,12288]{1,0:T(8,128)(2,1)} %sv.3, bf16[256,12288]{1,0:T(8,128)(2,1)} %sv.3, bf16[256,12288]{1,0:T(8,128)(2,1)} %sv.3, ...), custom_call_target="tpu_custom_call" | custom-call | tf_op jit(solution)/shard_map/pallas_call | solution.py:107
  32.0 0.0 collective-permute-done.1.gk_h.mh_ref
  32.0 0.0 copy-start.4
  32.0 0.0 collective-permute-done.hq.hk.hv
  32.0 0.0 copy-start
  32.0 5.2 %all-to-all-start = ((bf16[16,128,256]{2,1,0:T(8,128)(2,1)}), bf16[16,128,256]{2,1,0:T(8,128)(2,1)S(1)}, u32[]{:S(2)}, u32[]{:S(2)}) async-start(bf16[16,128,256]{2,1,0:T(8,128)(2,1)} %shard_map.104.hi_ref), calls=%async_computation | async-start | bytes 2097152 | tf_op jit(solution)/shard_map/all_to_all | solution.py:257
  37.3 0.0 copy-start.5
  37.3 0.0 copy-start.6
  37.3 0.0 copy-start.8
  37.3 0.0 copy-start.7
  37.3 2.2 %collective-permute-start.2 = (bf16[16,128,256]{2,1,0:T(8,128)(2,1)}, bf16[16,128,256]{2,1,0:T(8,128)(2,1)S(1)}, u32[]{:S(2)}, u32[]{:S(2)}) collective-permute-start(bf16[16,128,256]{2,1,0:T(8,128)(2,1)} %shard_map.104.hi_ref), channel_id=1, source_target_pairs={{0,1},{1,2},{2,3},{3,4},{4,5},{5,6},{6,7},{7,8},{8,9},{9,10},{10,1... | collective-permute-start | bytes 3145736 | tf_op jit(solution)/shard_map/ppermute | solution.py:16
  39.5 0.0 copy-done.4
  39.5 0.0 copy-done
  39.5 21.5 %shard_map.105.lo_ref = bf16[16,128,256]{2,1,0:T(8,128)(2,1)} custom-call(s32[384,1]{1,0:T(8,128)} %sub.30.rel_ref, bf16[256,12288]{1,0:T(8,128)(2,1)} %sv.3, bf16[256,12288]{1,0:T(8,128)(2,1)} %sv.3, bf16[256,12288]{1,0:T(8,128)(2,1)} %sv.3, bf16[18,12288]{1,0:T(8,128)(2,1)} %copy-done, bf16[18,12288]{1,0:T(8,128)(2,1)} %copy-done, ...), custom_call_target="tpu_custom_call" | custom-call | tf_op jit(solution)/shard_map/pallas_call | solution.py:107
  61.0 12.8 %collective-permute-done.2.prev_ref = bf16[16,128,256]{2,1,0:T(8,128)(2,1)S(1)} collective-permute-done((bf16[16,128,256]{2,1,0:T(8,128)(2,1)}, bf16[16,128,256]{2,1,0:T(8,128)(2,1)S(1)}, u32[]{:S(2)}, u32[]{:S(2)}) %collective-permute-start.2) | collective-permute-done | bytes 1048608 | tf_op jit(solution)/shard_map/ppermute | solution.py:16
  73.7 0.0 copy-start.3
  73.8 0.0 all-to-all-done.hi_ref
  73.8 0.0 copy-start.1
  73.8 1.0 copy-done.3
  74.7 4.2 %all-to-all-start.1 = ((bf16[16,128,256]{2,1,0:T(8,128)(2,1)}), bf16[16,128,256]{2,1,0:T(8,128)(2,1)S(1)}, u32[]{:S(2)}, u32[]{:S(2)}) async-start(bf16[16,128,256]{2,1,0:T(8,128)(2,1)} %shard_map.105.lo_ref), calls=%async_computation.1 | async-start | bytes 2097152 | tf_op jit(solution)/shard_map/all_to_all | solution.py:262
  79.0 0.0 copy-done.5
  79.0 0.1 copy.18
  79.1 0.2 rev.3
  79.3 0.1 pad.2.clone
  79.4 0.0 copy-done.6
  79.4 0.6 broadcast_in_dim.65.skip_ref
  80.0 0.0 copy-done.8
  80.0 0.1 select_reduce_fusion.3
  80.1 0.0 copy-done.7
  80.1 0.2 select_reduce_fusion.1
  80.3 0.6 compare_select_fusion
  80.9 0.8 maximum_maximum_fusion.u_ref
  81.8 21.8 %shard_map.106 = bf16[256,4096]{1,0:T(8,128)(2,1)} custom-call(s32[384,1]{1,0:T(8,128)} %sub.30.rel_ref, bf16[256,8192]{1,0:T(8,128)(2,1)} %mg_ref.1, bf16[6,8192]{1,0:T(8,128)(2,1)} %copy-done.4, bf16[7,12288]{1,0:T(8,128)(2,1)} %wq_ref.1, bf16[16,128,256]{2,1,0:T(8,128)(2,1)} %copy-done.3, bf16[16,128,256]{2,1,0:T(8,128)(2,1)} %shard_map.105.lo_ref, ...), custom_call_target="tpu_custom_call" | custom-call | tf_op jit(solution)/shard_map/pallas_call | solution.py:166
  103.5 0.0 copy-done.1
  103.5 0.6 all-to-all-done.1.lo_ref
  104.1 0.0 copy-start.2
  104.1 1.0 copy-done.2
  105.1 5.5 %shard_map.107 = bf16[127,16,256]{2,1,0:T(8,128)(2,1)} custom-call(s32[16]{0:T(128)} %get-tuple-element.17.begin_ref, s32[16]{0:T(128)} %get-tuple-element.16.first_ref, bf16[16,128,256]{2,1,0:T(8,128)(2,1)} %copy-done.2, bf16[16,128,256]{2,1,0:T(8,128)(2,1)} %copy-done.1), custom_call_target="tpu_custom_call" | custom-call | tf_op jit(solution)/shard_map/pallas_call | solution.py:208
  (7 shorter events, 0.0 us)
Async XLA Ops:
  1.8 30.2 %collective-permute-start = (bf16[18,12288]{1,0:T(8,128)(2,1)S(1)}, bf16[18,12288]{1,0:T(8,128)(2,1)S(1)}, u32[]{:S(2)}, u32[]{:S(2)}) collective-permute-start(bf16[18,12288]{1,0:T(8,128)(2,1)S(1)} %slice.6), channel_id=1, source_target_pairs={{0,1},{1,2},{2,3},{3,4},{4,5},{5,6},{6,7},{7,8},{8,9},{9,10},{10,1... | collective-permute-start | bytes 1327112 | tf_op jit(solution)/shard_map/ppermute | solution.py:16
  4.7 27.3 %collective-permute-start.1 = (bf16[6,8192]{1,0:T(8,128)(2,1)S(1)}, bf16[6,8192]{1,0:T(8,128)(2,1)S(1)}, u32[]{:S(2)}, u32[]{:S(2)}) collective-permute-start(bf16[6,8192]{1,0:T(8,128)(2,1)S(1)} %slice.7), channel_id=1, source_target_pairs={{0,1},{1,2},{2,3},{3,4},{4,5},{5,6},{6,7},{7,8},{8,9},{9,10},{10,1... | collective-permute-start | bytes 294920 | tf_op jit(solution)/shard_map/ppermute | solution.py:16
  32.0 7.5 %copy-start.4 = (bf16[6,8192]{1,0:T(8,128)(2,1)}, bf16[6,8192]{1,0:T(8,128)(2,1)S(1)}, u32[]{:S(2)}) copy-start(bf16[6,8192]{1,0:T(8,128)(2,1)S(1)} %collective-permute-done.1.gk_h.mh_ref) | copy-start | bytes 294916
  32.0 7.5 %copy-start = (bf16[18,12288]{1,0:T(8,128)(2,1)}, bf16[18,12288]{1,0:T(8,128)(2,1)S(1)}, u32[]{:S(2)}) copy-start(bf16[18,12288]{1,0:T(8,128)(2,1)S(1)} %collective-permute-done.hq.hk.hv) | copy-start | bytes 1327108
  32.0 41.7 %all-to-all-start = ((bf16[16,128,256]{2,1,0:T(8,128)(2,1)}), bf16[16,128,256]{2,1,0:T(8,128)(2,1)S(1)}, u32[]{:S(2)}, u32[]{:S(2)}) async-start(bf16[16,128,256]{2,1,0:T(8,128)(2,1)} %shard_map.104.hi_ref), calls=%async_computation | async-start | bytes 2097152 | tf_op jit(solution)/shard_map/all_to_all | solution.py:257
  37.3 41.7 %copy-start.5 = (bf16[128,256]{1,0:T(8,128)(2,1)S(1)}, bf16[128,256]{1,0:T(8,128)(2,1)}, u32[]{:S(2)}) copy-start(bf16[128,256]{1,0:T(8,128)(2,1)} %param.14) | copy-start | bytes 196612
  37.3 42.1 %copy-start.6 = (bf16[4096]{0:T(1024)(128)(2,1)S(1)}, bf16[4096]{0:T(1024)(128)(2,1)}, u32[]{:S(2)}) copy-start(bf16[4096]{0:T(1024)(128)(2,1)} %param.15) | copy-start | bytes 24580
  37.3 42.7 %copy-start.8 = (s32[16]{0:T(128)S(1)}, s32[16]{0:T(128)}, u32[]{:S(2)}) copy-start(s32[16]{0:T(128)} %param.17) | copy-start | bytes 196
  37.3 42.8 %copy-start.7 = (s32[16]{0:T(128)S(1)}, s32[16]{0:T(128)}, u32[]{:S(2)}) copy-start(s32[16]{0:T(128)} %param.16) | copy-start | bytes 196
  37.3 36.5 %collective-permute-start.2 = (bf16[16,128,256]{2,1,0:T(8,128)(2,1)}, bf16[16,128,256]{2,1,0:T(8,128)(2,1)S(1)}, u32[]{:S(2)}, u32[]{:S(2)}) collective-permute-start(bf16[16,128,256]{2,1,0:T(8,128)(2,1)} %shard_map.104.hi_ref), channel_id=1, source_target_pairs={{0,1},{1,2},{2,3},{3,4},{4,5},{5,6},{6,7},{7,8},{8,9},{9,10},{10,1... | collective-permute-start | bytes 3145736 | tf_op jit(solution)/shard_map/ppermute | solution.py:16
  73.7 1.0 copy-start.3
  73.8 29.8 %copy-start.1 = (bf16[16,128,256]{2,1,0:T(8,128)(2,1)}, bf16[16,128,256]{2,1,0:T(8,128)(2,1)S(1)}, u32[]{:S(2)}) copy-start(bf16[16,128,256]{2,1,0:T(8,128)(2,1)S(1)} %all-to-all-done.hi_ref) | copy-start | bytes 3145732
  74.7 29.4 %all-to-all-start.1 = ((bf16[16,128,256]{2,1,0:T(8,128)(2,1)}), bf16[16,128,256]{2,1,0:T(8,128)(2,1)S(1)}, u32[]{:S(2)}, u32[]{:S(2)}) async-start(bf16[16,128,256]{2,1,0:T(8,128)(2,1)} %shard_map.105.lo_ref), calls=%async_computation.1 | async-start | bytes 2097152 | tf_op jit(solution)/shard_map/all_to_all | solution.py:262
  104.1 1.0 copy-start.2

commit v12 on v11

--- a/solution.py
+++ b/solution.py
@@ -138,6 +138,7 @@
         lax.broadcasted_iota(jnp.int32, (1, width), 1) + b * blk >= rel_ref[(b + 1) * blk : (b + 2) * blk, :]
         for b in range(2)
     ]
+    keep = [m.astype(jnp.bfloat16) for m in masks]
     lane_grp = lax.broadcasted_iota(jnp.int32, (1, GROUP_LANES), 1) // per_group
     halves = tile // GROUP_LANES
     groups_half = GROUP_LANES // per_group
@@ -145,9 +146,9 @@
     for g in range(u_ref.shape[0]):
         half = g // groups_half
         row = jnp.broadcast_to(u_ref[g : g + 1, :], (blk, width))
-        taps = pltpu.roll(row, 0, 1, stride=1, stride_axis=0)
+        taps = pltpu.roll(row, 0, 1, stride=1, stride_axis=0).astype(jnp.bfloat16)
         for b in range(2):
-            mat = jnp.where(masks[b], taps, 0.0).astype(jnp.bfloat16)
+            mat = taps * keep[b]
             part = windows[b][:, half * GROUP_LANES : (half + 1) * GROUP_LANES]
             res = jnp.dot(mat, part, preferred_element_type=jnp.float32)
             acc[b][half] = jnp.where(lane_grp == g % groups_half, res, acc[b][half])

time: 112 us -> 112 us (level)
  transfers between devices with their start and end apart: 5 -> 5, of which waited for: 2 -> 2; matrix products, arithmetic and copies ran while one was open for 5% -> 5% of each run, Pallas kernels for 58% -> 59%
where the time goes in v12:
time: 112 us; the launch traced here: 111 us
  Pallas kernels  70.3 us (63%)
  starting transfers between devices  17.1 us (15%)
  waiting for transfers between devices  13.3 us (12%)
  local copies, waits for them, and re-layouts  5.93 us (5%)
  other arithmetic  3.25 us (3%)
    pallas_call x2, Pallas kernels, short_chain(): pl.pallas_call(functools.partial(chain_kernel, group_ch=channels // se_fi...  42.9 us
    pallas_call x1, Pallas kernels, long_conv_out(): pl.pallas_call(long_kernel, grid=(steps,), in_specs=[pl.BlockSpec(rel.sha...  21.9 us
    ppermute x3, waiting for transfers between devices, passed_along(): return lax.ppermute(x, axis, pairs)  12.8 us
    ppermute x3, starting transfers between devices, passed_along(): return lax.ppermute(x, axis, pairs)  7.64 us
    pallas_call x1, Pallas kernels, cut_tails_all(): pl.pallas_call(tail_kernel, in_specs=[smem, smem, vmem, vmem], out_specs=...  5.54 us
    all_to_all x1, starting transfers between devices, local(): lax.all_to_all(z_hi, 'seq', split_axis=0, concat_axis=0, tiled=True)  5.24 us
    all_to_all x1, starting transfers between devices, local(): lax.all_to_all(z_lo, 'seq', split_axis=0, concat_axis=0, tiled=True)  4.22 us
  transfers between devices with their start and end apart: 5, of which 2 were waited for; matrix products, arithmetic and copies ran while one was open for 5% of the time, Pallas kernels for 59%

profile of v12, /device:TPU:18, one launch (start us, length us, event | category | flops | bytes accessed | tf_op | source)
XLA Modules:
  0.0 110.6 jit_solution(927355630956885112)
XLA Ops:
  0.6 1.2 %slice.6 = bf16[18,12288]{1,0:T(8,128)(2,1)S(1)} slice(bf16[256,12288]{1,0:T(8,128)(2,1)} %sv.3), slice={[238:256], [0:12288]} | slice | bytes 884736 | tf_op jit(solution)/shard_map/slice | solution.py:246
  1.8 1.9 %collective-permute-start = (bf16[18,12288]{1,0:T(8,128)(2,1)S(1)}, bf16[18,12288]{1,0:T(8,128)(2,1)S(1)}, u32[]{:S(2)}, u32[]{:S(2)}) collective-permute-start(bf16[18,12288]{1,0:T(8,128)(2,1)S(1)} %slice.6), channel_id=1, source_target_pairs={{0,1},{1,2},{2,3},{3,4},{4,5},{5,6},{6,7},{7,8},{8,9},{9,10},{10,1... | collective-permute-start | bytes 1327112 | tf_op jit(solution)/shard_map/ppermute | solution.py:16
  3.8 0.9 slice.7
  4.7 3.5 %collective-permute-start.1 = (bf16[6,8192]{1,0:T(8,128)(2,1)S(1)}, bf16[6,8192]{1,0:T(8,128)(2,1)S(1)}, u32[]{:S(2)}, u32[]{:S(2)}) collective-permute-start(bf16[6,8192]{1,0:T(8,128)(2,1)S(1)} %slice.7), channel_id=1, source_target_pairs={{0,1},{1,2},{2,3},{3,4},{4,5},{5,6},{6,7},{7,8},{8,9},{9,10},{10,1... | collective-permute-start | bytes 294920 | tf_op jit(solution)/shard_map/ppermute | solution.py:16
  8.3 0.7 convert_reduce_fusion
  9.0 0.7 select_reduce_fusion
  9.8 0.8 sub.30.rel_ref
  10.6 21.4 %shard_map.104.hi_ref = bf16[16,128,256]{2,1,0:T(8,128)(2,1)} custom-call(s32[384,1]{1,0:T(8,128)} %sub.30.rel_ref, bf16[256,12288]{1,0:T(8,128)(2,1)} %sv.3, bf16[256,12288]{1,0:T(8,128)(2,1)} %sv.3, bf16[256,12288]{1,0:T(8,128)(2,1)} %sv.3, bf16[256,12288]{1,0:T(8,128)(2,1)} %sv.3, bf16[256,12288]{1,0:T(8,128)(2,1)} %sv.3, bf16[256,12288]{1,0:T(8,128)(2,1)} %sv.3, ...), custom_call_target="tpu_custom_call" | custom-call | tf_op jit(solution)/shard_map/pallas_call | solution.py:107
  32.0 0.0 collective-permute-done.1.gk_h.mh_ref
  32.0 0.0 copy-start.4
  32.0 0.0 collective-permute-done.hq.hk.hv
  32.0 0.0 copy-start
  32.0 5.2 %all-to-all-start = ((bf16[16,128,256]{2,1,0:T(8,128)(2,1)}), bf16[16,128,256]{2,1,0:T(8,128)(2,1)S(1)}, u32[]{:S(2)}, u32[]{:S(2)}) async-start(bf16[16,128,256]{2,1,0:T(8,128)(2,1)} %shard_map.104.hi_ref), calls=%async_computation | async-start | bytes 2097152 | tf_op jit(solution)/shard_map/all_to_all | solution.py:258
  37.3 0.0 copy-start.5
  37.3 0.0 copy-start.6
  37.3 0.0 copy-start.8
  37.3 0.0 copy-start.7
  37.3 2.2 %collective-permute-start.2 = (bf16[16,128,256]{2,1,0:T(8,128)(2,1)}, bf16[16,128,256]{2,1,0:T(8,128)(2,1)S(1)}, u32[]{:S(2)}, u32[]{:S(2)}) collective-permute-start(bf16[16,128,256]{2,1,0:T(8,128)(2,1)} %shard_map.104.hi_ref), channel_id=1, source_target_pairs={{0,1},{1,2},{2,3},{3,4},{4,5},{5,6},{6,7},{7,8},{8,9},{9,10},{10,1... | collective-permute-start | bytes 3145736 | tf_op jit(solution)/shard_map/ppermute | solution.py:16
  39.5 0.0 copy-done.4
  39.5 0.0 copy-done
  39.5 21.5 %shard_map.105.lo_ref = bf16[16,128,256]{2,1,0:T(8,128)(2,1)} custom-call(s32[384,1]{1,0:T(8,128)} %sub.30.rel_ref, bf16[256,12288]{1,0:T(8,128)(2,1)} %sv.3, bf16[256,12288]{1,0:T(8,128)(2,1)} %sv.3, bf16[256,12288]{1,0:T(8,128)(2,1)} %sv.3, bf16[18,12288]{1,0:T(8,128)(2,1)} %copy-done, bf16[18,12288]{1,0:T(8,128)(2,1)} %copy-done, ...), custom_call_target="tpu_custom_call" | custom-call | tf_op jit(solution)/shard_map/pallas_call | solution.py:107
  61.0 12.8 %collective-permute-done.2.prev_ref = bf16[16,128,256]{2,1,0:T(8,128)(2,1)S(1)} collective-permute-done((bf16[16,128,256]{2,1,0:T(8,128)(2,1)}, bf16[16,128,256]{2,1,0:T(8,128)(2,1)S(1)}, u32[]{:S(2)}, u32[]{:S(2)}) %collective-permute-start.2) | collective-permute-done | bytes 1048608 | tf_op jit(solution)/shard_map/ppermute | solution.py:16
  73.7 0.0 copy-start.3
  73.8 0.0 all-to-all-done.hi_ref
  73.8 0.0 copy-start.1
  73.8 1.0 copy-done.3
  74.7 4.2 %all-to-all-start.1 = ((bf16[16,128,256]{2,1,0:T(8,128)(2,1)}), bf16[16,128,256]{2,1,0:T(8,128)(2,1)S(1)}, u32[]{:S(2)}, u32[]{:S(2)}) async-start(bf16[16,128,256]{2,1,0:T(8,128)(2,1)} %shard_map.105.lo_ref), calls=%async_computation.1 | async-start | bytes 2097152 | tf_op jit(solution)/shard_map/all_to_all | solution.py:263
  79.0 0.0 copy-done.5
  79.0 0.1 copy.18
  79.1 0.2 rev.3
  79.3 0.1 pad.2.clone
  79.4 0.0 copy-done.6
  79.4 0.6 broadcast_in_dim.65.skip_ref
  80.0 0.0 copy-done.8
  80.0 0.1 select_reduce_fusion.3
  80.1 0.0 copy-done.7
  80.1 0.2 select_reduce_fusion.1
  80.3 0.6 compare_select_fusion
  80.9 0.8 maximum_maximum_fusion.u_ref
  81.8 21.9 %shard_map.106 = bf16[256,4096]{1,0:T(8,128)(2,1)} custom-call(s32[384,1]{1,0:T(8,128)} %sub.30.rel_ref, bf16[256,8192]{1,0:T(8,128)(2,1)} %mg_ref.1, bf16[6,8192]{1,0:T(8,128)(2,1)} %copy-done.4, bf16[7,12288]{1,0:T(8,128)(2,1)} %wq_ref.1, bf16[16,128,256]{2,1,0:T(8,128)(2,1)} %copy-done.3, bf16[16,128,256]{2,1,0:T(8,128)(2,1)} %shard_map.105.lo_ref, ...), custom_call_target="tpu_custom_call" | custom-call | tf_op jit(solution)/shard_map/pallas_call | solution.py:167
  103.6 0.0 copy-done.1
  103.6 0.5 all-to-all-done.1.lo_ref
  104.1 0.0 copy-start.2
  104.1 1.0 copy-done.2
  105.1 5.5 %shard_map.107 = bf16[127,16,256]{2,1,0:T(8,128)(2,1)} custom-call(s32[16]{0:T(128)} %get-tuple-element.17.begin_ref, s32[16]{0:T(128)} %get-tuple-element.16.first_ref, bf16[16,128,256]{2,1,0:T(8,128)(2,1)} %copy-done.2, bf16[16,128,256]{2,1,0:T(8,128)(2,1)} %copy-done.1), custom_call_target="tpu_custom_call" | custom-call | tf_op jit(solution)/shard_map/pallas_call | solution.py:209
  (7 shorter events, 0.0 us)
Async XLA Ops:
  1.8 30.2 %collective-permute-start = (bf16[18,12288]{1,0:T(8,128)(2,1)S(1)}, bf16[18,12288]{1,0:T(8,128)(2,1)S(1)}, u32[]{:S(2)}, u32[]{:S(2)}) collective-permute-start(bf16[18,12288]{1,0:T(8,128)(2,1)S(1)} %slice.6), channel_id=1, source_target_pairs={{0,1},{1,2},{2,3},{3,4},{4,5},{5,6},{6,7},{7,8},{8,9},{9,10},{10,1... | collective-permute-start | bytes 1327112 | tf_op jit(solution)/shard_map/ppermute | solution.py:16
  4.7 27.3 %collective-permute-start.1 = (bf16[6,8192]{1,0:T(8,128)(2,1)S(1)}, bf16[6,8192]{1,0:T(8,128)(2,1)S(1)}, u32[]{:S(2)}, u32[]{:S(2)}) collective-permute-start(bf16[6,8192]{1,0:T(8,128)(2,1)S(1)} %slice.7), channel_id=1, source_target_pairs={{0,1},{1,2},{2,3},{3,4},{4,5},{5,6},{6,7},{7,8},{8,9},{9,10},{10,1... | collective-permute-start | bytes 294920 | tf_op jit(solution)/shard_map/ppermute | solution.py:16
  32.0 7.5 %copy-start.4 = (bf16[6,8192]{1,0:T(8,128)(2,1)}, bf16[6,8192]{1,0:T(8,128)(2,1)S(1)}, u32[]{:S(2)}) copy-start(bf16[6,8192]{1,0:T(8,128)(2,1)S(1)} %collective-permute-done.1.gk_h.mh_ref) | copy-start | bytes 294916
  32.0 7.5 %copy-start = (bf16[18,12288]{1,0:T(8,128)(2,1)}, bf16[18,12288]{1,0:T(8,128)(2,1)S(1)}, u32[]{:S(2)}) copy-start(bf16[18,12288]{1,0:T(8,128)(2,1)S(1)} %collective-permute-done.hq.hk.hv) | copy-start | bytes 1327108
  32.0 41.7 %all-to-all-start = ((bf16[16,128,256]{2,1,0:T(8,128)(2,1)}), bf16[16,128,256]{2,1,0:T(8,128)(2,1)S(1)}, u32[]{:S(2)}, u32[]{:S(2)}) async-start(bf16[16,128,256]{2,1,0:T(8,128)(2,1)} %shard_map.104.hi_ref), calls=%async_computation | async-start | bytes 2097152 | tf_op jit(solution)/shard_map/all_to_all | solution.py:258
  37.3 41.7 %copy-start.5 = (bf16[128,256]{1,0:T(8,128)(2,1)S(1)}, bf16[128,256]{1,0:T(8,128)(2,1)}, u32[]{:S(2)}) copy-start(bf16[128,256]{1,0:T(8,128)(2,1)} %param.14) | copy-start | bytes 196612
  37.3 42.1 %copy-start.6 = (bf16[4096]{0:T(1024)(128)(2,1)S(1)}, bf16[4096]{0:T(1024)(128)(2,1)}, u32[]{:S(2)}) copy-start(bf16[4096]{0:T(1024)(128)(2,1)} %param.15) | copy-start | bytes 24580
  37.3 42.7 %copy-start.8 = (s32[16]{0:T(128)S(1)}, s32[16]{0:T(128)}, u32[]{:S(2)}) copy-start(s32[16]{0:T(128)} %param.17) | copy-start | bytes 196
  37.3 42.8 %copy-start.7 = (s32[16]{0:T(128)S(1)}, s32[16]{0:T(128)}, u32[]{:S(2)}) copy-start(s32[16]{0:T(128)} %param.16) | copy-start | bytes 196
  37.3 36.5 %collective-permute-start.2 = (bf16[16,128,256]{2,1,0:T(8,128)(2,1)}, bf16[16,128,256]{2,1,0:T(8,128)(2,1)S(1)}, u32[]{:S(2)}, u32[]{:S(2)}) collective-permute-start(bf16[16,128,256]{2,1,0:T(8,128)(2,1)} %shard_map.104.hi_ref), channel_id=1, source_target_pairs={{0,1},{1,2},{2,3},{3,4},{4,5},{5,6},{6,7},{7,8},{8,9},{9,10},{10,1... | collective-permute-start | bytes 3145736 | tf_op jit(solution)/shard_map/ppermute | solution.py:16
  73.7 1.0 copy-start.3
  73.8 29.9 %copy-start.1 = (bf16[16,128,256]{2,1,0:T(8,128)(2,1)}, bf16[16,128,256]{2,1,0:T(8,128)(2,1)S(1)}, u32[]{:S(2)}) copy-start(bf16[16,128,256]{2,1,0:T(8,128)(2,1)S(1)} %all-to-all-done.hi_ref) | copy-start | bytes 3145732
  74.7 29.4 %all-to-all-start.1 = ((bf16[16,128,256]{2,1,0:T(8,128)(2,1)}), bf16[16,128,256]{2,1,0:T(8,128)(2,1)S(1)}, u32[]{:S(2)}, u32[]{:S(2)}) async-start(bf16[16,128,256]{2,1,0:T(8,128)(2,1)} %shard_map.105.lo_ref), calls=%async_computation.1 | async-start | bytes 2097152 | tf_op jit(solution)/shard_map/all_to_all | solution.py:263
  104.1 1.0 copy-start.2

commit v13 on v11

--- a/solution.py
+++ b/solution.py
@@ -216,9 +216,8 @@
 
 
 def seg_start(positions, req_ends):
-    seg = request_of(positions, req_ends)
-    prev_end = jnp.where(seg > 0, pick_entries(req_ends, jnp.maximum(seg - 1, 0)), -1)
-    return prev_end + 1
+    before = req_ends[None, :] < positions[:, None]
+    return jnp.max(jnp.where(before, req_ends[None, :] + 1, 0), axis=1)
 
 
 def pick_entries(lookup_table, indices):

time: 112 us -> 112 us (level)
  no operation moved by 1% of the time
where the time goes in v13:
time: 112 us; the launch traced here: 111 us
  Pallas kernels  70.2 us (63%)
  starting transfers between devices  17.1 us (15%)
  waiting for transfers between devices  13.4 us (12%)
  local copies, waits for them, and re-layouts  5.94 us (5%)
  other arithmetic  3.15 us (3%)
    pallas_call x2, Pallas kernels, short_chain(): pl.pallas_call(functools.partial(chain_kernel, group_ch=channels // se_fi...  42.9 us
    pallas_call x1, Pallas kernels, long_conv_out(): pl.pallas_call(long_kernel, grid=(steps,), in_specs=[pl.BlockSpec(rel.sha...  21.7 us
    ppermute x3, waiting for transfers between devices, passed_along(): return lax.ppermute(x, axis, pairs)  12.8 us
    ppermute x3, starting transfers between devices, passed_along(): return lax.ppermute(x, axis, pairs)  7.64 us
    pallas_call x1, Pallas kernels, cut_tails_all(): pl.pallas_call(tail_kernel, in_specs=[smem, smem, vmem, vmem], out_specs=...  5.54 us
    all_to_all x1, starting transfers between devices, local(): lax.all_to_all(z_hi, 'seq', split_axis=0, concat_axis=0, tiled=True)  5.24 us
    all_to_all x1, starting transfers between devices, local(): lax.all_to_all(z_lo, 'seq', split_axis=0, concat_axis=0, tiled=True)  4.22 us
  transfers between devices with their start and end apart: 5, of which 2 were waited for; matrix products, arithmetic and copies ran while one was open for 5% of the time, Pallas kernels for 58%

profile of v13, /device:TPU:18, one launch (start us, length us, event | category | flops | bytes accessed | tf_op | source)
XLA Modules:
  0.0 110.6 jit_solution(14290538412672728161)
XLA Ops:
  0.6 1.2 %slice.6 = bf16[18,12288]{1,0:T(8,128)(2,1)S(1)} slice(bf16[256,12288]{1,0:T(8,128)(2,1)} %sv.3), slice={[238:256], [0:12288]} | slice | bytes 884736 | tf_op jit(solution)/shard_map/slice | solution.py:244
  1.8 1.9 %collective-permute-start = (bf16[18,12288]{1,0:T(8,128)(2,1)S(1)}, bf16[18,12288]{1,0:T(8,128)(2,1)S(1)}, u32[]{:S(2)}, u32[]{:S(2)}) collective-permute-start(bf16[18,12288]{1,0:T(8,128)(2,1)S(1)} %slice.6), channel_id=1, source_target_pairs={{0,1},{1,2},{2,3},{3,4},{4,5},{5,6},{6,7},{7,8},{8,9},{9,10},{10,1... | collective-permute-start | bytes 1327112 | tf_op jit(solution)/shard_map/ppermute | solution.py:16
  3.8 0.9 slice.7
  4.7 3.5 %collective-permute-start.1 = (bf16[6,8192]{1,0:T(8,128)(2,1)S(1)}, bf16[6,8192]{1,0:T(8,128)(2,1)S(1)}, u32[]{:S(2)}, u32[]{:S(2)}) collective-permute-start(bf16[6,8192]{1,0:T(8,128)(2,1)S(1)} %slice.7), channel_id=1, source_target_pairs={{0,1},{1,2},{2,3},{3,4},{4,5},{5,6},{6,7},{7,8},{8,9},{9,10},{10,1... | collective-permute-start | bytes 294920 | tf_op jit(solution)/shard_map/ppermute | solution.py:16
  8.2 0.7 broadcast_add_fusion.1
  8.9 0.7 select_reduce_fusion
  9.7 0.8 sub.26.rel_ref
  10.5 21.4 %shard_map.104.hi_ref = bf16[16,128,256]{2,1,0:T(8,128)(2,1)} custom-call(s32[384,1]{1,0:T(8,128)} %sub.26.rel_ref, bf16[256,12288]{1,0:T(8,128)(2,1)} %sv.3, bf16[256,12288]{1,0:T(8,128)(2,1)} %sv.3, bf16[256,12288]{1,0:T(8,128)(2,1)} %sv.3, bf16[256,12288]{1,0:T(8,128)(2,1)} %sv.3, bf16[256,12288]{1,0:T(8,128)(2,1)} %sv.3, bf16[256,12288]{1,0:T(8,128)(2,1)} %sv.3, ...), custom_call_target="tpu_custom_call" | custom-call | tf_op jit(solution)/shard_map/pallas_call | solution.py:107
  31.9 0.0 collective-permute-done.1.gk_h.mh_ref
  31.9 0.0 copy-start.4
  31.9 0.0 collective-permute-done.hq.hk.hv
  31.9 0.0 copy-start
  31.9 5.2 %all-to-all-start = ((bf16[16,128,256]{2,1,0:T(8,128)(2,1)}), bf16[16,128,256]{2,1,0:T(8,128)(2,1)S(1)}, u32[]{:S(2)}, u32[]{:S(2)}) async-start(bf16[16,128,256]{2,1,0:T(8,128)(2,1)} %shard_map.104.hi_ref), calls=%async_computation | async-start | bytes 2097152 | tf_op jit(solution)/shard_map/all_to_all | solution.py:256
  37.2 0.0 copy-start.5
  37.2 0.0 copy-start.6
  37.2 0.0 copy-start.8
  37.2 0.0 copy-start.7
  37.2 2.2 %collective-permute-start.2 = (bf16[16,128,256]{2,1,0:T(8,128)(2,1)}, bf16[16,128,256]{2,1,0:T(8,128)(2,1)S(1)}, u32[]{:S(2)}, u32[]{:S(2)}) collective-permute-start(bf16[16,128,256]{2,1,0:T(8,128)(2,1)} %shard_map.104.hi_ref), channel_id=1, source_target_pairs={{0,1},{1,2},{2,3},{3,4},{4,5},{5,6},{6,7},{7,8},{8,9},{9,10},{10,1... | collective-permute-start | bytes 3145736 | tf_op jit(solution)/shard_map/ppermute | solution.py:16
  39.4 0.0 copy-done.4
  39.4 0.0 copy-done
  39.4 21.5 %shard_map.105.lo_ref = bf16[16,128,256]{2,1,0:T(8,128)(2,1)} custom-call(s32[384,1]{1,0:T(8,128)} %sub.26.rel_ref, bf16[256,12288]{1,0:T(8,128)(2,1)} %sv.3, bf16[256,12288]{1,0:T(8,128)(2,1)} %sv.3, bf16[256,12288]{1,0:T(8,128)(2,1)} %sv.3, bf16[18,12288]{1,0:T(8,128)(2,1)} %copy-done, bf16[18,12288]{1,0:T(8,128)(2,1)} %copy-done, ...), custom_call_target="tpu_custom_call" | custom-call | tf_op jit(solution)/shard_map/pallas_call | solution.py:107
  60.9 12.8 %collective-permute-done.2.prev_ref = bf16[16,128,256]{2,1,0:T(8,128)(2,1)S(1)} collective-permute-done((bf16[16,128,256]{2,1,0:T(8,128)(2,1)}, bf16[16,128,256]{2,1,0:T(8,128)(2,1)S(1)}, u32[]{:S(2)}, u32[]{:S(2)}) %collective-permute-start.2) | collective-permute-done | bytes 1048608 | tf_op jit(solution)/shard_map/ppermute | solution.py:16
  73.7 0.0 copy-start.3
  73.7 0.0 all-to-all-done.hi_ref
  73.7 0.0 copy-start.1
  73.7 1.0 copy-done.3
  74.6 4.2 %all-to-all-start.1 = ((bf16[16,128,256]{2,1,0:T(8,128)(2,1)}), bf16[16,128,256]{2,1,0:T(8,128)(2,1)S(1)}, u32[]{:S(2)}, u32[]{:S(2)}) async-start(bf16[16,128,256]{2,1,0:T(8,128)(2,1)} %shard_map.105.lo_ref), calls=%async_computation.1 | async-start | bytes 2097152 | tf_op jit(solution)/shard_map/all_to_all | solution.py:261
  78.9 0.0 copy-done.5
  78.9 0.1 copy.18
  79.0 0.2 rev.3
  79.2 0.1 pad.2.clone
  79.3 0.0 copy-done.6
  79.3 0.6 broadcast_in_dim.64.skip_ref
  79.9 0.0 copy-done.8
  79.9 0.1 select_reduce_fusion.3
  80.0 0.0 copy-done.7
  80.0 0.2 select_reduce_fusion.1
  80.2 0.6 compare_select_fusion
  80.8 0.8 maximum_maximum_fusion.u_ref
  81.7 21.7 %shard_map.106 = bf16[256,4096]{1,0:T(8,128)(2,1)} custom-call(s32[384,1]{1,0:T(8,128)} %sub.26.rel_ref, bf16[256,8192]{1,0:T(8,128)(2,1)} %mg_ref.1, bf16[6,8192]{1,0:T(8,128)(2,1)} %copy-done.4, bf16[7,12288]{1,0:T(8,128)(2,1)} %wq_ref.1, bf16[16,128,256]{2,1,0:T(8,128)(2,1)} %copy-done.3, bf16[16,128,256]{2,1,0:T(8,128)(2,1)} %shard_map.105.lo_ref, ...), custom_call_target="tpu_custom_call" | custom-call | tf_op jit(solution)/shard_map/pallas_call | solution.py:166
  103.4 0.0 copy-done.1
  103.4 0.6 all-to-all-done.1.lo_ref
  104.0 0.0 copy-start.2
  104.0 1.0 copy-done.2
  105.0 5.5 %shard_map.107 = bf16[127,16,256]{2,1,0:T(8,128)(2,1)} custom-call(s32[16]{0:T(128)} %get-tuple-element.17.begin_ref, s32[16]{0:T(128)} %get-tuple-element.16.first_ref, bf16[16,128,256]{2,1,0:T(8,128)(2,1)} %copy-done.2, bf16[16,128,256]{2,1,0:T(8,128)(2,1)} %copy-done.1), custom_call_target="tpu_custom_call" | custom-call | tf_op jit(solution)/shard_map/pallas_call | solution.py:208
  (6 shorter events, 0.0 us)
Async XLA Ops:
  1.8 30.1 %collective-permute-start = (bf16[18,12288]{1,0:T(8,128)(2,1)S(1)}, bf16[18,12288]{1,0:T(8,128)(2,1)S(1)}, u32[]{:S(2)}, u32[]{:S(2)}) collective-permute-start(bf16[18,12288]{1,0:T(8,128)(2,1)S(1)} %slice.6), channel_id=1, source_target_pairs={{0,1},{1,2},{2,3},{3,4},{4,5},{5,6},{6,7},{7,8},{8,9},{9,10},{10,1... | collective-permute-start | bytes 1327112 | tf_op jit(solution)/shard_map/ppermute | solution.py:16
  4.7 27.2 %collective-permute-start.1 = (bf16[6,8192]{1,0:T(8,128)(2,1)S(1)}, bf16[6,8192]{1,0:T(8,128)(2,1)S(1)}, u32[]{:S(2)}, u32[]{:S(2)}) collective-permute-start(bf16[6,8192]{1,0:T(8,128)(2,1)S(1)} %slice.7), channel_id=1, source_target_pairs={{0,1},{1,2},{2,3},{3,4},{4,5},{5,6},{6,7},{7,8},{8,9},{9,10},{10,1... | collective-permute-start | bytes 294920 | tf_op jit(solution)/shard_map/ppermute | solution.py:16
  31.9 7.5 %copy-start.4 = (bf16[6,8192]{1,0:T(8,128)(2,1)}, bf16[6,8192]{1,0:T(8,128)(2,1)S(1)}, u32[]{:S(2)}) copy-start(bf16[6,8192]{1,0:T(8,128)(2,1)S(1)} %collective-permute-done.1.gk_h.mh_ref) | copy-start | bytes 294916
  31.9 7.5 %copy-start = (bf16[18,12288]{1,0:T(8,128)(2,1)}, bf16[18,12288]{1,0:T(8,128)(2,1)S(1)}, u32[]{:S(2)}) copy-start(bf16[18,12288]{1,0:T(8,128)(2,1)S(1)} %collective-permute-done.hq.hk.hv) | copy-start | bytes 1327108
  31.9 41.7 %all-to-all-start = ((bf16[16,128,256]{2,1,0:T(8,128)(2,1)}), bf16[16,128,256]{2,1,0:T(8,128)(2,1)S(1)}, u32[]{:S(2)}, u32[]{:S(2)}) async-start(bf16[16,128,256]{2,1,0:T(8,128)(2,1)} %shard_map.104.hi_ref), calls=%async_computation | async-start | bytes 2097152 | tf_op jit(solution)/shard_map/all_to_all | solution.py:256
  37.2 41.7 %copy-start.5 = (bf16[128,256]{1,0:T(8,128)(2,1)S(1)}, bf16[128,256]{1,0:T(8,128)(2,1)}, u32[]{:S(2)}) copy-start(bf16[128,256]{1,0:T(8,128)(2,1)} %param.14) | copy-start | bytes 196612
  37.2 42.1 %copy-start.6 = (bf16[4096]{0:T(1024)(128)(2,1)S(1)}, bf16[4096]{0:T(1024)(128)(2,1)}, u32[]{:S(2)}) copy-start(bf16[4096]{0:T(1024)(128)(2,1)} %param.15) | copy-start | bytes 24580
  37.2 42.7 %copy-start.8 = (s32[16]{0:T(128)S(1)}, s32[16]{0:T(128)}, u32[]{:S(2)}) copy-start(s32[16]{0:T(128)} %param.17) | copy-start | bytes 196
  37.2 42.8 %copy-start.7 = (s32[16]{0:T(128)S(1)}, s32[16]{0:T(128)}, u32[]{:S(2)}) copy-start(s32[16]{0:T(128)} %param.16) | copy-start | bytes 196
  37.2 36.5 %collective-permute-start.2 = (bf16[16,128,256]{2,1,0:T(8,128)(2,1)}, bf16[16,128,256]{2,1,0:T(8,128)(2,1)S(1)}, u32[]{:S(2)}, u32[]{:S(2)}) collective-permute-start(bf16[16,128,256]{2,1,0:T(8,128)(2,1)} %shard_map.104.hi_ref), channel_id=1, source_target_pairs={{0,1},{1,2},{2,3},{3,4},{4,5},{5,6},{6,7},{7,8},{8,9},{9,10},{10,1... | collective-permute-start | bytes 3145736 | tf_op jit(solution)/shard_map/ppermute | solution.py:16
  73.7 1.0 copy-start.3
  73.7 29.8 %copy-start.1 = (bf16[16,128,256]{2,1,0:T(8,128)(2,1)}, bf16[16,128,256]{2,1,0:T(8,128)(2,1)S(1)}, u32[]{:S(2)}) copy-start(bf16[16,128,256]{2,1,0:T(8,128)(2,1)S(1)} %all-to-all-done.hi_ref) | copy-start | bytes 3145732
  74.6 29.4 %all-to-all-start.1 = ((bf16[16,128,256]{2,1,0:T(8,128)(2,1)}), bf16[16,128,256]{2,1,0:T(8,128)(2,1)S(1)}, u32[]{:S(2)}, u32[]{:S(2)}) async-start(bf16[16,128,256]{2,1,0:T(8,128)(2,1)} %shard_map.105.lo_ref), calls=%async_computation.1 | async-start | bytes 2097152 | tf_op jit(solution)/shard_map/all_to_all | solution.py:261
  104.0 1.0 copy-start.2

commit v14 on v13

--- a/solution.py
+++ b/solution.py
@@ -96,9 +96,9 @@
     def col(part, row_block=half):
         return lambda j: (row_block, j + part * steps)
 
-    def halo_spec(halo, part):
+    def halo_spec(halo, part, skip=0):
         if halo.shape[0] < HALO:
-            return pl.BlockSpec((halo.shape[0], TILE), col(part, 0))
+            return pl.BlockSpec((halo.shape[0], TILE), col(part + skip, 0))
         return pl.BlockSpec((HALO, TILE), col(part, half * tok_rows // HALO - 1))
 
     main = [pl.BlockSpec((tok_rows, TILE), col(p)) for p in range(3)]
@@ -110,7 +110,7 @@
         ),
         grid=(steps,),
         in_specs=[pl.BlockSpec(rel.shape, lambda j: (0, 0))] + main + halo
-        + [main[1], halo_spec(mr_halo, 1)] + wts
+        + [main[1], halo_spec(mr_halo, 1, (mr_halo.shape[1] - mr_gates.shape[1]) // channels)] + wts
         + [pl.BlockSpec(se_filt.shape, lambda j: (0, 0)), wts[1], wts[2]],
         out_specs=pl.BlockSpec((TILE // chunk, tok_rows, chunk), lambda j: (j, 0, 0)),
         out_shape=jax.ShapeDtypeStruct((shards, tok_rows, chunk), jnp.bfloat16),
@@ -169,7 +169,9 @@
         in_specs=[
             pl.BlockSpec(rel.shape, lambda j: (0, 0)),
             pl.BlockSpec((tok_rows, lanes), lambda j: (0, j)),
-            pl.BlockSpec((mr_halo.shape[0], lanes), lambda j: (0, j)),
+            pl.BlockSpec(
+                (mr_halo.shape[0], lanes), lambda j: (0, j + (mr_halo.shape[1] - mr_gates.shape[1]) // lanes)
+            ),
             pl.BlockSpec((mr_feat.shape[0], lanes), lambda j: (0, j)),
             piece,
             piece,
@@ -240,9 +242,9 @@
     total_req = req_ends.shape[0]
     slot_total = ENDS_MAX + 1
     rim_depth = 2 * reach_rows
-    prev_se, prev_mr = passed_along(
-        (se_streams[tok_rows - 3 * reach_rows :], mr_gates[tok_rows - reach_rows :]), "seq", 1
-    )
+    se_tail = se_streams[tok_rows - 3 * reach_rows :]
+    mr_tail = jnp.pad(mr_gates[tok_rows - reach_rows :], ((2 * reach_rows, 0), (0, 0)))
+    prev_se = passed_along(jnp.concatenate([se_tail, mr_tail], axis=1), "seq", 1)
     blk = tok_rows // 2
     se_filt = se_filter
 
@@ -252,10 +254,10 @@
         rel, se_streams, se_streams, mr_gates, mr_gates, se_feat, se_filt, mr_feat, shards, 1
     )
     prev_z = passed_along(z_hi, "seq", 1)
-    z_hi, prev_se, prev_mr = lax.optimization_barrier((z_hi, prev_se, prev_mr))
+    z_hi, prev_se = lax.optimization_barrier((z_hi, prev_se))
     recv_hi = lax.all_to_all(z_hi, "seq", split_axis=0, concat_axis=0, tiled=True)
     z_lo = short_chain(
-        rel, se_streams, prev_se, mr_gates, prev_mr, se_feat, se_filt, mr_feat, shards, 0
+        rel, se_streams, prev_se, mr_gates, prev_se, se_feat, se_filt, mr_feat, shards, 0
     )
     z_lo, recv_hi, prev_z = lax.optimization_barrier((z_lo, recv_hi, prev_z))
     recv_lo = lax.all_to_all(z_lo, "seq", split_axis=0, concat_axis=0, tiled=True)
@@ -267,7 +269,7 @@
     )
 
     hyena_out = long_conv_out(
-        rel, mr_gates, prev_mr, mr_feat, prev_z, z_lo, z_hi, mr_skip[None, :], taps_rows
+        rel, mr_gates, prev_se, mr_feat, prev_z, z_lo, z_hi, mr_skip[None, :], taps_rows
     )
     rows_ids = jnp.arange(total_req, dtype=jnp.int32)
     owner = jnp.sum(

time: 112 us -> 108 us (0.964)
  starting transfers between devices: 17.1 us -> 14.8 us
  other arithmetic: 3.15 us -> 1.95 us
    ppermute x3 -> x2, starting transfers between devices: 7.64 us -> 3.98 us  [passed_along(): return lax.ppermute(x, axis, pairs)]
    all_to_all x1, starting transfers between devices: 5.24 us -> 6.6 us  [local(): lax.all_to_all(z_hi, 'seq', split_axis=0, concat_axis=0, tiled=True)]
    ppermute x3 -> x2, waiting for transfers between devices: 12.8 us -> 12.4 us  [passed_along(): return lax.ppermute(x, axis, pairs)]
  transfers between devices with their start and end apart: 5 -> 4, of which waited for: 2 -> 2; matrix products, arithmetic and copies ran while one was open for 5% -> 3% of each run, Pallas kernels for 58% -> 62%
where the time goes in v14:
time: 108 us; the launch traced here: 106 us
  Pallas kernels  71.1 us (66%)
  starting transfers between devices  14.8 us (14%)
  waiting for transfers between devices  12.8 us (12%)
  local copies, waits for them, and re-layouts  5 us (5%)
  other arithmetic  1.95 us (2%)
    pallas_call x2, Pallas kernels, short_chain(): pl.pallas_call(functools.partial(chain_kernel, group_ch=channels // se_fi...  43.5 us
    pallas_call x1, Pallas kernels, long_conv_out(): pl.pallas_call(long_kernel, grid=(steps,), in_specs=[pl.BlockSpec(rel.sha...  22 us
    ppermute x2, waiting for transfers between devices, passed_along(): return lax.ppermute(x, axis, pairs)  12.4 us
    all_to_all x1, starting transfers between devices, local(): lax.all_to_all(z_hi, 'seq', split_axis=0, concat_axis=0, tiled=True)  6.6 us
    pallas_call x1, Pallas kernels, cut_tails_all(): pl.pallas_call(tail_kernel, in_specs=[smem, smem, vmem, vmem], out_specs=...  5.55 us
    all_to_all x1, starting transfers between devices, local(): lax.all_to_all(z_lo, 'seq', split_axis=0, concat_axis=0, tiled=True)  4.22 us
    ppermute x2, starting transfers between devices, passed_along(): return lax.ppermute(x, axis, pairs)  3.98 us
  transfers between devices with their start and end apart: 4, of which 2 were waited for; matrix products, arithmetic and copies ran while one was open for 3% of the time, Pallas kernels for 62%

profile of v14, /device:TPU:18, one launch (start us, length us, event | category | flops | bytes accessed | tf_op | source)
XLA Modules:
  0.0 106.4 jit_solution(13120557741572669651)
XLA Ops:
  0.6 0.0 copy-start.6
  0.6 1.2 %slice.6 = bf16[18,12288]{1,0:T(8,128)(2,1)S(1)} slice(bf16[256,12288]{1,0:T(8,128)(2,1)} %sv.3), slice={[238:256], [0:12288]} | slice | bytes 884736 | tf_op jit(solution)/shard_map/slice | solution.py:245
  1.8 0.9 slice.7
  2.8 0.1 fusion.1
  2.9 1.9 %collective-permute-start = (bf16[18,20480]{1,0:T(8,128)(2,1)S(1)}, bf16[18,20480]{1,0:T(8,128)(2,1)S(1)}, u32[]{:S(2)}, u32[]{:S(2)}) collective-permute-start(bf16[18,20480]{1,0:T(8,128)(2,1)S(1)} %fusion.1), channel_id=1, source_target_pairs={{0,1},{1,2},{2,3},{3,4},{4,5},{5,6},{6,7},{7,8},{8,9},{9,10},{10,1... | collective-permute-start | bytes 2211848 | tf_op jit(solution)/shard_map/ppermute | solution.py:16
  4.8 0.0 copy-done.6
  4.9 0.1 select_reduce_fusion
  5.0 0.8 sub.26.rel_ref
  5.8 21.4 %shard_map.104.hi_ref = bf16[16,128,256]{2,1,0:T(8,128)(2,1)} custom-call(s32[384,1]{1,0:T(8,128)} %sub.26.rel_ref, bf16[256,12288]{1,0:T(8,128)(2,1)} %sv.3, bf16[256,12288]{1,0:T(8,128)(2,1)} %sv.3, bf16[256,12288]{1,0:T(8,128)(2,1)} %sv.3, bf16[256,12288]{1,0:T(8,128)(2,1)} %sv.3, bf16[256,12288]{1,0:T(8,128)(2,1)} %sv.3, bf16[256,12288]{1,0:T(8,128)(2,1)} %sv.3, ...), custom_call_target="tpu_custom_call" | custom-call | tf_op jit(solution)/shard_map/pallas_call | solution.py:107
  27.2 0.0 copy-start.1
  27.2 0.0 collective-permute-done.hq.hk.hv.gk_h.mh_ref
  27.2 0.0 copy-start
  27.2 6.6 %all-to-all-start = ((bf16[16,128,256]{2,1,0:T(8,128)(2,1)}), bf16[16,128,256]{2,1,0:T(8,128)(2,1)S(1)}, u32[]{:S(2)}, u32[]{:S(2)}) async-start(bf16[16,128,256]{2,1,0:T(8,128)(2,1)} %shard_map.104.hi_ref), calls=%async_computation | async-start | bytes 2097152 | tf_op jit(solution)/shard_map/all_to_all | solution.py:258
  33.8 0.0 copy-done.1
  33.8 2.1 %collective-permute-start.1 = (bf16[16,128,256]{2,1,0:T(8,128)(2,1)S(1)}, bf16[16,128,256]{2,1,0:T(8,128)(2,1)}, u32[]{:S(2)}, u32[]{:S(2)}) collective-permute-start(bf16[16,128,256]{2,1,0:T(8,128)(2,1)S(1)} %copy-done.1), channel_id=1, source_target_pairs={{0,1},{1,2},{2,3},{3,4},{4,5},{5,6},{6,7},{7,8},{8,9},{9,10},{10,1... | collective-permute-start | bytes 3145736 | tf_op jit(solution)/shard_map/ppermute | solution.py:16
  35.9 0.0 copy-done
  35.9 22.1 %shard_map.105.lo_ref = bf16[16,128,256]{2,1,0:T(8,128)(2,1)} custom-call(s32[384,1]{1,0:T(8,128)} %sub.26.rel_ref, bf16[256,12288]{1,0:T(8,128)(2,1)} %sv.3, bf16[256,12288]{1,0:T(8,128)(2,1)} %sv.3, bf16[256,12288]{1,0:T(8,128)(2,1)} %sv.3, bf16[18,20480]{1,0:T(8,128)(2,1)} %copy-done, bf16[18,20480]{1,0:T(8,128)(2,1)} %copy-done, ...), custom_call_target="tpu_custom_call" | custom-call | tf_op jit(solution)/shard_map/pallas_call | solution.py:107
  58.0 0.0 copy-start.4
  58.0 0.0 copy-start.5
  58.0 0.0 copy-start.7
  58.0 12.4 %collective-permute-done.1.prev_ref = bf16[16,128,256]{2,1,0:T(8,128)(2,1)} collective-permute-done((bf16[16,128,256]{2,1,0:T(8,128)(2,1)S(1)}, bf16[16,128,256]{2,1,0:T(8,128)(2,1)}, u32[]{:S(2)}, u32[]{:S(2)}) %collective-permute-start.1) | collective-permute-done | bytes 1048608 | tf_op jit(solution)/shard_map/ppermute | solution.py:16
  70.4 0.0 all-to-all-done.hi_ref
  70.4 0.0 copy-start.2
  70.4 4.2 %all-to-all-start.1 = ((bf16[16,128,256]{2,1,0:T(8,128)(2,1)}), bf16[16,128,256]{2,1,0:T(8,128)(2,1)S(1)}, u32[]{:S(2)}, u32[]{:S(2)}) async-start(bf16[16,128,256]{2,1,0:T(8,128)(2,1)} %shard_map.105.lo_ref), calls=%async_computation.1 | async-start | bytes 2097152 | tf_op jit(solution)/shard_map/all_to_all | solution.py:263
  74.6 0.0 copy-done.4
  74.6 0.1 copy.18
  74.8 0.2 rev.3
  75.0 0.1 pad.7.clone
  75.1 0.0 copy-done.5
  75.1 0.6 broadcast_in_dim.64.skip_ref
  75.7 0.0 copy-done.7
  75.7 0.1 select_reduce_fusion.3
  75.8 0.2 select_reduce_fusion.1
  76.0 0.6 compare_select_fusion
  76.6 0.8 maximum_maximum_fusion.u_ref
  77.4 22.0 %shard_map.106 = bf16[256,4096]{1,0:T(8,128)(2,1)} custom-call(s32[384,1]{1,0:T(8,128)} %sub.26.rel_ref, bf16[256,8192]{1,0:T(8,128)(2,1)} %mg_ref.1, bf16[18,20480]{1,0:T(8,128)(2,1)} %copy-done, bf16[7,12288]{1,0:T(8,128)(2,1)} %wq_ref.1, bf16[16,128,256]{2,1,0:T(8,128)(2,1)} %collective-permute-done.1.prev_ref, bf16[16,128,256]{2,1,0:T(8,128)(2,1)} %shard_map.105.lo_ref, ...), custom_call_target="tpu_custom_call" | custom-call | tf_op jit(solution)/shard_map/pallas_call | solution.py:166
  99.5 0.0 copy-done.2
  99.5 0.3 all-to-all-done.1.lo_ref
  99.8 0.0 copy-start.3
  99.8 1.0 copy-done.3
  100.8 5.5 %shard_map.107 = bf16[127,16,256]{2,1,0:T(8,128)(2,1)} custom-call(s32[16]{0:T(128)} %get-tuple-element.15.begin_ref, s32[16]{0:T(128)} %get-tuple-element.14.first_ref, bf16[16,128,256]{2,1,0:T(8,128)(2,1)} %copy-done.3, bf16[16,128,256]{2,1,0:T(8,128)(2,1)} %copy-done.2), custom_call_target="tpu_custom_call" | custom-call | tf_op jit(solution)/shard_map/pallas_call | solution.py:210
  (7 shorter events, 0.0 us)
Async XLA Ops:
  0.6 4.2 %copy-start.6 = (s32[16]{0:T(128)S(1)}, s32[16]{0:T(128)}, u32[]{:S(2)}) copy-start(s32[16]{0:T(128)} %param.16) | copy-start | bytes 196
  2.9 24.3 %collective-permute-start = (bf16[18,20480]{1,0:T(8,128)(2,1)S(1)}, bf16[18,20480]{1,0:T(8,128)(2,1)S(1)}, u32[]{:S(2)}, u32[]{:S(2)}) collective-permute-start(bf16[18,20480]{1,0:T(8,128)(2,1)S(1)} %fusion.1), channel_id=1, source_target_pairs={{0,1},{1,2},{2,3},{3,4},{4,5},{5,6},{6,7},{7,8},{8,9},{9,10},{10,1... | collective-permute-start | bytes 2211848 | tf_op jit(solution)/shard_map/ppermute | solution.py:16
  27.2 6.6 %copy-start.1 = (bf16[16,128,256]{2,1,0:T(8,128)(2,1)S(1)}, bf16[16,128,256]{2,1,0:T(8,128)(2,1)}, u32[]{:S(2)}) copy-start(bf16[16,128,256]{2,1,0:T(8,128)(2,1)} %shard_map.104.hi_ref) | copy-start | bytes 3145732
  27.2 8.7 %copy-start = (bf16[18,20480]{1,0:T(8,128)(2,1)}, bf16[18,20480]{1,0:T(8,128)(2,1)S(1)}, u32[]{:S(2)}) copy-start(bf16[18,20480]{1,0:T(8,128)(2,1)S(1)} %collective-permute-done.hq.hk.hv.gk_h.mh_ref) | copy-start | bytes 2211844
  27.2 43.2 %all-to-all-start = ((bf16[16,128,256]{2,1,0:T(8,128)(2,1)}), bf16[16,128,256]{2,1,0:T(8,128)(2,1)S(1)}, u32[]{:S(2)}, u32[]{:S(2)}) async-start(bf16[16,128,256]{2,1,0:T(8,128)(2,1)} %shard_map.104.hi_ref), calls=%async_computation | async-start | bytes 2097152 | tf_op jit(solution)/shard_map/all_to_all | solution.py:258
  33.8 36.6 %collective-permute-start.1 = (bf16[16,128,256]{2,1,0:T(8,128)(2,1)S(1)}, bf16[16,128,256]{2,1,0:T(8,128)(2,1)}, u32[]{:S(2)}, u32[]{:S(2)}) collective-permute-start(bf16[16,128,256]{2,1,0:T(8,128)(2,1)S(1)} %copy-done.1), channel_id=1, source_target_pairs={{0,1},{1,2},{2,3},{3,4},{4,5},{5,6},{6,7},{7,8},{8,9},{9,10},{10,1... | collective-permute-start | bytes 3145736 | tf_op jit(solution)/shard_map/ppermute | solution.py:16
  58.0 16.7 %copy-start.4 = (bf16[128,256]{1,0:T(8,128)(2,1)S(1)}, bf16[128,256]{1,0:T(8,128)(2,1)}, u32[]{:S(2)}) copy-start(bf16[128,256]{1,0:T(8,128)(2,1)} %param.14) | copy-start | bytes 196612
  58.0 17.1 %copy-start.5 = (bf16[4096]{0:T(1024)(128)(2,1)S(1)}, bf16[4096]{0:T(1024)(128)(2,1)}, u32[]{:S(2)}) copy-start(bf16[4096]{0:T(1024)(128)(2,1)} %param.15) | copy-start | bytes 24580
  58.0 17.7 %copy-start.7 = (s32[16]{0:T(128)S(1)}, s32[16]{0:T(128)}, u32[]{:S(2)}) copy-start(s32[16]{0:T(128)} %param.17) | copy-start | bytes 196
  70.4 29.1 %copy-start.2 = (bf16[16,128,256]{2,1,0:T(8,128)(2,1)}, bf16[16,128,256]{2,1,0:T(8,128)(2,1)S(1)}, u32[]{:S(2)}) copy-start(bf16[16,128,256]{2,1,0:T(8,128)(2,1)S(1)} %all-to-all-done.hi_ref) | copy-start | bytes 3145732
  70.4 29.4 %all-to-all-start.1 = ((bf16[16,128,256]{2,1,0:T(8,128)(2,1)}), bf16[16,128,256]{2,1,0:T(8,128)(2,1)S(1)}, u32[]{:S(2)}, u32[]{:S(2)}) async-start(bf16[16,128,256]{2,1,0:T(8,128)(2,1)} %shard_map.105.lo_ref), calls=%async_computation.1 | async-start | bytes 2097152 | tf_op jit(solution)/shard_map/all_to_all | solution.py:263
  99.8 1.0 copy-start.3

commit v15 on v14

--- a/solution.py
+++ b/solution.py
@@ -36,7 +36,7 @@
 
 
 HALO = 32
-TILE = 512
+TILE = 256
 GROUP_LANES = 128
 WINDOW = 144
 

time: 108 us -> 108 us (level)
  no operation moved by 1% of the time
where the time goes in v15:
time: 108 us; the launch traced here: 107 us
  Pallas kernels  71.5 us (66%)
  starting transfers between devices  14.8 us (14%)
  waiting for transfers between devices  12.6 us (12%)
  local copies, waits for them, and re-layouts  5 us (5%)
  other arithmetic  1.95 us (2%)
    pallas_call x2, Pallas kernels, short_chain(): pl.pallas_call(functools.partial(chain_kernel, group_ch=channels // se_fi...  43.9 us
    pallas_call x1, Pallas kernels, long_conv_out(): pl.pallas_call(long_kernel, grid=(steps,), in_specs=[pl.BlockSpec(rel.sha...  22 us
    ppermute x2, waiting for transfers between devices, passed_along(): return lax.ppermute(x, axis, pairs)  12.3 us
    all_to_all x1, starting transfers between devices, local(): lax.all_to_all(z_hi, 'seq', split_axis=0, concat_axis=0, tiled=True)  6.6 us
    pallas_call x1, Pallas kernels, cut_tails_all(): pl.pallas_call(tail_kernel, in_specs=[smem, smem, vmem, vmem], out_specs=...  5.54 us
    all_to_all x1, starting transfers between devices, local(): lax.all_to_all(z_lo, 'seq', split_axis=0, concat_axis=0, tiled=True)  4.22 us
    ppermute x2, starting transfers between devices, passed_along(): return lax.ppermute(x, axis, pairs)  3.98 us
  transfers between devices with their start and end apart: 4, of which 2 were waited for; matrix products, arithmetic and copies ran while one was open for 3% of the time, Pallas kernels for 62%

profile of v15, /device:TPU:18, one launch (start us, length us, event | category | flops | bytes accessed | tf_op | source)
XLA Modules:
  0.0 106.6 jit_solution(17141562702928367603)
XLA Ops:
  0.6 0.0 copy-start.6
  0.6 1.2 %slice.6 = bf16[18,12288]{1,0:T(8,128)(2,1)S(1)} slice(bf16[256,12288]{1,0:T(8,128)(2,1)} %sv.3), slice={[238:256], [0:12288]} | slice | bytes 884736 | tf_op jit(solution)/shard_map/slice | solution.py:245
  1.8 0.9 slice.7
  2.8 0.1 fusion.1
  2.9 1.9 %collective-permute-start = (bf16[18,20480]{1,0:T(8,128)(2,1)S(1)}, bf16[18,20480]{1,0:T(8,128)(2,1)S(1)}, u32[]{:S(2)}, u32[]{:S(2)}) collective-permute-start(bf16[18,20480]{1,0:T(8,128)(2,1)S(1)} %fusion.1), channel_id=1, source_target_pairs={{0,1},{1,2},{2,3},{3,4},{4,5},{5,6},{6,7},{7,8},{8,9},{9,10},{10,1... | collective-permute-start | bytes 2211848 | tf_op jit(solution)/shard_map/ppermute | solution.py:16
  4.8 0.0 copy-done.6
  4.9 0.1 select_reduce_fusion
  5.0 0.8 sub.26.rel_ref
  5.8 21.7 %shard_map.104.hi_ref = bf16[16,128,256]{2,1,0:T(8,128)(2,1)} custom-call(s32[384,1]{1,0:T(8,128)} %sub.26.rel_ref, bf16[256,12288]{1,0:T(8,128)(2,1)} %sv.3, bf16[256,12288]{1,0:T(8,128)(2,1)} %sv.3, bf16[256,12288]{1,0:T(8,128)(2,1)} %sv.3, bf16[256,12288]{1,0:T(8,128)(2,1)} %sv.3, bf16[256,12288]{1,0:T(8,128)(2,1)} %sv.3, bf16[256,12288]{1,0:T(8,128)(2,1)} %sv.3, ...), custom_call_target="tpu_custom_call" | custom-call | tf_op jit(solution)/shard_map/pallas_call | solution.py:107
  27.4 0.0 copy-start.1
  27.5 0.0 collective-permute-done.hq.hk.hv.gk_h.mh_ref
  27.5 0.0 copy-start
  27.5 6.6 %all-to-all-start = ((bf16[16,128,256]{2,1,0:T(8,128)(2,1)}), bf16[16,128,256]{2,1,0:T(8,128)(2,1)S(1)}, u32[]{:S(2)}, u32[]{:S(2)}) async-start(bf16[16,128,256]{2,1,0:T(8,128)(2,1)} %shard_map.104.hi_ref), calls=%async_computation | async-start | bytes 2097152 | tf_op jit(solution)/shard_map/all_to_all | solution.py:258
  34.1 0.0 copy-done.1
  34.1 2.1 %collective-permute-start.1 = (bf16[16,128,256]{2,1,0:T(8,128)(2,1)S(1)}, bf16[16,128,256]{2,1,0:T(8,128)(2,1)}, u32[]{:S(2)}, u32[]{:S(2)}) collective-permute-start(bf16[16,128,256]{2,1,0:T(8,128)(2,1)S(1)} %copy-done.1), channel_id=1, source_target_pairs={{0,1},{1,2},{2,3},{3,4},{4,5},{5,6},{6,7},{7,8},{8,9},{9,10},{10,1... | collective-permute-start | bytes 3145736 | tf_op jit(solution)/shard_map/ppermute | solution.py:16
  36.2 0.0 copy-done
  36.2 22.2 %shard_map.105.lo_ref = bf16[16,128,256]{2,1,0:T(8,128)(2,1)} custom-call(s32[384,1]{1,0:T(8,128)} %sub.26.rel_ref, bf16[256,12288]{1,0:T(8,128)(2,1)} %sv.3, bf16[256,12288]{1,0:T(8,128)(2,1)} %sv.3, bf16[256,12288]{1,0:T(8,128)(2,1)} %sv.3, bf16[18,20480]{1,0:T(8,128)(2,1)} %copy-done, bf16[18,20480]{1,0:T(8,128)(2,1)} %copy-done, ...), custom_call_target="tpu_custom_call" | custom-call | tf_op jit(solution)/shard_map/pallas_call | solution.py:107
  58.4 0.0 copy-start.4
  58.4 0.0 copy-start.5
  58.4 0.0 copy-start.7
  58.4 12.3 %collective-permute-done.1.prev_ref = bf16[16,128,256]{2,1,0:T(8,128)(2,1)} collective-permute-done((bf16[16,128,256]{2,1,0:T(8,128)(2,1)S(1)}, bf16[16,128,256]{2,1,0:T(8,128)(2,1)}, u32[]{:S(2)}, u32[]{:S(2)}) %collective-permute-start.1) | collective-permute-done | bytes 1048608 | tf_op jit(solution)/shard_map/ppermute | solution.py:16
  70.7 0.0 all-to-all-done.hi_ref
  70.7 0.0 copy-start.2
  70.7 4.2 %all-to-all-start.1 = ((bf16[16,128,256]{2,1,0:T(8,128)(2,1)}), bf16[16,128,256]{2,1,0:T(8,128)(2,1)S(1)}, u32[]{:S(2)}, u32[]{:S(2)}) async-start(bf16[16,128,256]{2,1,0:T(8,128)(2,1)} %shard_map.105.lo_ref), calls=%async_computation.1 | async-start | bytes 2097152 | tf_op jit(solution)/shard_map/all_to_all | solution.py:263
  74.9 0.0 copy-done.4
  74.9 0.1 copy.18
  75.0 0.2 rev.3
  75.3 0.1 pad.7.clone
  75.3 0.0 copy-done.5
  75.3 0.6 broadcast_in_dim.64.skip_ref
  76.0 0.0 copy-done.7
  76.0 0.1 select_reduce_fusion.3
  76.1 0.2 select_reduce_fusion.1
  76.3 0.6 compare_select_fusion
  76.9 0.8 maximum_maximum_fusion.u_ref
  77.7 22.0 %shard_map.106 = bf16[256,4096]{1,0:T(8,128)(2,1)} custom-call(s32[384,1]{1,0:T(8,128)} %sub.26.rel_ref, bf16[256,8192]{1,0:T(8,128)(2,1)} %mg_ref.1, bf16[18,20480]{1,0:T(8,128)(2,1)} %copy-done, bf16[7,12288]{1,0:T(8,128)(2,1)} %wq_ref.1, bf16[16,128,256]{2,1,0:T(8,128)(2,1)} %collective-permute-done.1.prev_ref, bf16[16,128,256]{2,1,0:T(8,128)(2,1)} %shard_map.105.lo_ref, ...), custom_call_target="tpu_custom_call" | custom-call | tf_op jit(solution)/shard_map/pallas_call | solution.py:166
  99.8 0.0 copy-done.2
  99.8 0.3 all-to-all-done.1.lo_ref
  100.1 0.0 copy-start.3
  100.1 1.0 copy-done.3
  101.1 5.5 %shard_map.107 = bf16[127,16,256]{2,1,0:T(8,128)(2,1)} custom-call(s32[16]{0:T(128)} %get-tuple-element.15.begin_ref, s32[16]{0:T(128)} %get-tuple-element.14.first_ref, bf16[16,128,256]{2,1,0:T(8,128)(2,1)} %copy-done.3, bf16[16,128,256]{2,1,0:T(8,128)(2,1)} %copy-done.2), custom_call_target="tpu_custom_call" | custom-call | tf_op jit(solution)/shard_map/pallas_call | solution.py:210
  (7 shorter events, 0.0 us)
Async XLA Ops:
  0.6 4.2 %copy-start.6 = (s32[16]{0:T(128)S(1)}, s32[16]{0:T(128)}, u32[]{:S(2)}) copy-start(s32[16]{0:T(128)} %param.16) | copy-start | bytes 196
  2.9 24.6 %collective-permute-start = (bf16[18,20480]{1,0:T(8,128)(2,1)S(1)}, bf16[18,20480]{1,0:T(8,128)(2,1)S(1)}, u32[]{:S(2)}, u32[]{:S(2)}) collective-permute-start(bf16[18,20480]{1,0:T(8,128)(2,1)S(1)} %fusion.1), channel_id=1, source_target_pairs={{0,1},{1,2},{2,3},{3,4},{4,5},{5,6},{6,7},{7,8},{8,9},{9,10},{10,1... | collective-permute-start | bytes 2211848 | tf_op jit(solution)/shard_map/ppermute | solution.py:16
  27.4 6.6 %copy-start.1 = (bf16[16,128,256]{2,1,0:T(8,128)(2,1)S(1)}, bf16[16,128,256]{2,1,0:T(8,128)(2,1)}, u32[]{:S(2)}) copy-start(bf16[16,128,256]{2,1,0:T(8,128)(2,1)} %shard_map.104.hi_ref) | copy-start | bytes 3145732
  27.5 8.7 %copy-start = (bf16[18,20480]{1,0:T(8,128)(2,1)}, bf16[18,20480]{1,0:T(8,128)(2,1)S(1)}, u32[]{:S(2)}) copy-start(bf16[18,20480]{1,0:T(8,128)(2,1)S(1)} %collective-permute-done.hq.hk.hv.gk_h.mh_ref) | copy-start | bytes 2211844
  27.5 43.2 %all-to-all-start = ((bf16[16,128,256]{2,1,0:T(8,128)(2,1)}), bf16[16,128,256]{2,1,0:T(8,128)(2,1)S(1)}, u32[]{:S(2)}, u32[]{:S(2)}) async-start(bf16[16,128,256]{2,1,0:T(8,128)(2,1)} %shard_map.104.hi_ref), calls=%async_computation | async-start | bytes 2097152 | tf_op jit(solution)/shard_map/all_to_all | solution.py:258
  34.1 36.6 %collective-permute-start.1 = (bf16[16,128,256]{2,1,0:T(8,128)(2,1)S(1)}, bf16[16,128,256]{2,1,0:T(8,128)(2,1)}, u32[]{:S(2)}, u32[]{:S(2)}) collective-permute-start(bf16[16,128,256]{2,1,0:T(8,128)(2,1)S(1)} %copy-done.1), channel_id=1, source_target_pairs={{0,1},{1,2},{2,3},{3,4},{4,5},{5,6},{6,7},{7,8},{8,9},{9,10},{10,1... | collective-permute-start | bytes 3145736 | tf_op jit(solution)/shard_map/ppermute | solution.py:16
  58.4 16.6 %copy-start.4 = (bf16[128,256]{1,0:T(8,128)(2,1)S(1)}, bf16[128,256]{1,0:T(8,128)(2,1)}, u32[]{:S(2)}) copy-start(bf16[128,256]{1,0:T(8,128)(2,1)} %param.14) | copy-start | bytes 196612
  58.4 17.0 %copy-start.5 = (bf16[4096]{0:T(1024)(128)(2,1)S(1)}, bf16[4096]{0:T(1024)(128)(2,1)}, u32[]{:S(2)}) copy-start(bf16[4096]{0:T(1024)(128)(2,1)} %param.15) | copy-start | bytes 24580
  58.4 17.6 %copy-start.7 = (s32[16]{0:T(128)S(1)}, s32[16]{0:T(128)}, u32[]{:S(2)}) copy-start(s32[16]{0:T(128)} %param.17) | copy-start | bytes 196
  70.7 29.1 %copy-start.2 = (bf16[16,128,256]{2,1,0:T(8,128)(2,1)}, bf16[16,128,256]{2,1,0:T(8,128)(2,1)S(1)}, u32[]{:S(2)}) copy-start(bf16[16,128,256]{2,1,0:T(8,128)(2,1)S(1)} %all-to-all-done.hi_ref) | copy-start | bytes 3145732
  70.7 29.4 %all-to-all-start.1 = ((bf16[16,128,256]{2,1,0:T(8,128)(2,1)}), bf16[16,128,256]{2,1,0:T(8,128)(2,1)S(1)}, u32[]{:S(2)}, u32[]{:S(2)}) async-start(bf16[16,128,256]{2,1,0:T(8,128)(2,1)} %shard_map.105.lo_ref), calls=%async_computation.1 | async-start | bytes 2097152 | tf_op jit(solution)/shard_map/all_to_all | solution.py:263
  100.1 1.0 copy-start.3

commit v16 on v14

--- a/solution.py
+++ b/solution.py
@@ -243,7 +243,7 @@
     slot_total = ENDS_MAX + 1
     rim_depth = 2 * reach_rows
     se_tail = se_streams[tok_rows - 3 * reach_rows :]
-    mr_tail = jnp.pad(mr_gates[tok_rows - reach_rows :], ((2 * reach_rows, 0), (0, 0)))
+    mr_tail = mr_gates[tok_rows - 3 * reach_rows :]
     prev_se = passed_along(jnp.concatenate([se_tail, mr_tail], axis=1), "seq", 1)
     blk = tok_rows // 2
     se_filt = se_filter

time: 108 us -> 108 us (level)
  no operation moved by 1% of the time
where the time goes in v16:
time: 108 us; the launch traced here: 106 us
  Pallas kernels  71.1 us (66%)
  starting transfers between devices  14.8 us (14%)
  waiting for transfers between devices  12.8 us (12%)
  local copies, waits for them, and re-layouts  5.15 us (5%)
  other arithmetic  1.91 us (2%)
    pallas_call x2, Pallas kernels, short_chain(): pl.pallas_call(functools.partial(chain_kernel, group_ch=channels // se_fi...  43.5 us
    pallas_call x1, Pallas kernels, long_conv_out(): pl.pallas_call(long_kernel, grid=(steps,), in_specs=[pl.BlockSpec(rel.sha...  22 us
    ppermute x2, waiting for transfers between devices, passed_along(): return lax.ppermute(x, axis, pairs)  12.4 us
    all_to_all x1, starting transfers between devices, local(): lax.all_to_all(z_hi, 'seq', split_axis=0, concat_axis=0, tiled=True)  6.6 us
    pallas_call x1, Pallas kernels, cut_tails_all(): pl.pallas_call(tail_kernel, in_specs=[smem, smem, vmem, vmem], out_specs=...  5.55 us
    all_to_all x1, starting transfers between devices, local(): lax.all_to_all(z_lo, 'seq', split_axis=0, concat_axis=0, tiled=True)  4.22 us
    ppermute x2, starting transfers between devices, passed_along(): return lax.ppermute(x, axis, pairs)  3.98 us
  transfers between devices with their start and end apart: 4, of which 2 were waited for; matrix products, arithmetic and copies ran while one was open for 3% of the time, Pallas kernels for 62%

profile of v16, /device:TPU:18, one launch (start us, length us, event | category | flops | bytes accessed | tf_op | source)
XLA Modules:
  0.0 106.5 jit_solution(1153568773854039946)
XLA Ops:
  0.6 0.0 copy-start.6
  0.6 1.2 %slice.6 = bf16[18,12288]{1,0:T(8,128)(2,1)S(1)} slice(bf16[256,12288]{1,0:T(8,128)(2,1)} %sv.3), slice={[238:256], [0:12288]} | slice | bytes 884736 | tf_op jit(solution)/shard_map/slice | solution.py:245
  1.8 1.1 %slice.7 = bf16[18,8192]{1,0:T(8,128)(2,1)S(1)} slice(bf16[256,8192]{1,0:T(8,128)(2,1)} %mg_ref.1), slice={[238:256], [0:8192]} | slice | bytes 589824 | tf_op jit(solution)/shard_map/slice | solution.py:246
  2.9 0.1 pad_maximum_fusion
  3.0 1.9 %collective-permute-start = (bf16[18,20480]{1,0:T(8,128)(2,1)S(1)}, bf16[18,20480]{1,0:T(8,128)(2,1)S(1)}, u32[]{:S(2)}, u32[]{:S(2)}) collective-permute-start(bf16[18,20480]{1,0:T(8,128)(2,1)S(1)} %pad_maximum_fusion), channel_id=1, source_target_pairs={{0,1},{1,2},{2,3},{3,4},{4,5},{5,6},{6,7},{7,8},{8,9},{9,10},{10,1... | collective-permute-start | bytes 2211848 | tf_op jit(solution)/shard_map/ppermute | solution.py:16
  5.0 0.0 copy-done.6
  5.0 0.1 select_reduce_fusion
  5.1 0.8 sub.26.rel_ref
  5.9 21.4 %shard_map.104.hi_ref = bf16[16,128,256]{2,1,0:T(8,128)(2,1)} custom-call(s32[384,1]{1,0:T(8,128)} %sub.26.rel_ref, bf16[256,12288]{1,0:T(8,128)(2,1)} %sv.3, bf16[256,12288]{1,0:T(8,128)(2,1)} %sv.3, bf16[256,12288]{1,0:T(8,128)(2,1)} %sv.3, bf16[256,12288]{1,0:T(8,128)(2,1)} %sv.3, bf16[256,12288]{1,0:T(8,128)(2,1)} %sv.3, bf16[256,12288]{1,0:T(8,128)(2,1)} %sv.3, ...), custom_call_target="tpu_custom_call" | custom-call | tf_op jit(solution)/shard_map/pallas_call | solution.py:107
  27.3 0.0 copy-start.1
  27.3 0.0 collective-permute-done.hq.hk.hv.gk_h.mh_ref
  27.3 0.0 copy-start
  27.3 6.6 %all-to-all-start = ((bf16[16,128,256]{2,1,0:T(8,128)(2,1)}), bf16[16,128,256]{2,1,0:T(8,128)(2,1)S(1)}, u32[]{:S(2)}, u32[]{:S(2)}) async-start(bf16[16,128,256]{2,1,0:T(8,128)(2,1)} %shard_map.104.hi_ref), calls=%async_computation | async-start | bytes 2097152 | tf_op jit(solution)/shard_map/all_to_all | solution.py:258
  33.9 0.0 copy-done.1
  33.9 2.1 %collective-permute-start.1 = (bf16[16,128,256]{2,1,0:T(8,128)(2,1)S(1)}, bf16[16,128,256]{2,1,0:T(8,128)(2,1)}, u32[]{:S(2)}, u32[]{:S(2)}) collective-permute-start(bf16[16,128,256]{2,1,0:T(8,128)(2,1)S(1)} %copy-done.1), channel_id=1, source_target_pairs={{0,1},{1,2},{2,3},{3,4},{4,5},{5,6},{6,7},{7,8},{8,9},{9,10},{10,1... | collective-permute-start | bytes 3145736 | tf_op jit(solution)/shard_map/ppermute | solution.py:16
  36.0 0.0 copy-done
  36.0 22.1 %shard_map.105.lo_ref = bf16[16,128,256]{2,1,0:T(8,128)(2,1)} custom-call(s32[384,1]{1,0:T(8,128)} %sub.26.rel_ref, bf16[256,12288]{1,0:T(8,128)(2,1)} %sv.3, bf16[256,12288]{1,0:T(8,128)(2,1)} %sv.3, bf16[256,12288]{1,0:T(8,128)(2,1)} %sv.3, bf16[18,20480]{1,0:T(8,128)(2,1)} %copy-done, bf16[18,20480]{1,0:T(8,128)(2,1)} %copy-done, ...), custom_call_target="tpu_custom_call" | custom-call | tf_op jit(solution)/shard_map/pallas_call | solution.py:107
  58.1 0.0 copy-start.4
  58.1 0.0 copy-start.5
  58.1 0.0 copy-start.7
  58.1 12.4 %collective-permute-done.1.prev_ref = bf16[16,128,256]{2,1,0:T(8,128)(2,1)} collective-permute-done((bf16[16,128,256]{2,1,0:T(8,128)(2,1)S(1)}, bf16[16,128,256]{2,1,0:T(8,128)(2,1)}, u32[]{:S(2)}, u32[]{:S(2)}) %collective-permute-start.1) | collective-permute-done | bytes 1048608 | tf_op jit(solution)/shard_map/ppermute | solution.py:16
  70.5 0.0 all-to-all-done.hi_ref
  70.5 0.0 copy-start.2
  70.5 4.2 %all-to-all-start.1 = ((bf16[16,128,256]{2,1,0:T(8,128)(2,1)}), bf16[16,128,256]{2,1,0:T(8,128)(2,1)S(1)}, u32[]{:S(2)}, u32[]{:S(2)}) async-start(bf16[16,128,256]{2,1,0:T(8,128)(2,1)} %shard_map.105.lo_ref), calls=%async_computation.1 | async-start | bytes 2097152 | tf_op jit(solution)/shard_map/all_to_all | solution.py:263
  74.8 0.0 copy-done.4
  74.8 0.1 copy.18
  74.9 0.2 rev.3
  75.1 0.1 pad.2.clone
  75.2 0.0 copy-done.5
  75.2 0.6 broadcast_in_dim.64.skip_ref
  75.8 0.0 copy-done.7
  75.8 0.1 select_reduce_fusion.3
  75.9 0.2 select_reduce_fusion.1
  76.1 0.6 compare_select_fusion
  76.7 0.8 maximum_maximum_fusion.u_ref
  77.6 22.0 %shard_map.106 = bf16[256,4096]{1,0:T(8,128)(2,1)} custom-call(s32[384,1]{1,0:T(8,128)} %sub.26.rel_ref, bf16[256,8192]{1,0:T(8,128)(2,1)} %mg_ref.1, bf16[18,20480]{1,0:T(8,128)(2,1)} %copy-done, bf16[7,12288]{1,0:T(8,128)(2,1)} %wq_ref.1, bf16[16,128,256]{2,1,0:T(8,128)(2,1)} %collective-permute-done.1.prev_ref, bf16[16,128,256]{2,1,0:T(8,128)(2,1)} %shard_map.105.lo_ref, ...), custom_call_target="tpu_custom_call" | custom-call | tf_op jit(solution)/shard_map/pallas_call | solution.py:166
  99.6 0.0 copy-done.2
  99.6 0.3 all-to-all-done.1.lo_ref
  99.9 0.0 copy-start.3
  99.9 1.0 copy-done.3
  100.9 5.5 %shard_map.107 = bf16[127,16,256]{2,1,0:T(8,128)(2,1)} custom-call(s32[16]{0:T(128)} %get-tuple-element.15.begin_ref, s32[16]{0:T(128)} %get-tuple-element.14.first_ref, bf16[16,128,256]{2,1,0:T(8,128)(2,1)} %copy-done.3, bf16[16,128,256]{2,1,0:T(8,128)(2,1)} %copy-done.2), custom_call_target="tpu_custom_call" | custom-call | tf_op jit(solution)/shard_map/pallas_call | solution.py:210
  (7 shorter events, 0.0 us)
Async XLA Ops:
  0.6 4.3 %copy-start.6 = (s32[16]{0:T(128)S(1)}, s32[16]{0:T(128)}, u32[]{:S(2)}) copy-start(s32[16]{0:T(128)} %param.16) | copy-start | bytes 196
  3.0 24.3 %collective-permute-start = (bf16[18,20480]{1,0:T(8,128)(2,1)S(1)}, bf16[18,20480]{1,0:T(8,128)(2,1)S(1)}, u32[]{:S(2)}, u32[]{:S(2)}) collective-permute-start(bf16[18,20480]{1,0:T(8,128)(2,1)S(1)} %pad_maximum_fusion), channel_id=1, source_target_pairs={{0,1},{1,2},{2,3},{3,4},{4,5},{5,6},{6,7},{7,8},{8,9},{9,10},{10,1... | collective-permute-start | bytes 2211848 | tf_op jit(solution)/shard_map/ppermute | solution.py:16
  27.3 6.6 %copy-start.1 = (bf16[16,128,256]{2,1,0:T(8,128)(2,1)S(1)}, bf16[16,128,256]{2,1,0:T(8,128)(2,1)}, u32[]{:S(2)}) copy-start(bf16[16,128,256]{2,1,0:T(8,128)(2,1)} %shard_map.104.hi_ref) | copy-start | bytes 3145732
  27.3 8.7 %copy-start = (bf16[18,20480]{1,0:T(8,128)(2,1)}, bf16[18,20480]{1,0:T(8,128)(2,1)S(1)}, u32[]{:S(2)}) copy-start(bf16[18,20480]{1,0:T(8,128)(2,1)S(1)} %collective-permute-done.hq.hk.hv.gk_h.mh_ref) | copy-start | bytes 2211844
  27.3 43.2 %all-to-all-start = ((bf16[16,128,256]{2,1,0:T(8,128)(2,1)}), bf16[16,128,256]{2,1,0:T(8,128)(2,1)S(1)}, u32[]{:S(2)}, u32[]{:S(2)}) async-start(bf16[16,128,256]{2,1,0:T(8,128)(2,1)} %shard_map.104.hi_ref), calls=%async_computation | async-start | bytes 2097152 | tf_op jit(solution)/shard_map/all_to_all | solution.py:258
  33.9 36.6 %collective-permute-start.1 = (bf16[16,128,256]{2,1,0:T(8,128)(2,1)S(1)}, bf16[16,128,256]{2,1,0:T(8,128)(2,1)}, u32[]{:S(2)}, u32[]{:S(2)}) collective-permute-start(bf16[16,128,256]{2,1,0:T(8,128)(2,1)S(1)} %copy-done.1), channel_id=1, source_target_pairs={{0,1},{1,2},{2,3},{3,4},{4,5},{5,6},{6,7},{7,8},{8,9},{9,10},{10,1... | collective-permute-start | bytes 3145736 | tf_op jit(solution)/shard_map/ppermute | solution.py:16
  58.1 16.7 %copy-start.4 = (bf16[128,256]{1,0:T(8,128)(2,1)S(1)}, bf16[128,256]{1,0:T(8,128)(2,1)}, u32[]{:S(2)}) copy-start(bf16[128,256]{1,0:T(8,128)(2,1)} %param.14) | copy-start | bytes 196612
  58.1 17.1 %copy-start.5 = (bf16[4096]{0:T(1024)(128)(2,1)S(1)}, bf16[4096]{0:T(1024)(128)(2,1)}, u32[]{:S(2)}) copy-start(bf16[4096]{0:T(1024)(128)(2,1)} %param.15) | copy-start | bytes 24580
  58.1 17.7 %copy-start.7 = (s32[16]{0:T(128)S(1)}, s32[16]{0:T(128)}, u32[]{:S(2)}) copy-start(s32[16]{0:T(128)} %param.17) | copy-start | bytes 196
  70.5 29.1 %copy-start.2 = (bf16[16,128,256]{2,1,0:T(8,128)(2,1)}, bf16[16,128,256]{2,1,0:T(8,128)(2,1)S(1)}, u32[]{:S(2)}) copy-start(bf16[16,128,256]{2,1,0:T(8,128)(2,1)S(1)} %all-to-all-done.hi_ref) | copy-start | bytes 3145732
  70.5 29.4 %all-to-all-start.1 = ((bf16[16,128,256]{2,1,0:T(8,128)(2,1)}), bf16[16,128,256]{2,1,0:T(8,128)(2,1)S(1)}, u32[]{:S(2)}, u32[]{:S(2)}) async-start(bf16[16,128,256]{2,1,0:T(8,128)(2,1)} %shard_map.105.lo_ref), calls=%async_computation.1 | async-start | bytes 2097152 | tf_op jit(solution)/shard_map/all_to_all | solution.py:263
  99.9 1.0 copy-start.3
